TPU v7x, 1024 devices: a whole 4x8x16 slice. The times are simulated.
1024 devices in a mesh: segment: 16 (over z_hi, x), dp: 4 (over z_lo), tensor: 16 (over y, core).
Axes of the slice: x: 4, y: 8, z: 16 (z_hi: 4, z_lo: 4; z = z_hi * 4 + z_lo), core: 2. Of those that a mesh axis runs over, the one named last changes fastest.
Arguments:
- inbound: bfloat16 [16, 2, 512, 4096], P('segment', None, 'dp'), may hold values from -21 to 21
- weights: bfloat16 [16, 4096, 3, 4096], P('segment', None, None, 'tensor'), may hold values from -0.09375 to 0.09375
- cotangent: bfloat16 [16, 2, 512, 4096], P('segment', None, 'dp', 'tensor'), may hold values from -20 to 20
Outputs:
- section_out: bfloat16 [16, 2, 512, 4096], P('segment', None, 'dp', 'tensor')
All inputs are finite; a program needn't handle non-finite values.
Results may differ from a plain program's by a relative error of at most 0.022.
The roundings to bfloat16 on the way count: a program that leaves them out, or rounds other values in their place, can miss the bound.
Values may be sent and summed in bfloat16 or wider, within the bound.
No kernel may reach another device: no remote copies, remote signals or barrier semaphores. Data moves between devices by JAX's collectives and lax.ppermute only.
A program may use at most 64 MiB of HBM per device.

v0:
```python
import jax
import jax.numpy as jnp
from jax import lax
from jax.sharding import PartitionSpec as P

HD = 64


def broadcast(value, axis, root):
    mine = lax.axis_index(axis) == root
    return lax.psum(jnp.where(mine, value, jnp.zeros_like(value)), axis)


def shards(inbound, weights, cotangent):
    states = inbound[0]
    micro_count, row_count, model_width = states.shape
    encoded = broadcast(states, "segment", 0)
    section_layer = weights[0]
    feat_width = section_layer.shape[2]
    head_count = feat_width // HD
    score_scale = HD ** (-0.5)
    query = jnp.dot(
        states.reshape(micro_count * row_count, model_width),
        section_layer[:, 0, :],
        preferred_element_type=jnp.float32,
    ).astype(jnp.bfloat16)
    query = query.reshape(micro_count, row_count, feat_width)
    upstream = cotangent[0]
    pair_weights = section_layer[:, 1:, :].reshape(model_width, 2 * feat_width)
    keyval = jnp.dot(
        encoded.reshape(micro_count * row_count, model_width),
        pair_weights,
        preferred_element_type=jnp.float32,
    ).astype(jnp.bfloat16)
    keyval = keyval.reshape(micro_count, row_count, 2, feat_width)
    all_keyval = lax.all_gather(keyval, "dp", axis=1, tiled=True)
    key_count = all_keyval.shape[1]
    all_query, all_upstream = (query, upstream)
    query_count = all_query.shape[1]

    def attend(items):
        query_one, upstream_one, keyval_one = items
        query_heads = query_one.reshape(query_count, head_count, HD)
        grad_heads = upstream_one.reshape(query_count, head_count, HD)
        key_heads = keyval_one[:, 0].reshape(key_count, head_count, HD)
        value_heads = keyval_one[:, 1].reshape(key_count, head_count, HD)
        scores = (
            jnp.einsum("qhe,khe->hqk", query_heads, key_heads, preferred_element_type=jnp.float32)
            * score_scale
        )
        score_peak = jnp.max(scores, axis=-1, keepdims=True)
        exp_scores = jnp.exp(scores - score_peak)
        attend_prob = exp_scores / jnp.sum(exp_scores, axis=-1, keepdims=True)
        prob_rounded = attend_prob.astype(jnp.bfloat16)
        prob_grad = jnp.einsum(
            "qhe,khe->hqk", grad_heads, value_heads, preferred_element_type=jnp.float32
        )
        row_delta = jnp.sum(attend_prob * prob_grad, axis=-1, keepdims=True)
        score_grad = (attend_prob * (prob_grad - row_delta) * score_scale).astype(jnp.bfloat16)
        context = jnp.einsum(
            "hqk,khe->qhe", prob_rounded, value_heads, preferred_element_type=jnp.float32
        )
        key_grad = jnp.einsum(
            "hqk,qhe->khe", score_grad, query_heads, preferred_element_type=jnp.float32
        )
        value_grad = jnp.einsum(
            "hqk,qhe->khe", prob_rounded, grad_heads, preferred_element_type=jnp.float32
        )
        context = context.astype(jnp.bfloat16).reshape(row_count, feat_width)
        joined = jnp.stack(
            [key_grad.reshape(-1, feat_width), value_grad.reshape(-1, feat_width)], axis=1
        )
        return (context, joined)

    context, joined_grads = lax.map(attend, (all_query, all_upstream, all_keyval))
    owned_grads = lax.psum_scatter(joined_grads, "dp", scatter_dimension=1, tiled=True).astype(
        jnp.bfloat16
    )
    head_terms = jnp.einsum(
        "rc,dc->rd",
        owned_grads.reshape(micro_count * row_count, 2 * feat_width),
        pair_weights,
        preferred_element_type=jnp.float32,
    )
    head_terms = head_terms.reshape(micro_count, row_count, model_width)
    heads_total = lax.psum_scatter(
        head_terms.astype(jnp.bfloat16), "tensor", scatter_dimension=2, tiled=True
    ).astype(jnp.float32)
    segment_index = lax.axis_index("segment")
    live_mask = (segment_index > 0).astype(jnp.float32)
    sections = lax.psum(heads_total * live_mask, "segment")
    encoder_grad = (sections + cotangent[0].astype(jnp.float32)).astype(jnp.bfloat16)
    result = jnp.where(segment_index == 0, encoder_grad, context)
    return result[None]


def solution(mesh):
    placed = (
        P("segment", None, "dp", None),
        P("segment", None, None, "tensor"),
        P("segment", None, "dp", "tensor"),
    )
    return jax.shard_map(
        shards,
        mesh=mesh,
        in_specs=placed,
        out_specs=P("segment", None, "dp", "tensor"),
        check_vma=False,
    )
```

profile of v0, /device:TPU:56, one launch (start us, length us, event | category | flops | bytes accessed | tf_op | source)
XLA Modules:
  0.0 695.1 jit_solution(15255595068390172533)
XLA Ops:
  6.5 0.0 all-reduce.3.cloned.1.call-start
  6.5 3.0 broadcast_select_fusion
  9.6 0.0 all-reduce.3.cloned.1.call-update
  9.6 0.0 all-gather.2.cloned.1.call-start
  9.6 4.4 slice.16
  14.1 6.4 copy.9
  20.5 262.3 %all-reduce.3.cloned.1.call-done = bf16[256,4096]{1,0:T(8,128)(2,1)} async-done(((bf16[256,4096]{1,0:T(8,128)(2,1)}), bf16[256,4096]{1,0:T(8,128)(2,1)}) %all-reduce.3.cloned.1.call-update) | async-done | bytes 2097168 | tf_op jit(solution)/shard_map/psum | solution.py:11
  282.8 0.0 copy-start
  282.8 4.2 convolution_convert_fusion.1
  287.0 0.1 reshape.40
  287.1 0.9 copy.10
  288.0 0.0 all-gather.2.cloned.1.call-update
  288.0 0.0 reduce-scatter.3.cloned.1.call-start
  288.1 0.0 copy-done
  288.1 0.0 copy-start.1
  288.1 2.3 fusion.23
  290.4 39.3 %all-gather.2.cloned.1.call-done = bf16[2,512,2,256]{1,3,2,0:T(8,128)(2,1)} async-done(((bf16[2,128,2,256]{1,3,2,0:T(8,128)(2,1)}), bf16[2,512,2,256]{1,3,2,0:T(8,128)(2,1)}) %all-gather.2.cloned.1.call-update) | async-done | bytes 1048592 | tf_op jit(solution)/shard_map/all_gather | solution.py:36
  329.7 0.0 copy-done.1
  329.7 16.4 %while.12 = (s32[]{:T(128)}, bf16[2,128,256]{2,1,0:T(8,128)(2,1)}, f32[2,512,2,256]{1,3,2,0:T(8,128)}, bf16[2,512,2,256]{1,3,2,0:T(8,128)(2,1)}, bf16[2,128,256]...) while((s32[]{:T(128)}, bf16[2,128,256]{2,1,0:T(8,128)(2,1)}, ...), condition=%wide.region_5.6_spmd, body=%wide.region_1.5_spmd.sunk | while | flops 239898112 | bytes 12002389 | solution.py:75
  329.7 1.1 dynamic-slice_bitcast_fusion.2
  330.9 0.1 copy.24
  331.0 0.6 fusion.80
  331.6 0.7 convolution_convert_fusion.3
  332.3 0.1 copy.25
  332.4 0.6 constant_dynamic-slice_fusion.5
  333.1 0.1 copy.26
  333.2 0.3 fusion.82
  333.5 2.6 fusion.83
  336.1 0.7 fusion.81
  336.8 1.1 fusion.84
  337.9 1.1 dynamic-slice_bitcast_fusion.2
  339.0 0.1 copy.24
  339.2 0.6 fusion.80
  339.7 0.7 convolution_convert_fusion.3
  340.5 0.1 copy.25
  340.6 0.6 constant_dynamic-slice_fusion.5
  341.2 0.1 copy.26
  341.3 0.3 fusion.82
  341.7 2.6 fusion.83
  344.3 0.7 fusion.81
  345.0 1.1 fusion.84
  346.1 0.0 reduce-scatter.3.cloned.1.call-update
  346.1 0.0 reduce-scatter.5.cloned.1.call-start
  346.2 55.7 %reduce-scatter.3.cloned.1.call-done = f32[2,128,2,256]{1,3,2,0:T(8,128)} async-done(((f32[2,512,2,256]{1,3,2,0:T(8,128)}), f32[2,128,2,256]{1,3,2,0:T(8,128)}) %reduce-scatter.3.cloned.1.call-update) | async-done | bytes 524304 | tf_op jit(solution)/shard_map/reduce_scatter | solution.py:76
  401.9 5.0 fusion.20
  406.9 0.0 reduce-scatter.5.cloned.1.call-update
  406.9 0.0 all-reduce.5.cloned.1.call-start
  407.0 64.0 %reduce-scatter.5.cloned.1.call-done = bf16[2,128,256]{2,1,0:T(8,128)(2,1)} async-done(((bf16[2,128,4096]{2,1,0:T(8,128)(2,1)}), bf16[2,128,256]{2,1,0:T(8,128)(2,1)}) %reduce-scatter.5.cloned.1.call-update) | async-done | bytes 131088 | tf_op jit(solution)/shard_map/reduce_scatter | solution.py:86
  471.0 1.6 convert_multiply_fusion
  472.6 0.0 all-reduce.5.cloned.1.call-update
  472.6 214.3 %all-reduce.5.cloned.1.call-done = f32[2,128,256]{2,1,0:T(8,128)} async-done(((f32[2,128,256]{2,1,0:T(8,128)}), f32[2,128,256]{2,1,0:T(8,128)}) %all-reduce.5.cloned.1.call-update) | async-done | bytes 262160 | tf_op jit(solution)/shard_map/psum | solution.py:91
  687.0 1.6 fusion.26
  (6 shorter events, 0.1 us)
Async XLA Ops:
  6.5 276.2 %all-reduce.3.cloned.1.call-start = ((), (), s32[]{:S(2)}) async-start(), calls=%async_computation.2 | async-start | bytes 4194304 | tf_op jit(solution)/shard_map/psum | solution.py:11
  9.6 320.2 %all-gather.2.cloned.1.call-start = ((), (), s32[]{:S(2)}) async-start(), calls=%async_computation.3 | async-start | bytes 1310720 | tf_op jit(solution)/shard_map/all_gather | solution.py:36
  282.8 5.3 copy-start
  288.0 113.9 %reduce-scatter.3.cloned.1.call-start = ((), (), s32[]{:S(2)}) async-start(), calls=%async_computation.4 | async-start | bytes 2621440 | tf_op jit(solution)/shard_map/reduce_scatter | solution.py:76
  288.1 41.7 %copy-start.1 = (bf16[1,2,128,256]{3,2,1,0:T(8,128)(2,1)S(1)}, bf16[1,2,128,256]{3,2,1,0:T(8,128)(2,1)}, u32[]{:S(2)}) copy-start(bf16[1,2,128,256]{3,2,1,0:T(8,128)(2,1)} %param.7) | copy-start | bytes 393220
  346.1 124.9 %reduce-scatter.5.cloned.1.call-start = ((), (), s32[]{:S(2)}) async-start(), calls=%async_computation.5 | async-start | bytes 2228224 | tf_op jit(solution)/shard_map/reduce_scatter | solution.py:86
  406.9 280.0 %all-reduce.5.cloned.1.call-start = ((), (), s32[]{:S(2)}) async-start(), calls=%async_computation.6 | async-start | bytes 524288 | tf_op jit(solution)/shard_map/psum | solution.py:91
Sparse Core Ops, SparseCore 0:
  10.8 271.8 all-reduce.2
  288.1 41.5 all-gather.1
  346.2 55.5 reduce-scatter.2
  407.0 63.9 reduce-scatter.4
  474.3 212.6 all-reduce.4
where the time goes:
time: 696 us; the launch traced here: 695 us
  waiting for transfers between devices  636 us (91%)
  matrix products  21.5 us (3%)
  local copies, waits for them, and re-layouts  16 us (2%)
  between operations  13.2 us (2%)
  other arithmetic  8.46 us (1%)
    psum x1, waiting for transfers between devices, broadcast(): return lax.psum(jnp.where(mine, value, jnp.zeros_like(value)), axis)  262 us
    psum x1, waiting for transfers between devices, shards(): sections = lax.psum(heads_total * live_mask, 'segment')  214 us
    reduce_scatter x1, waiting for transfers between devices, shards(): lax.psum_scatter(head_terms.astype(jnp.bfloat16), 'tensor', scatter_dimen...  64 us
    reduce_scatter x1, waiting for transfers between devices, shards(): lax.psum_scatter(joined_grads, 'dp', scatter_dimension=1, tiled=True)  55.7 us
    all_gather x1, waiting for transfers between devices, shards(): all_keyval = lax.all_gather(keyval, 'dp', axis=1, tiled=True)  39.3 us
  transfers between devices with their start and end apart: 5, of which 5 were waited for; matrix products, arithmetic and copies ran while one was open for 2% of the time, Pallas kernels for 0%

commit v1 on v0

v1 whole, which is shorter than its diff:
```python
import jax
import jax.numpy as jnp
from jax import lax
from jax.sharding import PartitionSpec as P

HD = 64
X_SIZE = 4


def seg_tree(n_seg):
    n_hi = n_seg // X_SIZE
    rounds = []
    hi_round = [(0, X_SIZE)]
    if n_hi > 2:
        hi_round.append((0, (n_hi - 1) * X_SIZE))
    rounds.append(hi_round)
    if n_hi > 3:
        rounds.append([(X_SIZE, 2 * X_SIZE)])
    x_round = [(z * X_SIZE, z * X_SIZE + 1) for z in range(n_hi)]
    x_round2 = [(z * X_SIZE, z * X_SIZE + X_SIZE - 1) for z in range(n_hi)]
    rounds.append(x_round + x_round2)
    rounds.append([(z * X_SIZE + 1, z * X_SIZE + 2) for z in range(n_hi)])
    return rounds


def split_pairs(pairs):
    groups = []
    for pair in pairs:
        for group in groups:
            if all(pair[0] != p[0] and pair[1] != p[1] for p in group):
                group.append(pair)
                break
        else:
            groups.append([pair])
    return groups


def seg_broadcast(value, rounds):
    seg = lax.axis_index("segment")
    cur = value
    for pairs in rounds:
        nxt = cur
        for group in split_pairs(pairs):
            got = lax.ppermute(cur, "segment", group)
            dests = jnp.array([p[1] for p in group])
            nxt = jnp.where(jnp.any(seg == dests), got, nxt)
        cur = nxt
    return cur


def seg_reduce(value, rounds):
    seg = lax.axis_index("segment")
    cur = value
    for pairs in reversed(rounds):
        rev = [(b, a) for a, b in pairs]
        acc = cur
        for group in split_pairs(rev):
            got = lax.ppermute(cur, "segment", group)
            dests = jnp.array([p[1] for p in group])
            acc = acc + jnp.where(jnp.any(seg == dests), got, jnp.zeros_like(got))
        cur = acc
    return cur


def dp_gather_small(value, n_dp):
    parts = [value]
    for shift in range(1, n_dp):
        parts.append(lax.ppermute(value, "dp", [(i, (i + shift) % n_dp) for i in range(n_dp)]))
    return jnp.stack(parts)


def shards(inbound, weights, cotangent):
    n_seg = lax.axis_size("segment")
    n_dp = lax.axis_size("dp")
    n_tensor = lax.axis_size("tensor")
    seg = lax.axis_index("segment")
    tix = lax.axis_index("tensor")
    rounds = seg_tree(n_seg)

    states = inbound[0]
    micro_count, row_count, model_width = states.shape
    layer = weights[0]
    feat_width = layer.shape[2]
    head_count = feat_width // HD
    scale = HD ** (-0.5)
    rows = micro_count * row_count

    query = jnp.dot(
        states.reshape(rows, model_width), layer[:, 0, :], preferred_element_type=jnp.float32
    ).astype(jnp.bfloat16)
    query = query.reshape(micro_count, row_count, feat_width)
    upstream = cotangent[0]
    all_query = lax.all_gather(query, "dp", axis=1, tiled=True)
    all_grad = lax.all_gather(upstream, "dp", axis=1, tiled=True)
    query_count = all_query.shape[1]

    chunk = lax.dynamic_slice_in_dim(states, tix * (model_width // n_tensor), model_width // n_tensor, axis=2)
    chunk = seg_broadcast(chunk, rounds)
    encoded = lax.all_gather(chunk, "tensor", axis=2, tiled=True)

    pair_weights = layer[:, 1:, :].reshape(model_width, 2 * feat_width)
    keyval = jnp.dot(
        encoded.reshape(rows, model_width), pair_weights, preferred_element_type=jnp.float32
    ).astype(jnp.bfloat16)
    keyval = keyval.reshape(micro_count, row_count, 2, head_count, HD)
    key_heads = keyval[:, :, 0]
    value_heads = keyval[:, :, 1]
    query_heads = all_query.reshape(micro_count, query_count, head_count, HD)
    grad_heads = all_grad.reshape(micro_count, query_count, head_count, HD)

    scores = (
        jnp.einsum("mqhe,mkhe->mhqk", query_heads, key_heads, preferred_element_type=jnp.float32)
        * scale
    )
    prob_grad = jnp.einsum(
        "mqhe,mkhe->mhqk", grad_heads, value_heads, preferred_element_type=jnp.float32
    )
    local_peak = jnp.max(scores, axis=-1)
    local_exp = jnp.exp(scores - local_peak[..., None])
    local_sum = jnp.sum(local_exp, axis=-1)
    local_delta = jnp.sum(local_exp * prob_grad, axis=-1)
    stats = jnp.stack([local_peak, local_sum, local_delta])
    all_stats = dp_gather_small(stats, n_dp)
    peaks = all_stats[:, 0]
    peak = jnp.max(peaks, axis=0)
    weight = jnp.exp(peaks - peak[None])
    total = jnp.sum(all_stats[:, 1] * weight, axis=0)
    row_delta = jnp.sum(all_stats[:, 2] * weight, axis=0) / total

    attend_prob = jnp.exp(scores - peak[..., None]) / total[..., None]
    prob_rounded = attend_prob.astype(jnp.bfloat16)
    score_grad = (attend_prob * (prob_grad - row_delta[..., None]) * scale).astype(jnp.bfloat16)

    context_part = jnp.einsum(
        "mhqk,mkhe->mqhe", prob_rounded, value_heads, preferred_element_type=jnp.float32
    ).reshape(micro_count, query_count, feat_width)
    context = lax.psum_scatter(context_part, "dp", scatter_dimension=1, tiled=True).astype(
        jnp.bfloat16
    )

    key_grad = jnp.einsum(
        "mhqk,mqhe->mkhe", score_grad, query_heads, preferred_element_type=jnp.float32
    ).astype(jnp.bfloat16)
    value_grad = jnp.einsum(
        "mhqk,mqhe->mkhe", prob_rounded, grad_heads, preferred_element_type=jnp.float32
    ).astype(jnp.bfloat16)
    joined = jnp.stack(
        [key_grad.reshape(rows, feat_width), value_grad.reshape(rows, feat_width)], axis=1
    ).reshape(rows, 2 * feat_width)
    head_terms = jnp.einsum(
        "rc,dc->rd", joined, pair_weights, preferred_element_type=jnp.float32
    ).astype(jnp.bfloat16)
    head_terms = head_terms.reshape(micro_count, row_count, model_width)
    heads_total = lax.psum_scatter(head_terms, "tensor", scatter_dimension=2, tiled=True).astype(
        jnp.float32
    )
    heads_total = jnp.where(seg > 0, heads_total, jnp.zeros_like(heads_total))
    sections = seg_reduce(heads_total, rounds)
    encoder_grad = (sections + cotangent[0].astype(jnp.float32)).astype(jnp.bfloat16)
    result = jnp.where(seg == 0, encoder_grad, context)
    return result[None]


def solution(mesh):
    placed = (
        P("segment", None, "dp", None),
        P("segment", None, None, "tensor"),
        P("segment", None, "dp", "tensor"),
    )
    return jax.shard_map(
        shards,
        mesh=mesh,
        in_specs=placed,
        out_specs=P("segment", None, "dp", "tensor"),
        check_vma=False,
    )
```

time: 696 us -> 295 us (0.42)
  the two profiles are of different devices: /device:TPU:56 before, /device:TPU:121 now
where the time goes in v1:
time: 295 us; the launch traced here: 294 us
  waiting for transfers between devices  168 us (57%)
  starting transfers between devices  38.5 us (13%)
  blocking collectives  31.2 us (11%)
  local copies, waits for them, and re-layouts  15.9 us (5%)
  matrix products  14.6 us (5%)
  between operations  13.5 us (5%)
  other arithmetic  12.2 us (4%)
    reduce_scatter x1, waiting for transfers between devices, shards(): lax.psum_scatter(head_terms, 'tensor', scatter_dimension=2, tiled=True)  64.4 us
    ppermute x6, waiting for transfers between devices, seg_reduce(): got = lax.ppermute(cur, 'segment', group)  44.2 us
    reduce_scatter x1, waiting for transfers between devices, shards(): lax.psum_scatter(context_part, 'dp', scatter_dimension=1, tiled=True)  26.3 us
    all_gather x1, waiting for transfers between devices, shards(): encoded = lax.all_gather(chunk, 'tensor', axis=2, tiled=True)  24.5 us
    ppermute x6, starting transfers between devices, seg_broadcast(): got = lax.ppermute(cur, 'segment', group)  22.2 us
    all_gather x1, blocking collectives, shards(): all_query = lax.all_gather(query, 'dp', axis=1, tiled=True)  17.8 us
    all_gather x1, blocking collectives, shards(): all_grad = lax.all_gather(upstream, 'dp', axis=1, tiled=True)  13.4 us
    slice x2, local copies, waits for them, and re-layouts, shards(): pair_weights = layer[:, 1:, :].reshape(model_width, 2 * feat_width)  11 us
  transfers between devices with their start and end apart: 18, of which 8 were waited for; matrix products, arithmetic and copies ran while one was open for 8% of the time, Pallas kernels for 0%

profile of v1, /device:TPU:121, one launch (start us, length us, event | category | flops | bytes accessed | tf_op | source)
XLA Modules:
  0.0 293.8 jit_solution(2586757947873893140)
XLA Ops:
  6.5 0.9 dynamic-slice_bitcast_fusion
  7.5 17.0 %collective-permute-start = (bf16[2,128,256]{2,1,0:T(8,128)(2,1)S(1)}, bf16[2,128,256]{2,1,0:T(8,128)(2,1)S(1)}, u32[]{:S(2)}, u32[]{:S(2)}) collective-permute-start(bf16[2,128,256]{2,1,0:T(8,128)(2,1)S(1)} %dynamic-slice_bitcast_fusion), channel_id=1, source_target_pairs={{0,768},{1,769},{2,770},{3,771},{4,772},{5,773},{6,774},{7,775},{8... | collective-permute-start | bytes 393224 | tf_op jit(solution)/shard_map/ppermute | solution.py:44
  24.5 1.3 collective-permute-start.1
  25.8 6.5 %collective-permute-done = bf16[2,128,256]{2,1,0:T(8,128)(2,1)S(1)} collective-permute-done((bf16[2,128,256]{2,1,0:T(8,128)(2,1)S(1)}, bf16[2,128,256]{2,1,0:T(8,128)(2,1)S(1)}, u32[]{:S(2)}, u32[]{:S(2)}) %collective-permute-start) | collective-permute-done | bytes 131104 | tf_op jit(solution)/shard_map/ppermute | solution.py:44
  32.3 1.0 select_select_fusion.1
  33.2 0.7 collective-permute-start.2
  34.0 1.3 collective-permute-start.3
  35.3 1.3 collective-permute-start.4
  36.6 1.4 compare_reduce_fusion.1
  37.9 0.5 collective-permute-done.4
  38.5 1.3 select_select_fusion
  39.8 0.7 collective-permute-start.5
  40.5 1.4 compare_reduce_fusion.3
  41.9 1.4 broadcast_select_fusion.1
  43.3 0.0 all-gather.3.cloned.1.call-update
  43.3 0.0 reduce-scatter.3.cloned.1.call-start
  43.3 4.4 %slice.29 = bf16[4096,2,256]{2,0,1:T(8,128)(2,1)} slice(bf16[4096,3,256]{2,0,1:T(8,128)(2,1)} %bitcast.98), slice={[0:4096], [1:3], [0:256]} | slice | bytes 8388608 | tf_op jit(solution)/shard_map/slice | solution.py:101
  47.8 6.6 %copy.27 = bf16[4096,2,256]{0,2,1:T(8,128)(2,1)} copy(bf16[4096,2,256]{2,0,1:T(8,128)(2,1)} %slice.29) | data formatting | bytes 8388608 | tf_op jit(solution)/shard_map/slice | solution.py:101
  54.3 2.3 fusion.7
  56.7 17.8 %all_gather.9 = bf16[2,512,256]{2,1,0:T(8,128)(2,1)S(1)} all-gather(bf16[2,128,256]{2,1,0:T(8,128)(2,1)S(1)} %bitcast.108), channel_id=1, replica_groups=mesh['segment'=16,'dp'=4,'tensor'=16] {'dp'}, dimensions={1}, use_global_device_ids=true | all-gather | bytes 655360 | tf_op jit(solution)/shard_map/all_gather | solution.py:93
  74.5 0.2 copy.26
  74.7 13.4 %all-gather = bf16[1,2,512,256]{3,2,1,0:T(8,128)(2,1)S(1)} all-gather(bf16[1,2,128,256]{3,2,1,0:T(8,128)(2,1)S(1)} %copy-done), channel_id=2, replica_groups=mesh['segment'=16,'dp'=4,'tensor'=16] {'dp'}, dimensions={2}, use_global_device_ids=true | all-gather | bytes 655360 | tf_op jit(solution)/shard_map/all_gather | solution.py:94
  88.1 0.2 copy.31
  88.3 24.5 %all-gather.3.cloned.1.call-done = bf16[2,128,4096]{2,1,0:T(8,128)(2,1)} async-done(((bf16[2,128,256]{2,1,0:T(8,128)(2,1)}), bf16[2,128,4096]{2,1,0:T(8,128)(2,1)}) %all-gather.3.cloned.1.call-update) | async-done | bytes 2097168 | tf_op jit(solution)/shard_map/all_gather | solution.py:99
  112.8 4.1 %convolution_convert_fusion = bf16[256,512]{1,0:T(8,128)(2,1)S(1)} fusion(bf16[256,4096]{1,0:T(8,128)(2,1)} %bitcast.115, bf16[4096,512]{0,1:T(8,128)(2,1)} %bitcast.97), kind=kOutput, calls=%fused_computation.14 | convolution fusion | flops 1073872896 | bytes 6553600 | tf_op jit(solution)/shard_map/dot_general | solution.py:102
  116.9 0.3 reshape.67
  117.2 0.2 fusion.36
  117.4 0.2 copy.51
  117.5 0.2 copy.52
  117.7 0.5 multiply_reduce_fusion
  118.2 0.7 fusion.6
  119.0 3.2 %collective-permute-start.6 = (f32[3,2,4,512]{3,2,1,0:T(4,128)S(1)}, f32[3,2,4,512]{3,2,1,0:T(4,128)S(1)}, u32[]{:S(2)}, u32[]{:S(2)}) collective-permute-start(f32[3,2,4,512]{3,2,1,0:T(4,128)S(1)} %get-tuple-element.12), channel_id=1, source_target_pairs={{0,16},{16,32},{32,48},{48,0},{1,17},{17,33},{33,49},{49,1},{2,18}... | collective-permute-start | bytes 147464 | tf_op jit(solution)/shard_map/ppermute | solution.py:68
  122.2 3.0 %collective-permute-start.7 = (f32[3,2,4,512]{3,2,1,0:T(4,128)S(1)}, f32[3,2,4,512]{3,2,1,0:T(4,128)S(1)}, u32[]{:S(2)}, u32[]{:S(2)}) collective-permute-start(f32[3,2,4,512]{3,2,1,0:T(4,128)S(1)} %get-tuple-element.12), channel_id=1, source_target_pairs={{0,32},{16,48},{32,0},{48,16},{1,33},{17,49},{33,1},{49,17},{2,34}... | collective-permute-start | bytes 147464 | tf_op jit(solution)/shard_map/ppermute | solution.py:68
  125.2 3.4 %collective-permute-start.8 = (f32[3,2,4,512]{3,2,1,0:T(4,128)S(1)}, f32[3,2,4,512]{3,2,1,0:T(4,128)S(1)}, u32[]{:S(2)}, u32[]{:S(2)}) collective-permute-start(f32[3,2,4,512]{3,2,1,0:T(4,128)S(1)} %get-tuple-element.12), channel_id=1, source_target_pairs={{0,48},{16,0},{32,16},{48,32},{1,49},{17,1},{33,17},{49,33},{2,50}... | collective-permute-start | bytes 147464 | tf_op jit(solution)/shard_map/ppermute | solution.py:68
  128.6 1.4 collective-permute-done.8
  130.1 0.1 fusion.28
  130.2 0.6 fusion.9
  130.9 0.9 fusion.8
  131.7 0.2 copy.45
  131.9 0.2 reshape.65
  132.1 0.2 copy.46
  132.4 0.2 reshape.66
  132.6 4.8 %fusion = bf16[256,4096]{1,0:T(8,128)(2,1)} fusion(bf16[256,1,256]{2,0,1:T(8,128)(2,1)S(1)} %reshape.66, bf16[256,1,256]{2,0,1:T(8,128)(2,1)S(1)} %reshape.65, bf16[4096,3,256]{2,0,1:T(8,128)(2,1)} %bitcast.100), kind=kOutput, calls=%fused_computation.1 | convolution fusion | flops 1074921472 | bytes 6553600 | tf_op jit(solution)/shard_map/rc,dc->rd/dot_general | solution.py:150
  137.4 0.0 reduce-scatter.3.cloned.1.call-update
  137.4 0.0 reduce-scatter.5.cloned.1.call-start
  137.5 0.6 copy-done.2
  138.1 0.6 fusion.13
  138.7 1.3 copy.41
  140.0 0.0 reduce-scatter.5.cloned.1.call-update
  140.1 64.4 %reduce-scatter.3.cloned.1.call-done = bf16[2,128,256]{2,1,0:T(8,128)(2,1)} async-done(((bf16[2,128,4096]{2,1,0:T(8,128)(2,1)}), bf16[2,128,256]{2,1,0:T(8,128)(2,1)}) %reduce-scatter.3.cloned.1.call-update) | async-done | bytes 131088 | tf_op jit(solution)/shard_map/reduce_scatter | solution.py:154
  204.4 0.9 convert_select_fusion
  205.4 0.7 collective-permute-start.9
  206.1 1.6 select_add_fusion.2
  207.7 1.3 collective-permute-start.10
  209.0 1.3 collective-permute-start.11
  210.3 0.6 compare_reduce_fusion
  210.9 14.8 %collective-permute-done.10 = f32[2,128,256]{2,1,0:T(8,128)S(1)} collective-permute-done((f32[2,128,256]{2,1,0:T(8,128)S(1)}, f32[2,128,256]{2,1,0:T(8,128)S(1)}, u32[]{:S(2)}, u32[]{:S(2)}) %collective-permute-start.10) | collective-permute-done | bytes 262176 | tf_op jit(solution)/shard_map/ppermute | solution.py:58
  225.7 0.7 select_add_fusion.1
  226.4 0.7 collective-permute-start.12
  227.1 1.3 collective-permute-start.13
  228.4 1.3 collective-permute-start.14
  229.7 26.3 %reduce-scatter.5.cloned.1.call-done = f32[2,128,256]{2,1,0:T(8,128)} async-done(((f32[2,512,256]{2,1,0:T(8,128)}), f32[2,128,256]{2,1,0:T(8,128)}) %reduce-scatter.5.cloned.1.call-update) | async-done | bytes 262160 | tf_op jit(solution)/shard_map/reduce_scatter | solution.py:137
  256.1 29.5 %collective-permute-done.13 = f32[2,128,256]{2,1,0:T(8,128)S(1)} collective-permute-done((f32[2,128,256]{2,1,0:T(8,128)S(1)}, f32[2,128,256]{2,1,0:T(8,128)S(1)}, u32[]{:S(2)}, u32[]{:S(2)}) %collective-permute-start.13) | collective-permute-done | bytes 262176 | tf_op jit(solution)/shard_map/ppermute | solution.py:58
  285.6 1.7 fusion.21
  (24 shorter events, 0.2 us)
Async XLA Ops:
  6.5 106.3 %all-gather.3.cloned.1.call-start = ((), (), s32[]{:S(2)}) async-start(), calls=%async_computation.2 | async-start | bytes 2228224 | tf_op jit(solution)/shard_map/all_gather | solution.py:99
  7.5 24.8 %collective-permute-start = (bf16[2,128,256]{2,1,0:T(8,128)(2,1)S(1)}, bf16[2,128,256]{2,1,0:T(8,128)(2,1)S(1)}, u32[]{:S(2)}, u32[]{:S(2)}) collective-permute-start(bf16[2,128,256]{2,1,0:T(8,128)(2,1)S(1)} %dynamic-slice_bitcast_fusion), channel_id=1, source_target_pairs={{0,768},{1,769},{2,770},{3,771},{4,772},{5,773},{6,774},{7,775},{8... | collective-permute-start | bytes 393224 | tf_op jit(solution)/shard_map/ppermute | solution.py:44
  24.5 7.8 %collective-permute-start.1 = (bf16[2,128,256]{2,1,0:T(8,128)(2,1)S(1)}, bf16[2,128,256]{2,1,0:T(8,128)(2,1)S(1)}, u32[]{:S(2)}, u32[]{:S(2)}) collective-permute-start(bf16[2,128,256]{2,1,0:T(8,128)(2,1)S(1)} %dynamic-slice_bitcast_fusion), channel_id=1, source_target_pairs={{0,256},{1,257},{2,258},{3,259},{4,260},{5,261},{6,262},{7,263},{8... | collective-permute-start | bytes 393224 | tf_op jit(solution)/shard_map/ppermute | solution.py:44
  33.2 0.7 collective-permute-start.2
  34.0 4.0 %collective-permute-start.3 = (bf16[2,128,256]{2,1,0:T(8,128)(2,1)S(1)}, bf16[2,128,256]{2,1,0:T(8,128)(2,1)S(1)}, u32[]{:S(2)}, u32[]{:S(2)}) collective-permute-start(bf16[2,128,256]{2,1,0:T(8,128)(2,1)S(1)} %broadcast_select_fusion), channel_id=1, source_target_pairs={{0,192},{256,448},{512,704},{768,960},{1,193},{257,449},{513,705},... | collective-permute-start | bytes 393224 | tf_op jit(solution)/shard_map/ppermute | solution.py:44
  35.3 3.2 %collective-permute-start.4 = (bf16[2,128,256]{2,1,0:T(8,128)(2,1)S(1)}, bf16[2,128,256]{2,1,0:T(8,128)(2,1)S(1)}, u32[]{:S(2)}, u32[]{:S(2)}) collective-permute-start(bf16[2,128,256]{2,1,0:T(8,128)(2,1)S(1)} %broadcast_select_fusion), channel_id=1, source_target_pairs={{0,64},{256,320},{512,576},{768,832},{1,65},{257,321},{513,577},{7... | collective-permute-start | bytes 393224 | tf_op jit(solution)/shard_map/ppermute | solution.py:44
  39.8 2.1 collective-permute-start.5
  43.3 161.2 %reduce-scatter.3.cloned.1.call-start = ((), (), s32[]{:S(2)}) async-start(), calls=%async_computation.3 | async-start | bytes 2228224 | tf_op jit(solution)/shard_map/reduce_scatter | solution.py:154
  47.8 6.6 %copy-start.3 = (bf16[1,2,128,4096]{3,2,1,0:T(8,128)(2,1)S(1)}, bf16[1,2,128,4096]{3,2,1,0:T(8,128)(2,1)}, u32[]{:S(2)}) copy-start(bf16[1,2,128,4096]{3,2,1,0:T(8,128)(2,1)} %param.15) | copy-start | bytes 6291460
  54.3 20.4 %copy-start = (bf16[1,2,128,256]{3,2,1,0:T(8,128)(2,1)S(1)}, bf16[1,2,128,256]{3,2,1,0:T(8,128)(2,1)}, u32[]{:S(2)}) copy-start(bf16[1,2,128,256]{3,2,1,0:T(8,128)(2,1)} %param.17) | copy-start | bytes 393220
  119.0 9.6 %collective-permute-start.6 = (f32[3,2,4,512]{3,2,1,0:T(4,128)S(1)}, f32[3,2,4,512]{3,2,1,0:T(4,128)S(1)}, u32[]{:S(2)}, u32[]{:S(2)}) collective-permute-start(f32[3,2,4,512]{3,2,1,0:T(4,128)S(1)} %get-tuple-element.12), channel_id=1, source_target_pairs={{0,16},{16,32},{32,48},{48,0},{1,17},{17,33},{33,49},{49,1},{2,18}... | collective-permute-start | bytes 147464 | tf_op jit(solution)/shard_map/ppermute | solution.py:68
  122.2 6.4 %collective-permute-start.7 = (f32[3,2,4,512]{3,2,1,0:T(4,128)S(1)}, f32[3,2,4,512]{3,2,1,0:T(4,128)S(1)}, u32[]{:S(2)}, u32[]{:S(2)}) collective-permute-start(f32[3,2,4,512]{3,2,1,0:T(4,128)S(1)} %get-tuple-element.12), channel_id=1, source_target_pairs={{0,32},{16,48},{32,0},{48,16},{1,33},{17,49},{33,1},{49,17},{2,34}... | collective-permute-start | bytes 147464 | tf_op jit(solution)/shard_map/ppermute | solution.py:68
  125.2 4.8 %collective-permute-start.8 = (f32[3,2,4,512]{3,2,1,0:T(4,128)S(1)}, f32[3,2,4,512]{3,2,1,0:T(4,128)S(1)}, u32[]{:S(2)}, u32[]{:S(2)}) collective-permute-start(f32[3,2,4,512]{3,2,1,0:T(4,128)S(1)} %get-tuple-element.12), channel_id=1, source_target_pairs={{0,48},{16,0},{32,16},{48,32},{1,49},{17,1},{33,17},{49,33},{2,50}... | collective-permute-start | bytes 147464 | tf_op jit(solution)/shard_map/ppermute | solution.py:68
  130.2 0.6 copy-start.1
  137.4 0.7 copy-start.2
  137.4 118.6 %reduce-scatter.5.cloned.1.call-start = ((), (), s32[]{:S(2)}) async-start(), calls=%async_computation.4 | async-start | bytes 1310720 | tf_op jit(solution)/shard_map/reduce_scatter | solution.py:137
  205.4 0.7 collective-permute-start.9
  207.7 18.0 %collective-permute-start.10 = (f32[2,128,256]{2,1,0:T(8,128)S(1)}, f32[2,128,256]{2,1,0:T(8,128)S(1)}, u32[]{:S(2)}, u32[]{:S(2)}) collective-permute-start(f32[2,128,256]{2,1,0:T(8,128)S(1)} %select_add_fusion.2), channel_id=1, source_target_pairs={{64,0},{320,256},{576,512},{832,768},{65,1},{321,257},{577,513},{8... | collective-permute-start | bytes 786440 | tf_op jit(solution)/shard_map/ppermute | solution.py:58
  209.0 16.7 %collective-permute-start.11 = (f32[2,128,256]{2,1,0:T(8,128)S(1)}, f32[2,128,256]{2,1,0:T(8,128)S(1)}, u32[]{:S(2)}, u32[]{:S(2)}) collective-permute-start(f32[2,128,256]{2,1,0:T(8,128)S(1)} %select_add_fusion.2), channel_id=1, source_target_pairs={{192,0},{448,256},{704,512},{960,768},{193,1},{449,257},{705,513},... | collective-permute-start | bytes 786440 | tf_op jit(solution)/shard_map/ppermute | solution.py:58
  226.4 0.7 collective-permute-start.12
  227.1 58.4 %collective-permute-start.13 = (f32[2,128,256]{2,1,0:T(8,128)S(1)}, f32[2,128,256]{2,1,0:T(8,128)S(1)}, u32[]{:S(2)}, u32[]{:S(2)}) collective-permute-start(f32[2,128,256]{2,1,0:T(8,128)S(1)} %select_add_fusion), channel_id=1, source_target_pairs={{256,0},{257,1},{258,2},{259,3},{260,4},{261,5},{262,6},{263,7},{2... | collective-permute-start | bytes 786440 | tf_op jit(solution)/shard_map/ppermute | solution.py:58
  228.4 57.1 %collective-permute-start.14 = (f32[2,128,256]{2,1,0:T(8,128)S(1)}, f32[2,128,256]{2,1,0:T(8,128)S(1)}, u32[]{:S(2)}, u32[]{:S(2)}) collective-permute-start(f32[2,128,256]{2,1,0:T(8,128)S(1)} %select_add_fusion), channel_id=1, source_target_pairs={{768,0},{769,1},{770,2},{771,3},{772,4},{773,5},{774,6},{775,7},{7... | collective-permute-start | bytes 786440 | tf_op jit(solution)/shard_map/ppermute | solution.py:58
Sparse Core Ops, SparseCore 0:
  43.4 69.3 all-gather.2
  137.6 66.8 reduce-scatter.2
  207.9 48.1 reduce-scatter.4

commit v2 on v1

v2 whole, which is shorter than its diff:
```python
import jax
import jax.numpy as jnp
from jax import lax
from jax.sharding import PartitionSpec as P

HD = 64
X_SIZE = 4


def hi_rounds(n_hi):
    rounds = [[(0, 1)] + ([(0, n_hi - 1)] if n_hi > 2 else [])]
    if n_hi > 3:
        rounds.append([(1, 2)])
    return rounds


def shift_perm(n, shift):
    return [(i, (i + shift) % n) for i in range(n)]


def pick(stacked, index):
    return lax.dynamic_index_in_dim(stacked, index, axis=0, keepdims=False)


def seg_broadcast(value, n_seg):
    seg = lax.axis_index("segment")
    n_hi = n_seg // X_SIZE
    x = seg % X_SIZE
    zh = seg // X_SIZE
    quarter = value.shape[1] // X_SIZE
    pieces = value.reshape(value.shape[0], X_SIZE, quarter, value.shape[2])
    mine = pieces[:, 0]
    for k in range(1, X_SIZE):
        got = lax.ppermute(pieces[:, k], "segment", [(0, k)])
        mine = jnp.where(seg == k, got, mine)
    for pairs in hi_rounds(n_hi):
        nxt = mine
        for a, b in pairs:
            perm = [(a * X_SIZE + c, b * X_SIZE + c) for c in range(X_SIZE)]
            got = lax.ppermute(mine, "segment", perm)
            nxt = jnp.where(zh == b, got, nxt)
        mine = nxt
    parts = [mine]
    for k in range(1, X_SIZE):
        perm = [(z * X_SIZE + c, z * X_SIZE + (c + k) % X_SIZE) for z in range(n_hi) for c in range(X_SIZE)]
        parts.append(lax.ppermute(mine, "segment", perm))
    stacked = jnp.stack(parts)
    full = jnp.stack([pick(stacked, (x - j) % X_SIZE) for j in range(X_SIZE)], axis=1)
    return full.reshape(value.shape)


def seg_reduce(value, n_seg):
    seg = lax.axis_index("segment")
    n_hi = n_seg // X_SIZE
    x = seg % X_SIZE
    zh = seg // X_SIZE
    quarter = value.shape[1] // X_SIZE
    pieces = value.reshape(value.shape[0], X_SIZE, quarter, value.shape[2])
    mine = pick(jnp.moveaxis(pieces, 1, 0), x)
    for k in range(1, X_SIZE):
        send = pick(jnp.moveaxis(pieces, 1, 0), (x + k) % X_SIZE)
        perm = [(z * X_SIZE + c, z * X_SIZE + (c + k) % X_SIZE) for z in range(n_hi) for c in range(X_SIZE)]
        mine = mine + lax.ppermute(send, "segment", perm)
    for pairs in reversed(hi_rounds(n_hi)):
        acc = mine
        for a, b in pairs:
            perm = [(b * X_SIZE + c, a * X_SIZE + c) for c in range(X_SIZE)]
            got = lax.ppermute(mine, "segment", perm)
            acc = acc + jnp.where(zh == a, got, jnp.zeros_like(got))
        mine = acc
    parts = [mine]
    for k in range(1, X_SIZE):
        parts.append(lax.ppermute(mine, "segment", [(k, 0)]))
    return jnp.stack(parts, axis=1).reshape(value.shape)


def tensor_gather(chunk, n_tensor):
    tix = lax.axis_index("tensor")
    core = tix % 2
    y = tix // 2
    n_y = n_tensor // 2
    other = lax.ppermute(chunk, "tensor", [(i, i ^ 1) for i in range(n_tensor)])
    block = jnp.where(core == 0, jnp.concatenate([chunk, other], axis=2),
                      jnp.concatenate([other, chunk], axis=2))
    half = n_y // 2
    ring = [(2 * j, 2 * ((j + 1) % n_y)) for j in range(n_y)]
    ring += [(2 * j + 1, 2 * ((j - 1) % n_y) + 1) for j in range(n_y)]
    collected = []
    cur = block
    for _ in range(half):
        cur = lax.ppermute(cur, "tensor", ring)
        collected.append(cur)
    mine = jnp.stack(collected)
    theirs = lax.ppermute(mine, "tensor", [(i, i ^ 1) for i in range(n_tensor)])
    down = jnp.where(core == 0, mine, theirs)
    up = jnp.where(core == 0, theirs, mine)
    n_up = n_y - 1 - half
    rel = [block] + [up[r - 1] for r in range(1, n_up + 1)] + [down[n_y - r - 1] for r in range(n_up + 1, n_y)]
    stacked = jnp.stack(rel)
    return jnp.concatenate([pick(stacked, (j - y) % n_y) for j in range(n_y)], axis=2)


def shards(inbound, weights, cotangent):
    n_seg = lax.axis_size("segment")
    n_dp = lax.axis_size("dp")
    n_tensor = lax.axis_size("tensor")
    seg = lax.axis_index("segment")
    tix = lax.axis_index("tensor")

    states = inbound[0]
    micro_count, row_count, model_width = states.shape
    layer = weights[0]
    feat_width = layer.shape[2]
    head_count = feat_width // HD
    scale = HD ** (-0.5)
    rows = micro_count * row_count

    query = jnp.dot(
        states.reshape(rows, model_width), layer[:, 0, :], preferred_element_type=jnp.float32
    ).astype(jnp.bfloat16)
    query = query.reshape(micro_count, row_count, feat_width)
    pair = jnp.stack([query, cotangent[0]])
    slots = [pair] + [lax.ppermute(pair, "dp", shift_perm(n_dp, k)) for k in range(1, n_dp)]
    slots = jnp.stack(slots)
    dix = lax.axis_index("dp")
    slots = jnp.stack([pick(slots, (dix - j) % n_dp) for j in range(n_dp)])
    query_heads = slots[:, 0].reshape(n_dp, micro_count, row_count, head_count, HD)
    grad_heads = slots[:, 1].reshape(n_dp, micro_count, row_count, head_count, HD)

    chunk_width = model_width // n_tensor
    chunk = lax.dynamic_slice_in_dim(states, tix * chunk_width, chunk_width, axis=2)
    chunk = seg_broadcast(chunk, n_seg)
    encoded = tensor_gather(chunk, n_tensor)

    pair_weights = layer[:, 1:, :].reshape(model_width, 2 * feat_width)
    keyval = jnp.dot(
        encoded.reshape(rows, model_width), pair_weights, preferred_element_type=jnp.float32
    ).astype(jnp.bfloat16)
    keyval = keyval.reshape(micro_count, row_count, 2, head_count, HD)
    key_heads = keyval[:, :, 0]
    value_heads = keyval[:, :, 1]

    scores = (
        jnp.einsum("jmqhe,mkhe->mhjqk", query_heads, key_heads, preferred_element_type=jnp.float32)
        * scale
    )
    prob_grad = jnp.einsum(
        "jmqhe,mkhe->mhjqk", grad_heads, value_heads, preferred_element_type=jnp.float32
    )
    local_peak = jnp.max(scores, axis=-1)
    local_exp = jnp.exp(scores - local_peak[..., None])
    local_sum = jnp.sum(local_exp, axis=-1)
    local_delta = jnp.sum(local_exp * prob_grad, axis=-1)
    stats = jnp.stack([local_peak, local_sum, local_delta])
    all_stats = jnp.stack(
        [stats] + [lax.ppermute(stats, "dp", shift_perm(n_dp, k)) for k in range(1, n_dp)]
    )
    peaks = all_stats[:, 0]
    peak = jnp.max(peaks, axis=0)
    weight = jnp.exp(peaks - peak[None])
    total = jnp.sum(all_stats[:, 1] * weight, axis=0)
    row_delta = jnp.sum(all_stats[:, 2] * weight, axis=0) / total

    attend_prob = jnp.exp(scores - peak[..., None]) / total[..., None]
    prob_rounded = attend_prob.astype(jnp.bfloat16)
    score_grad = (attend_prob * (prob_grad - row_delta[..., None]) * scale).astype(jnp.bfloat16)

    context_part = jnp.einsum(
        "mhjqk,mkhe->jmqhe", prob_rounded, value_heads, preferred_element_type=jnp.float32
    ).reshape(n_dp, micro_count, row_count, feat_width)
    context = pick(context_part, dix)
    for k in range(1, n_dp):
        send = pick(context_part, (dix - k) % n_dp)
        context = context + lax.ppermute(send, "dp", shift_perm(n_dp, -k))
    context = context.astype(jnp.bfloat16)

    key_grad = jnp.einsum(
        "mhjqk,jmqhe->mkhe", score_grad, query_heads, preferred_element_type=jnp.float32
    ).astype(jnp.bfloat16)
    value_grad = jnp.einsum(
        "mhjqk,jmqhe->mkhe", prob_rounded, grad_heads, preferred_element_type=jnp.float32
    ).astype(jnp.bfloat16)
    joined = jnp.stack(
        [key_grad.reshape(rows, feat_width), value_grad.reshape(rows, feat_width)], axis=1
    ).reshape(rows, 2 * feat_width)
    head_terms = jnp.einsum(
        "rc,dc->rd", joined, pair_weights, preferred_element_type=jnp.float32
    ).astype(jnp.bfloat16)
    head_terms = head_terms.reshape(micro_count, row_count, model_width)
    heads_total = lax.psum_scatter(head_terms, "tensor", scatter_dimension=2, tiled=True).astype(
        jnp.float32
    )
    heads_total = jnp.where(seg > 0, heads_total, jnp.zeros_like(heads_total))
    sections = seg_reduce(heads_total, n_seg)
    encoder_grad = (sections + cotangent[0].astype(jnp.float32)).astype(jnp.bfloat16)
    result = jnp.where(seg == 0, encoder_grad, context)
    return result[None]


def solution(mesh):
    placed = (
        P("segment", None, "dp", None),
        P("segment", None, None, "tensor"),
        P("segment", None, "dp", "tensor"),
    )
    return jax.shard_map(
        shards,
        mesh=mesh,
        in_specs=placed,
        out_specs=P("segment", None, "dp", "tensor"),
        check_vma=False,
    )
```

time: 295 us -> 300 us (1.017)
  the two profiles are of different devices: /device:TPU:121 before, /device:TPU:56 now
where the time goes in v2:
time: 300 us; the launch traced here: 298 us
  waiting for transfers between devices  129 us (43%)
  starting transfers between devices  99.7 us (33%)
  local copies, waits for them, and re-layouts  27.7 us (9%)
  between operations  14.7 us (5%)
  other arithmetic  13.9 us (5%)
  matrix products  13.1 us (4%)
    reduce_scatter x1, waiting for transfers between devices, shards(): lax.psum_scatter(head_terms, 'tensor', scatter_dimension=2, tiled=True)  71.9 us
    ppermute x4, waiting for transfers between devices, tensor_gather(): cur = lax.ppermute(cur, 'tensor', ring)  15.4 us
    ppermute x4, starting transfers between devices, tensor_gather(): cur = lax.ppermute(cur, 'tensor', ring)  14.9 us
    ppermute x3, starting transfers between devices, seg_broadcast(): got = lax.ppermute(mine, 'segment', perm)  13.4 us
    ppermute x3, starting transfers between devices, seg_broadcast(): parts.append(lax.ppermute(mine, 'segment', perm))  11.4 us
    ppermute x3, starting transfers between devices, seg_reduce(): mine = mine + lax.ppermute(send, 'segment', perm)  11.2 us
    slice x2, local copies, waits for them, and re-layouts, shards(): pair_weights = layer[:, 1:, :].reshape(model_width, 2 * feat_width)  10.9 us
    ppermute x3, starting transfers between devices, shards(): lax.ppermute(pair, 'dp', shift_perm(n_dp, k))  10.7 us
  transfers between devices with their start and end apart: 34, of which 18 were waited for; matrix products, arithmetic and copies ran while one was open for 8% of the time, Pallas kernels for 0%

profile of v2, /device:TPU:56, one launch (start us, length us, event | category | flops | bytes accessed | tf_op | source)
XLA Modules:
  0.0 298.4 jit_solution(12921453819731008207)
XLA Ops:
  6.5 1.6 copy-done
  8.2 4.7 %collective-permute-start.3 = (bf16[2,32,256]{2,1,0:T(8,128)(2,1)S(1)}, bf16[2,32,256]{2,1,0:T(8,128)(2,1)S(1)}, u32[]{:S(2)}, u32[]{:S(2)}) collective-permute-start(bf16[2,32,256]{2,1,0:T(8,128)(2,1)S(1)} %get-tuple-element.42), channel_id=1, source_target_pairs={{0,192},{1,193},{2,194},{3,195},{4,196},{5,197},{6,198},{7,199},{8... | collective-permute-start | bytes 98312 | tf_op jit(solution)/shard_map/ppermute | solution.py:34
  12.8 1.3 collective-permute-start.4
  14.1 1.3 collective-permute-start.5
  15.7 1.3 collective-permute-done.5
  17.0 11.4 %collective-permute-start.6 = (bf16[2,32,256]{2,1,0:T(8,128)(2,1)S(1)}, bf16[2,32,256]{2,1,0:T(8,128)(2,1)S(1)}, u32[]{:S(2)}, u32[]{:S(2)}) collective-permute-start(bf16[2,32,256]{2,1,0:T(8,128)(2,1)S(1)} %fusion.38), channel_id=1, source_target_pairs={{0,768},{64,832},{128,896},{192,960},{1,769},{65,833},{129,897},{1... | collective-permute-start | bytes 98312 | tf_op jit(solution)/shard_map/ppermute | solution.py:40
  28.4 1.3 collective-permute-start.7
  30.0 1.3 collective-permute-done.7
  32.0 3.4 %collective-permute-start.9 = (bf16[2,32,256]{2,1,0:T(8,128)(2,1)S(1)}, bf16[2,32,256]{2,1,0:T(8,128)(2,1)S(1)}, u32[]{:S(2)}, u32[]{:S(2)}) collective-permute-start(bf16[2,32,256]{2,1,0:T(8,128)(2,1)S(1)} %broadcast_select_fusion.1), channel_id=1, source_target_pairs={{0,64},{64,128},{128,192},{192,0},{256,320},{320,384},{384,448},{4... | collective-permute-start | bytes 98312 | tf_op jit(solution)/shard_map/ppermute | solution.py:46
  35.4 4.6 %collective-permute-start.10 = (bf16[2,32,256]{2,1,0:T(8,128)(2,1)S(1)}, bf16[2,32,256]{2,1,0:T(8,128)(2,1)S(1)}, u32[]{:S(2)}, u32[]{:S(2)}) collective-permute-start(bf16[2,32,256]{2,1,0:T(8,128)(2,1)S(1)} %broadcast_select_fusion.1), channel_id=1, source_target_pairs={{0,128},{64,192},{128,0},{192,64},{256,384},{320,448},{384,256},{4... | collective-permute-start | bytes 98312 | tf_op jit(solution)/shard_map/ppermute | solution.py:46
  40.1 3.3 %collective-permute-start.11 = (bf16[2,32,256]{2,1,0:T(8,128)(2,1)S(1)}, bf16[2,32,256]{2,1,0:T(8,128)(2,1)S(1)}, u32[]{:S(2)}, u32[]{:S(2)}) collective-permute-start(bf16[2,32,256]{2,1,0:T(8,128)(2,1)S(1)} %broadcast_select_fusion.1), channel_id=1, source_target_pairs={{0,192},{64,0},{128,64},{192,128},{256,448},{320,256},{384,320},{4... | collective-permute-start | bytes 98312 | tf_op jit(solution)/shard_map/ppermute | solution.py:46
  43.5 2.3 collective-permute-done.11
  46.0 1.9 collective-permute-start.12
  47.9 1.3 collective-permute-done.12
  49.3 1.9 collective-permute-start.13
  51.3 6.3 %collective-permute-done.13 = bf16[2,128,512]{2,1,0:T(8,128)(2,1)S(1)} collective-permute-done((bf16[2,128,512]{2,1,0:T(8,128)(2,1)S(1)}, bf16[2,128,512]{2,1,0:T(8,128)(2,1)S(1)}, u32[]{:S(2)}, u32[]{:S(2)}) %collective-permute-start.13) | collective-permute-done | bytes 262176 | tf_op jit(solution)/shard_map/ppermute | solution.py:91
  57.6 3.1 %collective-permute-start.14 = (bf16[2,128,512]{2,1,0:T(8,128)(2,1)S(1)}, bf16[2,128,512]{2,1,0:T(8,128)(2,1)S(1)}, u32[]{:S(2)}, u32[]{:S(2)}) collective-permute-start(bf16[2,128,512]{2,1,0:T(8,128)(2,1)S(1)} %collective-permute-done.13), channel_id=1, source_target_pairs={{0,2},{2,4},{4,6},{6,8},{8,10},{10,12},{12,14},{14,0},{1,15},{3,1}... | collective-permute-start | bytes 786440 | tf_op jit(solution)/shard_map/ppermute | solution.py:91
  60.7 5.1 %collective-permute-done.14 = bf16[2,128,512]{2,1,0:T(8,128)(2,1)S(1)} collective-permute-done((bf16[2,128,512]{2,1,0:T(8,128)(2,1)S(1)}, bf16[2,128,512]{2,1,0:T(8,128)(2,1)S(1)}, u32[]{:S(2)}, u32[]{:S(2)}) %collective-permute-start.14) | collective-permute-done | bytes 262176 | tf_op jit(solution)/shard_map/ppermute | solution.py:91
  65.9 4.3 %collective-permute-start.15 = (bf16[2,128,512]{2,1,0:T(8,128)(2,1)S(1)}, bf16[2,128,512]{2,1,0:T(8,128)(2,1)S(1)}, u32[]{:S(2)}, u32[]{:S(2)}) collective-permute-start(bf16[2,128,512]{2,1,0:T(8,128)(2,1)S(1)} %collective-permute-done.14), channel_id=1, source_target_pairs={{0,2},{2,4},{4,6},{6,8},{8,10},{10,12},{12,14},{14,0},{1,15},{3,1}... | collective-permute-start | bytes 786440 | tf_op jit(solution)/shard_map/ppermute | solution.py:91
  70.2 3.9 %collective-permute-done.15 = bf16[2,128,512]{2,1,0:T(8,128)(2,1)S(1)} collective-permute-done((bf16[2,128,512]{2,1,0:T(8,128)(2,1)S(1)}, bf16[2,128,512]{2,1,0:T(8,128)(2,1)S(1)}, u32[]{:S(2)}, u32[]{:S(2)}) %collective-permute-start.15) | collective-permute-done | bytes 262176 | tf_op jit(solution)/shard_map/ppermute | solution.py:91
  74.1 5.5 %collective-permute-start.16 = (bf16[2,128,512]{2,1,0:T(8,128)(2,1)S(1)}, bf16[2,128,512]{2,1,0:T(8,128)(2,1)S(1)}, u32[]{:S(2)}, u32[]{:S(2)}) collective-permute-start(bf16[2,128,512]{2,1,0:T(8,128)(2,1)S(1)} %collective-permute-done.15), channel_id=1, source_target_pairs={{0,2},{2,4},{4,6},{6,8},{8,10},{10,12},{12,14},{14,0},{1,15},{3,1}... | collective-permute-start | bytes 786440 | tf_op jit(solution)/shard_map/ppermute | solution.py:91
  79.7 2.3 fusion.3
  84.3 1.2 pad_maximum_fusion.2
  85.5 1.9 collective-permute-start.17
  88.2 6.3 %collective-permute-start.2 = (bf16[2,2,128,256]{2,3,1,0:T(8,128)(2,1)}, bf16[2,2,128,256]{2,3,1,0:T(8,128)(2,1)}, u32[]{:S(2)}, u32[]{:S(2)}) collective-permute-start(bf16[2,2,128,256]{2,3,1,0:T(8,128)(2,1)} %get-tuple-element.35), channel_id=1, source_target_pairs={{0,48},{16,0},{32,16},{48,32},{1,49},{17,1},{33,17},{49,33},{2,50}... | collective-permute-start | bytes 786440 | tf_op jit(solution)/shard_map/ppermute | solution.py:123
  94.6 1.9 collective-permute-start
  96.5 2.5 collective-permute-start.1
  99.1 4.5 %slice.87 = bf16[4096,2,256]{2,0,1:T(8,128)(2,1)} slice(bf16[4096,3,256]{2,0,1:T(8,128)(2,1)} %bitcast.204), slice={[0:4096], [1:3], [0:256]} | slice | bytes 8388608 | tf_op jit(solution)/shard_map/slice | solution.py:135
  103.6 6.4 %copy.52 = bf16[4096,2,256]{0,2,1:T(8,128)(2,1)} copy(bf16[4096,2,256]{2,0,1:T(8,128)(2,1)} %slice.87) | data formatting | bytes 8388608 | tf_op jit(solution)/shard_map/slice | solution.py:135
  111.1 7.5 %collective-permute-done.1 = bf16[2,2,128,256]{2,3,1,0:T(8,128)(2,1)} collective-permute-done((bf16[2,2,128,256]{2,3,1,0:T(8,128)(2,1)}, bf16[2,2,128,256]{2,3,1,0:T(8,128)(2,1)}, u32[]{:S(2)}, u32[]{:S(2)}) %collective-permute-start.1) | collective-permute-done | bytes 262176 | tf_op jit(solution)/shard_map/ppermute | solution.py:123
  118.7 1.2 pad_maximum_fusion
  121.6 1.3 fusion.8
  123.5 1.9 copy-done.1
  125.4 1.3 convolution_convert_fusion
  127.9 1.1 copy.99
  129.1 1.5 multiply_reduce_fusion.1
  131.5 2.1 collective-permute-start.18
  133.6 5.3 %collective-permute-start.19 = (f32[3,2,4,4,128]{4,3,2,1,0:T(4,128)S(1)}, f32[3,2,4,4,128]{4,3,2,1,0:T(4,128)S(1)}, u32[]{:S(2)}, u32[]{:S(2)}) collective-permute-start(f32[3,2,4,4,128]{4,3,2,1,0:T(4,128)S(1)} %get-tuple-element.44), channel_id=1, source_target_pairs={{0,32},{16,48},{32,0},{48,16},{1,33},{17,49},{33,1},{49,17},{2,34}... | collective-permute-start | bytes 147464 | tf_op jit(solution)/shard_map/ppermute | solution.py:156
  138.9 2.1 collective-permute-start.20
  141.1 1.3 collective-permute-done.19
  142.3 2.6 collective-permute-done.20
  147.2 1.1 copy.89
  149.2 1.5 fusion.4
  151.4 1.1 copy.91
  153.3 5.0 %fusion = bf16[256,4096]{1,0:T(8,128)(2,1)} fusion(bf16[256,1,256]{2,0,1:T(8,128)(2,1)} %reshape.139, bf16[256,1,256]{2,0,1:T(8,128)(2,1)} %reshape.138, bf16[4096,3,256]{2,0,1:T(8,128)(2,1)} %bitcast.205), kind=kOutput, calls=%fused_computation.1 | convolution fusion | flops 1074921472 | bytes 6553600 | tf_op jit(solution)/shard_map/rc,dc->rd/dot_general | solution.py:186
  158.4 71.9 %reduce-scatter.2.cloned.1.call-done = bf16[2,128,256]{2,1,0:T(8,128)(2,1)} async-done(((bf16[2,128,4096]{2,1,0:T(8,128)(2,1)}), bf16[2,128,256]{2,1,0:T(8,128)(2,1)}) %reduce-scatter.2.cloned.1.call-update) | async-done | bytes 131088 | tf_op jit(solution)/shard_map/reduce_scatter | solution.py:190
  231.9 3.2 %collective-permute-start.21 = (f32[2,32,256]{2,1,0:T(8,128)}, f32[2,32,256]{2,1,0:T(8,128)}, u32[]{:S(2)}, u32[]{:S(2)}) collective-permute-start(f32[2,32,256]{2,1,0:T(8,128)} %get-tuple-element.31), channel_id=1, source_target_pairs={{0,64},{64,128},{128,192},{192,0},{256,320},{320,384},{384,448},{4... | collective-permute-start | bytes 196616 | tf_op jit(solution)/shard_map/ppermute | solution.py:63
  235.1 4.6 %collective-permute-start.22 = (f32[2,32,256]{2,1,0:T(8,128)}, f32[2,32,256]{2,1,0:T(8,128)}, u32[]{:S(2)}, u32[]{:S(2)}) collective-permute-start(f32[2,32,256]{2,1,0:T(8,128)} %get-tuple-element.32), channel_id=1, source_target_pairs={{0,128},{64,192},{128,0},{192,64},{256,384},{320,448},{384,256},{4... | collective-permute-start | bytes 196616 | tf_op jit(solution)/shard_map/ppermute | solution.py:63
  239.7 3.4 %collective-permute-start.23 = (f32[2,32,256]{2,1,0:T(8,128)}, f32[2,32,256]{2,1,0:T(8,128)}, u32[]{:S(2)}, u32[]{:S(2)}) collective-permute-start(f32[2,32,256]{2,1,0:T(8,128)} %get-tuple-element.33), channel_id=1, source_target_pairs={{0,192},{64,0},{128,64},{192,128},{256,448},{320,256},{384,320},{4... | collective-permute-start | bytes 196616 | tf_op jit(solution)/shard_map/ppermute | solution.py:63
  243.1 3.4 %collective-permute-done.23 = f32[2,32,256]{2,1,0:T(8,128)} collective-permute-done((f32[2,32,256]{2,1,0:T(8,128)}, f32[2,32,256]{2,1,0:T(8,128)}, u32[]{:S(2)}, u32[]{:S(2)}) %collective-permute-start.23) | collective-permute-done | bytes 65568 | tf_op jit(solution)/shard_map/ppermute | solution.py:63
  249.1 1.3 collective-permute-start.25
  250.4 1.3 collective-permute-start.26
  251.9 5.7 %collective-permute-start.30 = (f32[2,128,256]{2,1,0:T(8,128)S(1)}, f32[2,128,256]{2,1,0:T(8,128)}, u32[]{:S(2)}, u32[]{:S(2)}) collective-permute-start(f32[2,128,256]{2,1,0:T(8,128)S(1)} %bitcast.237), channel_id=1, source_target_pairs={{0,48},{16,0},{32,16},{48,32},{1,49},{17,1},{33,17},{49,33},{2,50}... | collective-permute-start | bytes 786440 | tf_op jit(solution)/shard_map/ppermute | solution.py:174
  257.8 1.9 collective-permute-start.31
  259.9 2.8 collective-permute-start.32
  262.7 10.4 %collective-permute-done.25 = f32[2,32,256]{2,1,0:T(8,128)} collective-permute-done((f32[2,32,256]{2,1,0:T(8,128)}, f32[2,32,256]{2,1,0:T(8,128)}, u32[]{:S(2)}, u32[]{:S(2)}) %collective-permute-start.25) | collective-permute-done | bytes 65568 | tf_op jit(solution)/shard_map/ppermute | solution.py:68
  273.1 1.5 select_add_fusion
  274.7 1.3 collective-permute-start.27
  275.9 1.3 collective-permute-start.28
  277.2 3.8 %collective-permute-done.27 = f32[2,32,256]{2,1,0:T(8,128)S(1)} collective-permute-done((f32[2,32,256]{2,1,0:T(8,128)}, f32[2,32,256]{2,1,0:T(8,128)S(1)}, u32[]{:S(2)}, u32[]{:S(2)}) %collective-permute-start.27) | collective-permute-done | bytes 65568 | tf_op jit(solution)/shard_map/ppermute | solution.py:73
  281.0 1.3 collective-permute-start.29
  282.5 1.5 collective-permute-done.28
  283.9 4.8 %collective-permute-done.29 = f32[2,32,256]{2,1,0:T(8,128)} collective-permute-done((f32[2,32,256]{2,1,0:T(8,128)}, f32[2,32,256]{2,1,0:T(8,128)}, u32[]{:S(2)}, u32[]{:S(2)}) %collective-permute-start.29) | collective-permute-done | bytes 65568 | tf_op jit(solution)/shard_map/ppermute | solution.py:73
  289.7 1.9 fusion.25
  (114 shorter events, 20.1 us)
Async XLA Ops:
  6.5 1.6 copy-start
  6.5 223.7 %reduce-scatter.2.cloned.1.call-start = ((), (), s32[]{:S(2)}) async-start(), calls=%async_computation.1 | async-start | bytes 2228224 | tf_op jit(solution)/shard_map/reduce_scatter | solution.py:190
  8.2 7.3 %collective-permute-start.3 = (bf16[2,32,256]{2,1,0:T(8,128)(2,1)S(1)}, bf16[2,32,256]{2,1,0:T(8,128)(2,1)S(1)}, u32[]{:S(2)}, u32[]{:S(2)}) collective-permute-start(bf16[2,32,256]{2,1,0:T(8,128)(2,1)S(1)} %get-tuple-element.42), channel_id=1, source_target_pairs={{0,192},{1,193},{2,194},{3,195},{4,196},{5,197},{6,198},{7,199},{8... | collective-permute-start | bytes 98312 | tf_op jit(solution)/shard_map/ppermute | solution.py:34
  12.8 2.9 collective-permute-start.4
  14.1 2.9 collective-permute-start.5
  17.0 13.0 %collective-permute-start.6 = (bf16[2,32,256]{2,1,0:T(8,128)(2,1)S(1)}, bf16[2,32,256]{2,1,0:T(8,128)(2,1)S(1)}, u32[]{:S(2)}, u32[]{:S(2)}) collective-permute-start(bf16[2,32,256]{2,1,0:T(8,128)(2,1)S(1)} %fusion.38), channel_id=1, source_target_pairs={{0,768},{64,832},{128,896},{192,960},{1,769},{65,833},{129,897},{1... | collective-permute-start | bytes 98312 | tf_op jit(solution)/shard_map/ppermute | solution.py:40
  28.4 2.9 collective-permute-start.7
  31.3 0.7 collective-permute-start.8
  32.0 11.5 %collective-permute-start.9 = (bf16[2,32,256]{2,1,0:T(8,128)(2,1)S(1)}, bf16[2,32,256]{2,1,0:T(8,128)(2,1)S(1)}, u32[]{:S(2)}, u32[]{:S(2)}) collective-permute-start(bf16[2,32,256]{2,1,0:T(8,128)(2,1)S(1)} %broadcast_select_fusion.1), channel_id=1, source_target_pairs={{0,64},{64,128},{128,192},{192,0},{256,320},{320,384},{384,448},{4... | collective-permute-start | bytes 98312 | tf_op jit(solution)/shard_map/ppermute | solution.py:46
  35.4 8.1 %collective-permute-start.10 = (bf16[2,32,256]{2,1,0:T(8,128)(2,1)S(1)}, bf16[2,32,256]{2,1,0:T(8,128)(2,1)S(1)}, u32[]{:S(2)}, u32[]{:S(2)}) collective-permute-start(bf16[2,32,256]{2,1,0:T(8,128)(2,1)S(1)} %broadcast_select_fusion.1), channel_id=1, source_target_pairs={{0,128},{64,192},{128,0},{192,64},{256,384},{320,448},{384,256},{4... | collective-permute-start | bytes 98312 | tf_op jit(solution)/shard_map/ppermute | solution.py:46
  40.1 5.8 %collective-permute-start.11 = (bf16[2,32,256]{2,1,0:T(8,128)(2,1)S(1)}, bf16[2,32,256]{2,1,0:T(8,128)(2,1)S(1)}, u32[]{:S(2)}, u32[]{:S(2)}) collective-permute-start(bf16[2,32,256]{2,1,0:T(8,128)(2,1)S(1)} %broadcast_select_fusion.1), channel_id=1, source_target_pairs={{0,192},{64,0},{128,64},{192,128},{256,448},{320,256},{384,320},{4... | collective-permute-start | bytes 98312 | tf_op jit(solution)/shard_map/ppermute | solution.py:46
  46.0 3.2 %collective-permute-start.12 = (bf16[2,128,256]{2,1,0:T(8,128)(2,1)S(1)}, bf16[2,128,256]{2,1,0:T(8,128)(2,1)S(1)}, u32[]{:S(2)}, u32[]{:S(2)}) collective-permute-start(bf16[2,128,256]{2,1,0:T(8,128)(2,1)S(1)} %bitcast.211), channel_id=1, source_target_pairs={{0,1},{1,0},{2,3},{3,2},{4,5},{5,4},{6,7},{7,6},{8,9},{9,8},{10,11... | collective-permute-start | bytes 393224 | tf_op jit(solution)/shard_map/ppermute | solution.py:82
  49.2 2.1 copy-start.12
  49.3 8.3 %collective-permute-start.13 = (bf16[2,128,512]{2,1,0:T(8,128)(2,1)S(1)}, bf16[2,128,512]{2,1,0:T(8,128)(2,1)S(1)}, u32[]{:S(2)}, u32[]{:S(2)}) collective-permute-start(bf16[2,128,512]{2,1,0:T(8,128)(2,1)S(1)} %maximum_select_fusion.1), channel_id=1, source_target_pairs={{0,2},{2,4},{4,6},{6,8},{8,10},{10,12},{12,14},{14,0},{1,15},{3,1}... | collective-permute-start | bytes 786440 | tf_op jit(solution)/shard_map/ppermute | solution.py:91
  57.6 26.7 %copy-start.4 = (bf16[2,128,512]{2,1,0:T(8,128)(2,1)}, bf16[2,128,512]{2,1,0:T(8,128)(2,1)S(1)}, u32[]{:S(2)}) copy-start(bf16[2,128,512]{2,1,0:T(8,128)(2,1)S(1)} %collective-permute-done.13) | copy-start | bytes 786436
  57.6 8.3 %collective-permute-start.14 = (bf16[2,128,512]{2,1,0:T(8,128)(2,1)S(1)}, bf16[2,128,512]{2,1,0:T(8,128)(2,1)S(1)}, u32[]{:S(2)}, u32[]{:S(2)}) collective-permute-start(bf16[2,128,512]{2,1,0:T(8,128)(2,1)S(1)} %collective-permute-done.13), channel_id=1, source_target_pairs={{0,2},{2,4},{4,6},{6,8},{8,10},{10,12},{12,14},{14,0},{1,15},{3,1}... | collective-permute-start | bytes 786440 | tf_op jit(solution)/shard_map/ppermute | solution.py:91
  65.9 16.2 %copy-start.6 = (bf16[2,128,512]{2,1,0:T(8,128)(2,1)}, bf16[2,128,512]{2,1,0:T(8,128)(2,1)S(1)}, u32[]{:S(2)}) copy-start(bf16[2,128,512]{2,1,0:T(8,128)(2,1)S(1)} %collective-permute-done.14) | copy-start | bytes 786436
  65.9 8.3 %collective-permute-start.15 = (bf16[2,128,512]{2,1,0:T(8,128)(2,1)S(1)}, bf16[2,128,512]{2,1,0:T(8,128)(2,1)S(1)}, u32[]{:S(2)}, u32[]{:S(2)}) collective-permute-start(bf16[2,128,512]{2,1,0:T(8,128)(2,1)S(1)} %collective-permute-done.14), channel_id=1, source_target_pairs={{0,2},{2,4},{4,6},{6,8},{8,10},{10,12},{12,14},{14,0},{1,15},{3,1}... | collective-permute-start | bytes 786440 | tf_op jit(solution)/shard_map/ppermute | solution.py:91
  74.1 7.9 %copy-start.8 = (bf16[2,128,512]{2,1,0:T(8,128)(2,1)}, bf16[2,128,512]{2,1,0:T(8,128)(2,1)S(1)}, u32[]{:S(2)}) copy-start(bf16[2,128,512]{2,1,0:T(8,128)(2,1)S(1)} %collective-permute-done.15) | copy-start | bytes 786436
  74.1 9.5 %collective-permute-start.16 = (bf16[2,128,512]{2,1,0:T(8,128)(2,1)S(1)}, bf16[2,128,512]{2,1,0:T(8,128)(2,1)S(1)}, u32[]{:S(2)}, u32[]{:S(2)}) collective-permute-start(bf16[2,128,512]{2,1,0:T(8,128)(2,1)S(1)} %collective-permute-done.15), channel_id=1, source_target_pairs={{0,2},{2,4},{4,6},{6,8},{8,10},{10,12},{12,14},{14,0},{1,15},{3,1}... | collective-permute-start | bytes 786440 | tf_op jit(solution)/shard_map/ppermute | solution.py:91
  79.7 3.1 %copy-start.13 = (bf16[1,2,128,256]{3,2,1,0:T(8,128)(2,1)S(1)}, bf16[1,2,128,256]{3,2,1,0:T(8,128)(2,1)}, u32[]{:S(2)}) copy-start(bf16[1,2,128,256]{3,2,1,0:T(8,128)(2,1)} %param.5) | copy-start | bytes 393220
  83.6 3.9 %copy-start.15 = (bf16[1,2,128,256]{2,3,1,0:T(8,128)(2,1)S(1)}, bf16[1,2,128,256]{2,3,1,0:T(8,128)(2,1)}, u32[]{:S(2)}) copy-start(bf16[1,2,128,256]{2,3,1,0:T(8,128)(2,1)} %copy.44) | copy-start | bytes 393220
  83.6 3.9 %copy-start.16 = (bf16[1,2,128,256]{2,3,1,0:T(8,128)(2,1)S(1)}, bf16[1,2,128,256]{2,3,1,0:T(8,128)(2,1)}, u32[]{:S(2)}) copy-start(bf16[1,2,128,256]{2,3,1,0:T(8,128)(2,1)} %copy.45) | copy-start | bytes 393220
  83.6 0.7 copy-start.10
  85.5 35.8 %collective-permute-start.17 = (bf16[4,2,128,512]{3,2,1,0:T(8,128)(2,1)S(1)}, bf16[4,2,128,512]{3,2,1,0:T(8,128)(2,1)}, u32[]{:S(2)}, u32[]{:S(2)}) collective-permute-start(bf16[4,2,128,512]{3,2,1,0:T(8,128)(2,1)S(1)} %pad_maximum_fusion.2), channel_id=1, source_target_pairs={{0,1},{1,0},{2,3},{3,2},{4,5},{5,4},{6,7},{7,6},{8,9},{9,8},{10,11... | collective-permute-start | bytes 3145736 | tf_op jit(solution)/shard_map/ppermute | solution.py:94
  88.2 22.9 %collective-permute-start.2 = (bf16[2,2,128,256]{2,3,1,0:T(8,128)(2,1)}, bf16[2,2,128,256]{2,3,1,0:T(8,128)(2,1)}, u32[]{:S(2)}, u32[]{:S(2)}) collective-permute-start(bf16[2,2,128,256]{2,3,1,0:T(8,128)(2,1)} %get-tuple-element.35), channel_id=1, source_target_pairs={{0,48},{16,0},{32,16},{48,32},{1,49},{17,1},{33,17},{49,33},{2,50}... | collective-permute-start | bytes 786440 | tf_op jit(solution)/shard_map/ppermute | solution.py:123
  94.6 16.6 %collective-permute-start = (bf16[2,2,128,256]{2,3,1,0:T(8,128)(2,1)}, bf16[2,2,128,256]{2,3,1,0:T(8,128)(2,1)}, u32[]{:S(2)}, u32[]{:S(2)}) collective-permute-start(bf16[2,2,128,256]{2,3,1,0:T(8,128)(2,1)} %get-tuple-element.35), channel_id=1, source_target_pairs={{0,16},{16,32},{32,48},{48,0},{1,17},{17,33},{33,49},{49,1},{2,18}... | collective-permute-start | bytes 786440 | tf_op jit(solution)/shard_map/ppermute | solution.py:123
  96.5 22.2 %collective-permute-start.1 = (bf16[2,2,128,256]{2,3,1,0:T(8,128)(2,1)}, bf16[2,2,128,256]{2,3,1,0:T(8,128)(2,1)}, u32[]{:S(2)}, u32[]{:S(2)}) collective-permute-start(bf16[2,2,128,256]{2,3,1,0:T(8,128)(2,1)} %get-tuple-element.35), channel_id=1, source_target_pairs={{0,32},{16,48},{32,0},{48,16},{1,33},{17,49},{33,1},{49,17},{2,34}... | collective-permute-start | bytes 786440 | tf_op jit(solution)/shard_map/ppermute | solution.py:123
  120.0 1.3 copy-start.5
  120.1 1.3 copy-start.7
  120.1 1.2 copy-start.9
  120.1 1.3 copy-start.11
  123.2 2.2 copy-start.1
  127.0 3.7 %copy-start.2 = (bf16[4,1,2,128,256]{3,4,2,0,1:T(8,128)(2,1)S(1)}, bf16[4,1,2,128,256]{3,4,2,0,1:T(8,128)(2,1)}, u32[]{:S(2)}) copy-start(bf16[4,1,2,128,256]{3,4,2,0,1:T(8,128)(2,1)} %get-tuple-element.23) | copy-start | bytes 1572868
  131.5 9.6 %collective-permute-start.18 = (f32[3,2,4,4,128]{4,3,2,1,0:T(4,128)S(1)}, f32[3,2,4,4,128]{4,3,2,1,0:T(4,128)S(1)}, u32[]{:S(2)}, u32[]{:S(2)}) collective-permute-start(f32[3,2,4,4,128]{4,3,2,1,0:T(4,128)S(1)} %get-tuple-element.44), channel_id=1, source_target_pairs={{0,16},{16,32},{32,48},{48,0},{1,17},{17,33},{33,49},{49,1},{2,18}... | collective-permute-start | bytes 147464 | tf_op jit(solution)/shard_map/ppermute | solution.py:156
  133.6 8.7 %collective-permute-start.19 = (f32[3,2,4,4,128]{4,3,2,1,0:T(4,128)S(1)}, f32[3,2,4,4,128]{4,3,2,1,0:T(4,128)S(1)}, u32[]{:S(2)}, u32[]{:S(2)}) collective-permute-start(f32[3,2,4,4,128]{4,3,2,1,0:T(4,128)S(1)} %get-tuple-element.44), channel_id=1, source_target_pairs={{0,32},{16,48},{32,0},{48,16},{1,33},{17,49},{33,1},{49,17},{2,34}... | collective-permute-start | bytes 147464 | tf_op jit(solution)/shard_map/ppermute | solution.py:156
  138.9 6.0 %collective-permute-start.20 = (f32[3,2,4,4,128]{4,3,2,1,0:T(4,128)S(1)}, f32[3,2,4,4,128]{4,3,2,1,0:T(4,128)S(1)}, u32[]{:S(2)}, u32[]{:S(2)}) collective-permute-start(f32[3,2,4,4,128]{4,3,2,1,0:T(4,128)S(1)} %get-tuple-element.44), channel_id=1, source_target_pairs={{0,48},{16,0},{32,16},{48,32},{1,49},{17,1},{33,17},{49,33},{2,50}... | collective-permute-start | bytes 147464 | tf_op jit(solution)/shard_map/ppermute | solution.py:156
  145.0 1.0 copy-start.3
  231.9 11.2 %collective-permute-start.21 = (f32[2,32,256]{2,1,0:T(8,128)}, f32[2,32,256]{2,1,0:T(8,128)}, u32[]{:S(2)}, u32[]{:S(2)}) collective-permute-start(f32[2,32,256]{2,1,0:T(8,128)} %get-tuple-element.31), channel_id=1, source_target_pairs={{0,64},{64,128},{128,192},{192,0},{256,320},{320,384},{384,448},{4... | collective-permute-start | bytes 196616 | tf_op jit(solution)/shard_map/ppermute | solution.py:63
  235.1 8.0 %collective-permute-start.22 = (f32[2,32,256]{2,1,0:T(8,128)}, f32[2,32,256]{2,1,0:T(8,128)}, u32[]{:S(2)}, u32[]{:S(2)}) collective-permute-start(f32[2,32,256]{2,1,0:T(8,128)} %get-tuple-element.32), channel_id=1, source_target_pairs={{0,128},{64,192},{128,0},{192,64},{256,384},{320,448},{384,256},{4... | collective-permute-start | bytes 196616 | tf_op jit(solution)/shard_map/ppermute | solution.py:63
  239.7 6.8 %collective-permute-start.23 = (f32[2,32,256]{2,1,0:T(8,128)}, f32[2,32,256]{2,1,0:T(8,128)}, u32[]{:S(2)}, u32[]{:S(2)}) collective-permute-start(f32[2,32,256]{2,1,0:T(8,128)} %get-tuple-element.33), channel_id=1, source_target_pairs={{0,192},{64,0},{128,64},{192,128},{256,448},{320,256},{384,320},{4... | collective-permute-start | bytes 196616 | tf_op jit(solution)/shard_map/ppermute | solution.py:63
  247.4 1.1 collective-permute-start.24
  249.1 24.0 %collective-permute-start.25 = (f32[2,32,256]{2,1,0:T(8,128)}, f32[2,32,256]{2,1,0:T(8,128)}, u32[]{:S(2)}, u32[]{:S(2)}) collective-permute-start(f32[2,32,256]{2,1,0:T(8,128)} %select_add_fusion.1), channel_id=1, source_target_pairs={{256,0},{320,64},{384,128},{448,192},{257,1},{321,65},{385,129},{4... | collective-permute-start | bytes 196616 | tf_op jit(solution)/shard_map/ppermute | solution.py:68
  250.4 22.7 %collective-permute-start.26 = (f32[2,32,256]{2,1,0:T(8,128)}, f32[2,32,256]{2,1,0:T(8,128)}, u32[]{:S(2)}, u32[]{:S(2)}) collective-permute-start(f32[2,32,256]{2,1,0:T(8,128)} %select_add_fusion.1), channel_id=1, source_target_pairs={{768,0},{832,64},{896,128},{960,192},{769,1},{833,65},{897,129},{9... | collective-permute-start | bytes 196616 | tf_op jit(solution)/shard_map/ppermute | solution.py:68
  251.8 37.9 %copy-start.14 = (bf16[1,2,128,256]{3,2,1,0:T(8,128)(2,1)S(1)}, bf16[1,2,128,256]{3,2,1,0:T(8,128)(2,1)}, u32[]{:S(2)}) copy-start(bf16[1,2,128,256]{3,2,1,0:T(8,128)(2,1)} %param.5) | copy-start | bytes 393220
  251.9 37.7 %collective-permute-start.30 = (f32[2,128,256]{2,1,0:T(8,128)S(1)}, f32[2,128,256]{2,1,0:T(8,128)}, u32[]{:S(2)}, u32[]{:S(2)}) collective-permute-start(f32[2,128,256]{2,1,0:T(8,128)S(1)} %bitcast.237), channel_id=1, source_target_pairs={{0,48},{16,0},{32,16},{48,32},{1,49},{17,1},{33,17},{49,33},{2,50}... | collective-permute-start | bytes 786440 | tf_op jit(solution)/shard_map/ppermute | solution.py:174
  257.8 31.9 %collective-permute-start.31 = (f32[2,128,256]{2,1,0:T(8,128)S(1)}, f32[2,128,256]{2,1,0:T(8,128)}, u32[]{:S(2)}, u32[]{:S(2)}) collective-permute-start(f32[2,128,256]{2,1,0:T(8,128)S(1)} %bitcast.238), channel_id=1, source_target_pairs={{0,32},{16,48},{32,0},{48,16},{1,33},{17,49},{33,1},{49,17},{2,34}... | collective-permute-start | bytes 786440 | tf_op jit(solution)/shard_map/ppermute | solution.py:174
  259.9 29.9 %collective-permute-start.32 = (f32[2,128,256]{2,1,0:T(8,128)S(1)}, f32[2,128,256]{2,1,0:T(8,128)}, u32[]{:S(2)}, u32[]{:S(2)}) collective-permute-start(f32[2,128,256]{2,1,0:T(8,128)S(1)} %bitcast.239), channel_id=1, source_target_pairs={{0,16},{16,32},{32,48},{48,0},{1,17},{17,33},{33,49},{49,1},{2,18}... | collective-permute-start | bytes 786440 | tf_op jit(solution)/shard_map/ppermute | solution.py:174
  274.7 6.4 %collective-permute-start.27 = (f32[2,32,256]{2,1,0:T(8,128)}, f32[2,32,256]{2,1,0:T(8,128)S(1)}, u32[]{:S(2)}, u32[]{:S(2)}) collective-permute-start(f32[2,32,256]{2,1,0:T(8,128)} %select_add_fusion), channel_id=1, source_target_pairs={{64,0},{65,1},{66,2},{67,3},{68,4},{69,5},{70,6},{71,7},{72,8},{73... | collective-permute-start | bytes 196616 | tf_op jit(solution)/shard_map/ppermute | solution.py:73
  275.9 8.0 %collective-permute-start.28 = (f32[2,32,256]{2,1,0:T(8,128)}, f32[2,32,256]{2,1,0:T(8,128)}, u32[]{:S(2)}, u32[]{:S(2)}) collective-permute-start(f32[2,32,256]{2,1,0:T(8,128)} %select_add_fusion), channel_id=1, source_target_pairs={{128,0},{129,1},{130,2},{131,3},{132,4},{133,5},{134,6},{135,7},{1... | collective-permute-start | bytes 196616 | tf_op jit(solution)/shard_map/ppermute | solution.py:73
  281.0 1.3 copy-start.17
  281.0 7.7 %collective-permute-start.29 = (f32[2,32,256]{2,1,0:T(8,128)}, f32[2,32,256]{2,1,0:T(8,128)}, u32[]{:S(2)}, u32[]{:S(2)}) collective-permute-start(f32[2,32,256]{2,1,0:T(8,128)} %select_add_fusion), channel_id=1, source_target_pairs={{192,0},{193,1},{194,2},{195,3},{196,4},{197,5},{198,6},{199,7},{2... | collective-permute-start | bytes 196616 | tf_op jit(solution)/shard_map/ppermute | solution.py:73
Sparse Core Ops, SparseCore 0:
  158.4 71.8 reduce-scatter.1

commit v3 on v2

--- a/solution.py
+++ b/solution.py
@@ -100,6 +100,11 @@
     return jnp.concatenate([pick(stacked, (j - y) % n_y) for j in range(n_y)], axis=2)
 
 
+def dp_gather(value, n_dp):
+    spread = jnp.broadcast_to(value[None], (n_dp,) + value.shape)
+    return lax.all_to_all(spread, "dp", 0, 0, tiled=False)
+
+
 def shards(inbound, weights, cotangent):
     n_seg = lax.axis_size("segment")
     n_dp = lax.axis_size("dp")
@@ -120,25 +125,24 @@
     ).astype(jnp.bfloat16)
     query = query.reshape(micro_count, row_count, feat_width)
     pair = jnp.stack([query, cotangent[0]])
-    slots = [pair] + [lax.ppermute(pair, "dp", shift_perm(n_dp, k)) for k in range(1, n_dp)]
-    slots = jnp.stack(slots)
-    dix = lax.axis_index("dp")
-    slots = jnp.stack([pick(slots, (dix - j) % n_dp) for j in range(n_dp)])
+    slots = dp_gather(pair, n_dp)
     query_heads = slots[:, 0].reshape(n_dp, micro_count, row_count, head_count, HD)
     grad_heads = slots[:, 1].reshape(n_dp, micro_count, row_count, head_count, HD)
 
     chunk_width = model_width // n_tensor
     chunk = lax.dynamic_slice_in_dim(states, tix * chunk_width, chunk_width, axis=2)
     chunk = seg_broadcast(chunk, n_seg)
-    encoded = tensor_gather(chunk, n_tensor)
-
-    pair_weights = layer[:, 1:, :].reshape(model_width, 2 * feat_width)
-    keyval = jnp.dot(
-        encoded.reshape(rows, model_width), pair_weights, preferred_element_type=jnp.float32
-    ).astype(jnp.bfloat16)
-    keyval = keyval.reshape(micro_count, row_count, 2, head_count, HD)
-    key_heads = keyval[:, :, 0]
-    value_heads = keyval[:, :, 1]
+    spread = jnp.broadcast_to(chunk[None], (n_tensor,) + chunk.shape)
+    encoded = lax.all_to_all(spread, "tensor", 0, 0, tiled=False)
+    encoded = jnp.moveaxis(encoded, 0, 2).reshape(micro_count, row_count, model_width)
+
+    flat_enc = encoded.reshape(rows, model_width)
+    key_heads = jnp.dot(flat_enc, layer[:, 1, :], preferred_element_type=jnp.float32).astype(
+        jnp.bfloat16
+    ).reshape(micro_count, row_count, head_count, HD)
+    value_heads = jnp.dot(flat_enc, layer[:, 2, :], preferred_element_type=jnp.float32).astype(
+        jnp.bfloat16
+    ).reshape(micro_count, row_count, head_count, HD)
 
     scores = (
         jnp.einsum("jmqhe,mkhe->mhjqk", query_heads, key_heads, preferred_element_type=jnp.float32)
@@ -152,9 +156,7 @@
     local_sum = jnp.sum(local_exp, axis=-1)
     local_delta = jnp.sum(local_exp * prob_grad, axis=-1)
     stats = jnp.stack([local_peak, local_sum, local_delta])
-    all_stats = jnp.stack(
-        [stats] + [lax.ppermute(stats, "dp", shift_perm(n_dp, k)) for k in range(1, n_dp)]
-    )
+    all_stats = dp_gather(stats, n_dp)
     peaks = all_stats[:, 0]
     peak = jnp.max(peaks, axis=0)
     weight = jnp.exp(peaks - peak[None])
@@ -168,10 +170,7 @@
     context_part = jnp.einsum(
         "mhjqk,mkhe->jmqhe", prob_rounded, value_heads, preferred_element_type=jnp.float32
     ).reshape(n_dp, micro_count, row_count, feat_width)
-    context = pick(context_part, dix)
-    for k in range(1, n_dp):
-        send = pick(context_part, (dix - k) % n_dp)
-        context = context + lax.ppermute(send, "dp", shift_perm(n_dp, -k))
+    context = jnp.sum(lax.all_to_all(context_part, "dp", 0, 0, tiled=False), axis=0)
     context = context.astype(jnp.bfloat16)
 
     key_grad = jnp.einsum(
@@ -180,15 +179,16 @@
     value_grad = jnp.einsum(
         "mhjqk,jmqhe->mkhe", prob_rounded, grad_heads, preferred_element_type=jnp.float32
     ).astype(jnp.bfloat16)
-    joined = jnp.stack(
-        [key_grad.reshape(rows, feat_width), value_grad.reshape(rows, feat_width)], axis=1
-    ).reshape(rows, 2 * feat_width)
-    head_terms = jnp.einsum(
-        "rc,dc->rd", joined, pair_weights, preferred_element_type=jnp.float32
-    ).astype(jnp.bfloat16)
-    head_terms = head_terms.reshape(micro_count, row_count, model_width)
-    heads_total = lax.psum_scatter(head_terms, "tensor", scatter_dimension=2, tiled=True).astype(
-        jnp.float32
+    head_terms = (
+        jnp.einsum("rc,dc->rd", key_grad.reshape(rows, feat_width), layer[:, 1, :],
+                   preferred_element_type=jnp.float32)
+        + jnp.einsum("rc,dc->rd", value_grad.reshape(rows, feat_width), layer[:, 2, :],
+                     preferred_element_type=jnp.float32)
+    ).astype(jnp.bfloat16)
+    head_terms = head_terms.reshape(micro_count, row_count, n_tensor, chunk_width)
+    head_terms = jnp.moveaxis(head_terms, 2, 0)
+    heads_total = jnp.sum(
+        lax.all_to_all(head_terms, "tensor", 0, 0, tiled=False).astype(jnp.float32), axis=0
     )
     heads_total = jnp.where(seg > 0, heads_total, jnp.zeros_like(heads_total))
     sections = seg_reduce(heads_total, n_seg)

time: 300 us -> 261 us (0.87)
  the two profiles are of different devices: /device:TPU:56 before, /device:TPU:64 now
where the time goes in v3:
time: 261 us; the launch traced here: 259 us
  waiting for transfers between devices  143 us (55%)
  starting transfers between devices  70.8 us (27%)
  local copies, waits for them, and re-layouts  18.4 us (7%)
  matrix products  11.6 us (4%)
  blocking collectives  9.79 us (4%)
  other arithmetic  5.57 us (2%)
    all_to_all x1, waiting for transfers between devices, shards(): encoded = lax.all_to_all(spread, 'tensor', 0, 0, tiled=False)  48.2 us
    all_to_all x1, waiting for transfers between devices, shards(): lax.all_to_all(head_terms, 'tensor', 0, 0, tiled=False).astype(jnp.float32)  47.9 us
    ppermute x3, waiting for transfers between devices, seg_reduce(): got = lax.ppermute(mine, 'segment', perm)  26.6 us
    all_to_all x1, starting transfers between devices, dp_gather(): return lax.all_to_all(spread, 'dp', 0, 0, tiled=False)  15.8 us
    ppermute x3, starting transfers between devices, seg_broadcast(): parts.append(lax.ppermute(mine, 'segment', perm))  12.7 us
    all_to_all x1, blocking collectives, dp_gather(): return lax.all_to_all(spread, 'dp', 0, 0, tiled=False)  9.79 us
    ppermute x3, starting transfers between devices, seg_reduce(): mine = mine + lax.ppermute(send, 'segment', perm)  9.23 us
    all_to_all x1, starting transfers between devices, shards(): encoded = lax.all_to_all(spread, 'tensor', 0, 0, tiled=False)  7.26 us
  transfers between devices with their start and end apart: 22, of which 13 were waited for; matrix products, arithmetic and copies ran while one was open for 3% of the time, Pallas kernels for 0%

profile of v3, /device:TPU:64, one launch (start us, length us, event | category | flops | bytes accessed | tf_op | source)
XLA Modules:
  0.0 259.4 jit_solution(16461134104120394361)
XLA Ops:
  0.0 1.6 copy-done
  1.6 2.3 fusion.8
  4.2 1.2 broadcast_in_dim.10
  5.4 15.8 %all-to-all-start = ((bf16[4,2,2,128,256]{3,4,2,1,0:T(8,128)(2,1)}), bf16[4,2,2,128,256]{3,4,2,1,0:T(8,128)(2,1)S(1)}, u32[]{:S(2)}, u32[]{:S(2)}) async-start(bf16[4,2,2,128,256]{3,4,2,1,0:T(8,128)(2,1)} %broadcast_in_dim.10), calls=%async_computation | async-start | bytes 2097152 | tf_op jit(solution)/shard_map/all_to_all | solution.py:105
  21.1 1.3 collective-permute-start
  22.4 1.3 collective-permute-start.1
  23.7 1.3 collective-permute-start.2
  25.3 1.3 collective-permute-done.2
  26.6 3.2 %collective-permute-start.3 = (bf16[2,32,256]{2,1,0:T(8,128)(2,1)S(1)}, bf16[2,32,256]{2,1,0:T(8,128)(2,1)S(1)}, u32[]{:S(2)}, u32[]{:S(2)}) collective-permute-start(bf16[2,32,256]{2,1,0:T(8,128)(2,1)S(1)} %fusion.39), channel_id=1, source_target_pairs={{0,768},{64,832},{128,896},{192,960},{1,769},{65,833},{129,897},{1... | collective-permute-start | bytes 98312 | tf_op jit(solution)/shard_map/ppermute | solution.py:40
  29.9 1.3 collective-permute-start.4
  31.2 0.3 collective-permute-done.3
  31.5 4.6 %collective-permute-done.4 = bf16[2,32,256]{2,1,0:T(8,128)(2,1)S(1)} collective-permute-done((bf16[2,32,256]{2,1,0:T(8,128)(2,1)S(1)}, bf16[2,32,256]{2,1,0:T(8,128)(2,1)S(1)}, u32[]{:S(2)}, u32[]{:S(2)}) %collective-permute-start.4) | collective-permute-done | bytes 32800 | tf_op jit(solution)/shard_map/ppermute | solution.py:40
  36.0 0.7 collective-permute-start.5
  36.7 4.7 %collective-permute-start.6 = (bf16[2,32,256]{2,1,0:T(8,128)(2,1)S(1)}, bf16[2,32,256]{2,1,0:T(8,128)(2,1)S(1)}, u32[]{:S(2)}, u32[]{:S(2)}) collective-permute-start(bf16[2,32,256]{2,1,0:T(8,128)(2,1)S(1)} %broadcast_select_fusion.1), channel_id=1, source_target_pairs={{0,64},{64,128},{128,192},{192,0},{256,320},{320,384},{384,448},{4... | collective-permute-start | bytes 98312 | tf_op jit(solution)/shard_map/ppermute | solution.py:46
  41.4 4.6 %collective-permute-start.7 = (bf16[2,32,256]{2,1,0:T(8,128)(2,1)S(1)}, bf16[2,32,256]{2,1,0:T(8,128)(2,1)S(1)}, u32[]{:S(2)}, u32[]{:S(2)}) collective-permute-start(bf16[2,32,256]{2,1,0:T(8,128)(2,1)S(1)} %broadcast_select_fusion.1), channel_id=1, source_target_pairs={{0,128},{64,192},{128,0},{192,64},{256,384},{320,448},{384,256},{4... | collective-permute-start | bytes 98312 | tf_op jit(solution)/shard_map/ppermute | solution.py:46
  46.1 3.3 %collective-permute-start.8 = (bf16[2,32,256]{2,1,0:T(8,128)(2,1)S(1)}, bf16[2,32,256]{2,1,0:T(8,128)(2,1)S(1)}, u32[]{:S(2)}, u32[]{:S(2)}) collective-permute-start(bf16[2,32,256]{2,1,0:T(8,128)(2,1)S(1)} %broadcast_select_fusion.1), channel_id=1, source_target_pairs={{0,192},{64,0},{128,64},{192,128},{256,448},{320,256},{384,320},{4... | collective-permute-start | bytes 98312 | tf_op jit(solution)/shard_map/ppermute | solution.py:46
  49.5 2.3 collective-permute-done.8
  52.0 1.5 broadcast_in_dim.12
  53.5 7.3 %all-to-all-start.1 = ((bf16[16,2,128,256]{3,2,1,0:T(8,128)(2,1)}), bf16[16,2,128,256]{3,2,1,0:T(8,128)(2,1)}, u32[]{:S(2)}, u32[]{:S(2)}) async-start(bf16[16,2,128,256]{3,2,1,0:T(8,128)(2,1)} %broadcast_in_dim.12), calls=%async_computation.1 | async-start | bytes 4194304 | tf_op jit(solution)/shard_map/all_to_all | solution.py:136
  60.8 1.1 fusion.40
  61.8 48.2 %all-to-all-done.1 = bf16[16,2,128,256]{3,2,1,0:T(8,128)(2,1)} async-done(((bf16[16,2,128,256]{3,2,1,0:T(8,128)(2,1)}), bf16[16,2,128,256]{3,2,1,0:T(8,128)(2,1)}, u32[]{:S(2)}, u32[]{:S(2)}) %all-to-all-start.1) | async-done | bytes 2097184 | tf_op jit(solution)/shard_map/all_to_all | solution.py:136
  110.1 2.8 %copy.117 = bf16[2,128,16,256]{3,2,1,0:T(8,128)(2,1)S(1)} copy(bf16[2,128,16,256]{3,1,0,2:T(8,128)(2,1)} %bitcast.19) | data formatting | bytes 4194304 | tf_op jit(solution)/shard_map/transpose | solution.py:137
  112.8 0.9 copy.166
  113.8 2.3 fusion.7
  116.1 3.1 %fusion.6 = bf16[256,256]{1,0:T(8,128)(2,1)} fusion(bf16[256,4096]{1,0:T(8,128)(2,1)S(1)} %bitcast.173, bf16[4096,3,256]{2,0,1:T(8,128)(2,1)} %bitcast.167), kind=kOutput, calls=%fused_computation.18 | convolution fusion | flops 536936448 | bytes 4325376 | tf_op jit(solution)/shard_map/dot_general | solution.py:143
  119.3 1.7 copy.122
  121.0 0.9 reshape.66
  122.0 0.4 multiply_reduce_fusion.1
  122.4 0.7 fusion.2
  123.2 9.8 %all_to_all.25 = f32[4,3,2,4,4,128]{5,4,3,2,1,0:T(4,128)S(1)} all-to-all(f32[4,3,2,4,4,128]{5,4,3,2,1,0:T(4,128)S(1)} %broadcast_in_dim.13), channel_id=1, replica_groups=mesh['segment'=16,'dp'=4,'tensor'=16] {'dp'}, dimensions={0} | all-to-all | bytes 393216 | tf_op jit(solution)/shard_map/all_to_all | solution.py:105
  133.1 0.8 fusion.19
  134.1 0.5 fusion.11
  134.8 0.8 fusion.3
  135.6 0.3 copy-done.2
  135.9 0.5 fusion.9
  136.5 0.8 fusion
  137.3 0.6 copy.169
  137.9 2.0 copy.211
  139.9 4.6 %all-to-all-start.3 = ((bf16[16,2,128,256]{3,2,1,0:T(8,128)(2,1)}), bf16[16,2,128,256]{3,2,1,0:T(8,128)(2,1)}, u32[]{:S(2)}, u32[]{:S(2)}) async-start(bf16[16,2,128,256]{3,2,1,0:T(8,128)(2,1)} %bitcast.161), calls=%async_computation.3 | async-start | bytes 4194304 | tf_op jit(solution)/shard_map/all_to_all | solution.py:191
  144.5 0.3 convolution_bitcast_fusion
  144.8 1.1 copy.137
  145.9 47.9 %all-to-all-done.3 = bf16[16,2,128,256]{3,2,1,0:T(8,128)(2,1)} async-done(((bf16[16,2,128,256]{3,2,1,0:T(8,128)(2,1)}), bf16[16,2,128,256]{3,2,1,0:T(8,128)(2,1)}, u32[]{:S(2)}, u32[]{:S(2)}) %all-to-all-start.3) | async-done | bytes 2097184 | tf_op jit(solution)/shard_map/all_to_all | solution.py:191
  193.8 5.1 %all-to-all-start.4 = ((f32[4,2,128,256]{2,3,1,0:T(8,128)}), f32[4,2,128,256]{2,3,1,0:T(8,128)S(1)}, u32[]{:S(2)}, u32[]{:S(2)}) async-start(f32[4,2,128,256]{2,3,1,0:T(8,128)} %bitcast.48), calls=%async_computation.4 | async-start | bytes 2097152 | tf_op jit(solution)/shard_map/all_to_all | solution.py:173
  198.9 1.9 convert_reduce_fusion
  200.9 0.7 dynamic-slice_bitcast_fusion.2
  201.6 2.8 %collective-permute-start.10 = (f32[2,32,256]{2,1,0:T(8,128)}, f32[2,32,256]{2,1,0:T(8,128)}, u32[]{:S(2)}, u32[]{:S(2)}) collective-permute-start(f32[2,32,256]{2,1,0:T(8,128)} %get-tuple-element.15), channel_id=1, source_target_pairs={{0,128},{64,192},{128,0},{192,64},{256,384},{320,448},{384,256},{4... | collective-permute-start | bytes 196616 | tf_op jit(solution)/shard_map/ppermute | solution.py:63
  204.4 3.7 %collective-permute-start.11 = (f32[2,32,256]{2,1,0:T(8,128)}, f32[2,32,256]{2,1,0:T(8,128)}, u32[]{:S(2)}, u32[]{:S(2)}) collective-permute-start(f32[2,32,256]{2,1,0:T(8,128)} %get-tuple-element.14), channel_id=1, source_target_pairs={{0,192},{64,0},{128,64},{192,128},{256,448},{320,256},{384,320},{4... | collective-permute-start | bytes 196616 | tf_op jit(solution)/shard_map/ppermute | solution.py:63
  208.1 2.8 %collective-permute-start.9 = (f32[2,32,256]{2,1,0:T(8,128)}, f32[2,32,256]{2,1,0:T(8,128)}, u32[]{:S(2)}, u32[]{:S(2)}) collective-permute-start(f32[2,32,256]{2,1,0:T(8,128)} %get-tuple-element.13), channel_id=1, source_target_pairs={{0,64},{64,128},{128,192},{192,0},{256,320},{320,384},{384,448},{4... | collective-permute-start | bytes 196616 | tf_op jit(solution)/shard_map/ppermute | solution.py:63
  210.9 0.6 collective-permute-done.11
  211.5 4.3 %collective-permute-done.9 = f32[2,32,256]{2,1,0:T(8,128)} collective-permute-done((f32[2,32,256]{2,1,0:T(8,128)}, f32[2,32,256]{2,1,0:T(8,128)}, u32[]{:S(2)}, u32[]{:S(2)}) %collective-permute-start.9) | collective-permute-done | bytes 65568 | tf_op jit(solution)/shard_map/ppermute | solution.py:63
  215.8 0.9 fusion.36
  216.7 0.7 collective-permute-start.12
  217.4 1.3 collective-permute-start.13
  218.7 1.3 collective-permute-start.14
  220.0 26.6 %collective-permute-done.13 = f32[2,32,256]{2,1,0:T(8,128)S(1)} collective-permute-done((f32[2,32,256]{2,1,0:T(8,128)S(1)}, f32[2,32,256]{2,1,0:T(8,128)S(1)}, u32[]{:S(2)}, u32[]{:S(2)}) %collective-permute-start.13) | collective-permute-done | bytes 65568 | tf_op jit(solution)/shard_map/ppermute | solution.py:68
  246.6 0.6 select_add_fusion
  247.2 1.3 collective-permute-start.15
  248.5 1.3 collective-permute-start.16
  249.8 1.3 collective-permute-start.17
  251.3 2.4 collective-permute-done.15
  253.7 2.8 %collective-permute-done.16 = f32[2,32,256]{2,1,0:T(8,128)} collective-permute-done((f32[2,32,256]{2,1,0:T(8,128)}, f32[2,32,256]{2,1,0:T(8,128)}, u32[]{:S(2)}, u32[]{:S(2)}) %collective-permute-start.16) | collective-permute-done | bytes 65568 | tf_op jit(solution)/shard_map/ppermute | solution.py:73
  256.5 1.0 collective-permute-done.17
  257.5 1.0 pad_maximum_fusion.1
  258.7 0.8 copy.138
  (54 shorter events, 1.9 us)
Async XLA Ops:
  0.0 1.6 copy-start
  1.6 2.3 copy-start.5
  5.4 46.6 %all-to-all-start = ((bf16[4,2,2,128,256]{3,4,2,1,0:T(8,128)(2,1)}), bf16[4,2,2,128,256]{3,4,2,1,0:T(8,128)(2,1)S(1)}, u32[]{:S(2)}, u32[]{:S(2)}) async-start(bf16[4,2,2,128,256]{3,4,2,1,0:T(8,128)(2,1)} %broadcast_in_dim.10), calls=%async_computation | async-start | bytes 2097152 | tf_op jit(solution)/shard_map/all_to_all | solution.py:105
  21.1 3.9 %collective-permute-start = (bf16[2,32,256]{2,1,0:T(8,128)(2,1)S(1)}, bf16[2,32,256]{2,1,0:T(8,128)(2,1)S(1)}, u32[]{:S(2)}, u32[]{:S(2)}) collective-permute-start(bf16[2,32,256]{2,1,0:T(8,128)(2,1)S(1)} %get-tuple-element.22), channel_id=1, source_target_pairs={{0,192},{1,193},{2,194},{3,195},{4,196},{5,197},{6,198},{7,199},{8... | collective-permute-start | bytes 98312 | tf_op jit(solution)/shard_map/ppermute | solution.py:34
  22.4 2.9 %collective-permute-start.1 = (bf16[2,32,256]{2,1,0:T(8,128)(2,1)S(1)}, bf16[2,32,256]{2,1,0:T(8,128)(2,1)S(1)}, u32[]{:S(2)}, u32[]{:S(2)}) collective-permute-start(bf16[2,32,256]{2,1,0:T(8,128)(2,1)S(1)} %get-tuple-element.21), channel_id=1, source_target_pairs={{0,128},{1,129},{2,130},{3,131},{4,132},{5,133},{6,134},{7,135},{8... | collective-permute-start | bytes 98312 | tf_op jit(solution)/shard_map/ppermute | solution.py:34
  23.7 2.9 %collective-permute-start.2 = (bf16[2,32,256]{2,1,0:T(8,128)(2,1)S(1)}, bf16[2,32,256]{2,1,0:T(8,128)(2,1)S(1)}, u32[]{:S(2)}, u32[]{:S(2)}) collective-permute-start(bf16[2,32,256]{2,1,0:T(8,128)(2,1)S(1)} %get-tuple-element.20), channel_id=1, source_target_pairs={{0,64},{1,65},{2,66},{3,67},{4,68},{5,69},{6,70},{7,71},{8,72},{9,... | collective-permute-start | bytes 98312 | tf_op jit(solution)/shard_map/ppermute | solution.py:34
  26.6 4.8 %collective-permute-start.3 = (bf16[2,32,256]{2,1,0:T(8,128)(2,1)S(1)}, bf16[2,32,256]{2,1,0:T(8,128)(2,1)S(1)}, u32[]{:S(2)}, u32[]{:S(2)}) collective-permute-start(bf16[2,32,256]{2,1,0:T(8,128)(2,1)S(1)} %fusion.39), channel_id=1, source_target_pairs={{0,768},{64,832},{128,896},{192,960},{1,769},{65,833},{129,897},{1... | collective-permute-start | bytes 98312 | tf_op jit(solution)/shard_map/ppermute | solution.py:40
  29.9 6.1 %collective-permute-start.4 = (bf16[2,32,256]{2,1,0:T(8,128)(2,1)S(1)}, bf16[2,32,256]{2,1,0:T(8,128)(2,1)S(1)}, u32[]{:S(2)}, u32[]{:S(2)}) collective-permute-start(bf16[2,32,256]{2,1,0:T(8,128)(2,1)S(1)} %fusion.39), channel_id=1, source_target_pairs={{0,256},{64,320},{128,384},{192,448},{1,257},{65,321},{129,385},{1... | collective-permute-start | bytes 98312 | tf_op jit(solution)/shard_map/ppermute | solution.py:40
  36.0 0.7 collective-permute-start.5
  36.7 12.8 %collective-permute-start.6 = (bf16[2,32,256]{2,1,0:T(8,128)(2,1)S(1)}, bf16[2,32,256]{2,1,0:T(8,128)(2,1)S(1)}, u32[]{:S(2)}, u32[]{:S(2)}) collective-permute-start(bf16[2,32,256]{2,1,0:T(8,128)(2,1)S(1)} %broadcast_select_fusion.1), channel_id=1, source_target_pairs={{0,64},{64,128},{128,192},{192,0},{256,320},{320,384},{384,448},{4... | collective-permute-start | bytes 98312 | tf_op jit(solution)/shard_map/ppermute | solution.py:46
  41.4 8.1 %collective-permute-start.7 = (bf16[2,32,256]{2,1,0:T(8,128)(2,1)S(1)}, bf16[2,32,256]{2,1,0:T(8,128)(2,1)S(1)}, u32[]{:S(2)}, u32[]{:S(2)}) collective-permute-start(bf16[2,32,256]{2,1,0:T(8,128)(2,1)S(1)} %broadcast_select_fusion.1), channel_id=1, source_target_pairs={{0,128},{64,192},{128,0},{192,64},{256,384},{320,448},{384,256},{4... | collective-permute-start | bytes 98312 | tf_op jit(solution)/shard_map/ppermute | solution.py:46
  46.1 5.8 %collective-permute-start.8 = (bf16[2,32,256]{2,1,0:T(8,128)(2,1)S(1)}, bf16[2,32,256]{2,1,0:T(8,128)(2,1)S(1)}, u32[]{:S(2)}, u32[]{:S(2)}) collective-permute-start(bf16[2,32,256]{2,1,0:T(8,128)(2,1)S(1)} %broadcast_select_fusion.1), channel_id=1, source_target_pairs={{0,192},{64,0},{128,64},{192,128},{256,448},{320,256},{384,320},{4... | collective-permute-start | bytes 98312 | tf_op jit(solution)/shard_map/ppermute | solution.py:46
  53.5 56.6 %all-to-all-start.1 = ((bf16[16,2,128,256]{3,2,1,0:T(8,128)(2,1)}), bf16[16,2,128,256]{3,2,1,0:T(8,128)(2,1)}, u32[]{:S(2)}, u32[]{:S(2)}) async-start(bf16[16,2,128,256]{3,2,1,0:T(8,128)(2,1)} %broadcast_in_dim.12), calls=%async_computation.1 | async-start | bytes 4194304 | tf_op jit(solution)/shard_map/all_to_all | solution.py:136
  116.1 5.8 %copy-start.3 = (bf16[4,1,2,128,256]{3,4,2,1,0:T(8,128)(2,1)S(1)}, bf16[4,1,2,128,256]{3,4,2,1,0:T(8,128)(2,1)}, u32[]{:S(2)}) copy-start(bf16[4,1,2,128,256]{3,4,2,1,0:T(8,128)(2,1)} %get-tuple-element.11) | copy-start | bytes 1572868
  119.2 3.2 %copy-start.1 = (bf16[4,1,2,128,256]{3,4,2,1,0:T(8,128)(2,1)S(1)}, bf16[4,1,2,128,256]{3,4,2,1,0:T(8,128)(2,1)}, u32[]{:S(2)}) copy-start(bf16[4,1,2,128,256]{3,4,2,1,0:T(8,128)(2,1)} %get-tuple-element.12) | copy-start | bytes 1572868
  122.4 12.4 %slice-start = ((s8[6291456]{0:T(1024)(128)(4,1)}), s8[4194304]{0:T(1024)(128)(4,1)S(1)}, s32[]{:S(2)}) async-start(s8[6291456]{0:T(1024)(128)(4,1)} %bitcast.168), calls=%async_computation.5 | async-start | bytes 8388608
  133.1 1.0 copy-start.4
  133.1 1.7 slice-start.1
  134.8 1.0 copy-start.2
  139.9 53.9 %all-to-all-start.3 = ((bf16[16,2,128,256]{3,2,1,0:T(8,128)(2,1)}), bf16[16,2,128,256]{3,2,1,0:T(8,128)(2,1)}, u32[]{:S(2)}, u32[]{:S(2)}) async-start(bf16[16,2,128,256]{3,2,1,0:T(8,128)(2,1)} %bitcast.161), calls=%async_computation.3 | async-start | bytes 4194304 | tf_op jit(solution)/shard_map/all_to_all | solution.py:191
  193.8 57.4 %all-to-all-start.4 = ((f32[4,2,128,256]{2,3,1,0:T(8,128)}), f32[4,2,128,256]{2,3,1,0:T(8,128)S(1)}, u32[]{:S(2)}, u32[]{:S(2)}) async-start(f32[4,2,128,256]{2,3,1,0:T(8,128)} %bitcast.48), calls=%async_computation.4 | async-start | bytes 2097152 | tf_op jit(solution)/shard_map/all_to_all | solution.py:173
  198.9 52.2 %copy-start.6 = (bf16[1,2,128,256]{3,2,1,0:T(8,128)(2,1)S(1)}, bf16[1,2,128,256]{3,2,1,0:T(8,128)(2,1)}, u32[]{:S(2)}) copy-start(bf16[1,2,128,256]{3,2,1,0:T(8,128)(2,1)} %param.5) | copy-start | bytes 393220
  201.6 9.3 %collective-permute-start.10 = (f32[2,32,256]{2,1,0:T(8,128)}, f32[2,32,256]{2,1,0:T(8,128)}, u32[]{:S(2)}, u32[]{:S(2)}) collective-permute-start(f32[2,32,256]{2,1,0:T(8,128)} %get-tuple-element.15), channel_id=1, source_target_pairs={{0,128},{64,192},{128,0},{192,64},{256,384},{320,448},{384,256},{4... | collective-permute-start | bytes 196616 | tf_op jit(solution)/shard_map/ppermute | solution.py:63
  204.4 7.1 %collective-permute-start.11 = (f32[2,32,256]{2,1,0:T(8,128)}, f32[2,32,256]{2,1,0:T(8,128)}, u32[]{:S(2)}, u32[]{:S(2)}) collective-permute-start(f32[2,32,256]{2,1,0:T(8,128)} %get-tuple-element.14), channel_id=1, source_target_pairs={{0,192},{64,0},{128,64},{192,128},{256,448},{320,256},{384,320},{4... | collective-permute-start | bytes 196616 | tf_op jit(solution)/shard_map/ppermute | solution.py:63
  208.1 7.7 %collective-permute-start.9 = (f32[2,32,256]{2,1,0:T(8,128)}, f32[2,32,256]{2,1,0:T(8,128)}, u32[]{:S(2)}, u32[]{:S(2)}) collective-permute-start(f32[2,32,256]{2,1,0:T(8,128)} %get-tuple-element.13), channel_id=1, source_target_pairs={{0,64},{64,128},{128,192},{192,0},{256,320},{320,384},{384,448},{4... | collective-permute-start | bytes 196616 | tf_op jit(solution)/shard_map/ppermute | solution.py:63
  216.7 0.7 collective-permute-start.12
  217.4 29.2 %collective-permute-start.13 = (f32[2,32,256]{2,1,0:T(8,128)S(1)}, f32[2,32,256]{2,1,0:T(8,128)S(1)}, u32[]{:S(2)}, u32[]{:S(2)}) collective-permute-start(f32[2,32,256]{2,1,0:T(8,128)S(1)} %select_add_fusion.1), channel_id=1, source_target_pairs={{256,0},{320,64},{384,128},{448,192},{257,1},{321,65},{385,129},{4... | collective-permute-start | bytes 196616 | tf_op jit(solution)/shard_map/ppermute | solution.py:68
  218.7 27.9 %collective-permute-start.14 = (f32[2,32,256]{2,1,0:T(8,128)S(1)}, f32[2,32,256]{2,1,0:T(8,128)S(1)}, u32[]{:S(2)}, u32[]{:S(2)}) collective-permute-start(f32[2,32,256]{2,1,0:T(8,128)S(1)} %select_add_fusion.1), channel_id=1, source_target_pairs={{768,0},{832,64},{896,128},{960,192},{769,1},{833,65},{897,129},{9... | collective-permute-start | bytes 196616 | tf_op jit(solution)/shard_map/ppermute | solution.py:68
  247.2 6.5 %collective-permute-start.15 = (f32[2,32,256]{2,1,0:T(8,128)}, f32[2,32,256]{2,1,0:T(8,128)}, u32[]{:S(2)}, u32[]{:S(2)}) collective-permute-start(f32[2,32,256]{2,1,0:T(8,128)} %select_add_fusion), channel_id=1, source_target_pairs={{64,0},{65,1},{66,2},{67,3},{68,4},{69,5},{70,6},{71,7},{72,8},{73... | collective-permute-start | bytes 196616 | tf_op jit(solution)/shard_map/ppermute | solution.py:73
  248.5 8.0 %collective-permute-start.16 = (f32[2,32,256]{2,1,0:T(8,128)}, f32[2,32,256]{2,1,0:T(8,128)}, u32[]{:S(2)}, u32[]{:S(2)}) collective-permute-start(f32[2,32,256]{2,1,0:T(8,128)} %select_add_fusion), channel_id=1, source_target_pairs={{128,0},{129,1},{130,2},{131,3},{132,4},{133,5},{134,6},{135,7},{1... | collective-permute-start | bytes 196616 | tf_op jit(solution)/shard_map/ppermute | solution.py:73
  249.8 7.7 %collective-permute-start.17 = (f32[2,32,256]{2,1,0:T(8,128)}, f32[2,32,256]{2,1,0:T(8,128)}, u32[]{:S(2)}, u32[]{:S(2)}) collective-permute-start(f32[2,32,256]{2,1,0:T(8,128)} %select_add_fusion), channel_id=1, source_target_pairs={{192,0},{193,1},{194,2},{195,3},{196,4},{197,5},{198,6},{199,7},{2... | collective-permute-start | bytes 196616 | tf_op jit(solution)/shard_map/ppermute | solution.py:73

commit v4 on v3

v4 whole, which is shorter than its diff:
```python
import jax
import jax.numpy as jnp
from jax import lax
from jax.sharding import Mesh, PartitionSpec as P

HD = 64
X_SIZE = 4
SEG = ("zh", "x")
TEN = ("ty", "tc")


def hi_rounds(n_hi):
    rounds = [[(0, 1)] + ([(0, n_hi - 1)] if n_hi > 2 else [])]
    if n_hi > 3:
        rounds.append([(1, 2)])
    return rounds


def gather_axis(value, axis, n):
    spread = jnp.broadcast_to(value[None], (n,) + value.shape)
    return lax.all_to_all(spread, axis, 0, 0, tiled=False)


def seg_broadcast(value, n_hi, n_x):
    x = lax.axis_index("x")
    zh = lax.axis_index("zh")
    quarter = value.shape[1] // n_x
    pieces = value.reshape(value.shape[0], n_x, quarter, value.shape[2])
    mine = pieces[:, 0]
    for k in range(1, n_x):
        got = lax.ppermute(pieces[:, k], "x", [(0, k)])
        mine = jnp.where(x == k, got, mine)
    for pairs in hi_rounds(n_hi):
        nxt = mine
        for a, b in pairs:
            got = lax.ppermute(mine, "zh", [(a, b)])
            nxt = jnp.where(zh == b, got, nxt)
        mine = nxt
    full = gather_axis(mine, "x", n_x)
    return jnp.moveaxis(full, 0, 1).reshape(value.shape)


def seg_reduce(value, n_hi, n_x):
    zh = lax.axis_index("zh")
    quarter = value.shape[1] // n_x
    pieces = jnp.moveaxis(value.reshape(value.shape[0], n_x, quarter, value.shape[2]), 1, 0)
    mine = jnp.sum(lax.all_to_all(pieces, "x", 0, 0, tiled=False), axis=0)
    for pairs in reversed(hi_rounds(n_hi)):
        acc = mine
        for a, b in pairs:
            got = lax.ppermute(mine, "zh", [(b, a)])
            acc = acc + jnp.where(zh == a, got, jnp.zeros_like(got))
        mine = acc
    parts = [mine]
    for k in range(1, n_x):
        parts.append(lax.ppermute(mine, "x", [(k, 0)]))
    return jnp.stack(parts, axis=1).reshape(value.shape)


def shards(inbound, weights, cotangent):
    n_hi = lax.axis_size("zh")
    n_x = lax.axis_size("x")
    n_dp = lax.axis_size("dp")
    n_y = lax.axis_size("ty")
    n_c = lax.axis_size("tc")
    n_tensor = n_y * n_c
    seg = lax.axis_index("zh") * n_x + lax.axis_index("x")
    core = lax.axis_index("tc")
    tix = lax.axis_index("ty") * n_c + core

    states = inbound[0]
    micro_count, row_count, model_width = states.shape
    layer = weights[0]
    feat_width = layer.shape[2]
    head_count = feat_width // HD
    scale = HD ** (-0.5)
    rows = micro_count * row_count
    chunk_width = model_width // n_tensor

    query = jnp.dot(
        states.reshape(rows, model_width), layer[:, 0, :], preferred_element_type=jnp.float32
    ).astype(jnp.bfloat16)
    query = query.reshape(micro_count, row_count, feat_width)
    slots = gather_axis(jnp.stack([query, cotangent[0]]), "dp", n_dp)
    query_heads = slots[:, 0].reshape(n_dp, micro_count, row_count, head_count, HD)
    grad_heads = slots[:, 1].reshape(n_dp, micro_count, row_count, head_count, HD)

    chunk = lax.dynamic_slice_in_dim(states, tix * chunk_width, chunk_width, axis=2)
    chunk = seg_broadcast(chunk, n_hi, n_x)
    own = gather_axis(chunk, "ty", n_y)
    both = gather_axis(own, "tc", n_c)
    encoded = jnp.transpose(both, (2, 3, 1, 0, 4)).reshape(micro_count, row_count, model_width)

    flat_enc = encoded.reshape(rows, model_width)
    key_heads = jnp.dot(flat_enc, layer[:, 1, :], preferred_element_type=jnp.float32).astype(
        jnp.bfloat16
    ).reshape(micro_count, row_count, head_count, HD)
    value_heads = jnp.dot(flat_enc, layer[:, 2, :], preferred_element_type=jnp.float32).astype(
        jnp.bfloat16
    ).reshape(micro_count, row_count, head_count, HD)

    scores = (
        jnp.einsum("jmqhe,mkhe->mhjqk", query_heads, key_heads, preferred_element_type=jnp.float32)
        * scale
    )
    prob_grad = jnp.einsum(
        "jmqhe,mkhe->mhjqk", grad_heads, value_heads, preferred_element_type=jnp.float32
    )
    local_peak = jnp.max(scores, axis=-1)
    local_exp = jnp.exp(scores - local_peak[..., None])
    local_sum = jnp.sum(local_exp, axis=-1)
    local_delta = jnp.sum(local_exp * prob_grad, axis=-1)
    stats = jnp.stack([local_peak, local_sum, local_delta])
    all_stats = gather_axis(stats, "dp", n_dp)
    peaks = all_stats[:, 0]
    peak = jnp.max(peaks, axis=0)
    weight = jnp.exp(peaks - peak[None])
    total = jnp.sum(all_stats[:, 1] * weight, axis=0)
    row_delta = jnp.sum(all_stats[:, 2] * weight, axis=0) / total

    attend_prob = jnp.exp(scores - peak[..., None]) / total[..., None]
    prob_rounded = attend_prob.astype(jnp.bfloat16)
    score_grad = (attend_prob * (prob_grad - row_delta[..., None]) * scale).astype(jnp.bfloat16)

    context_part = jnp.einsum(
        "mhjqk,mkhe->jmqhe", prob_rounded, value_heads, preferred_element_type=jnp.float32
    ).reshape(n_dp, micro_count, row_count, feat_width)
    context = jnp.sum(lax.all_to_all(context_part, "dp", 0, 0, tiled=False), axis=0)
    context = context.astype(jnp.bfloat16)

    key_grad = jnp.einsum(
        "mhjqk,jmqhe->mkhe", score_grad, query_heads, preferred_element_type=jnp.float32
    ).astype(jnp.bfloat16)
    value_grad = jnp.einsum(
        "mhjqk,jmqhe->mkhe", prob_rounded, grad_heads, preferred_element_type=jnp.float32
    ).astype(jnp.bfloat16)
    head_terms = (
        jnp.einsum("rc,dc->rd", key_grad.reshape(rows, feat_width), layer[:, 1, :],
                   preferred_element_type=jnp.float32)
        + jnp.einsum("rc,dc->rd", value_grad.reshape(rows, feat_width), layer[:, 2, :],
                     preferred_element_type=jnp.float32)
    ).astype(jnp.bfloat16)
    head_terms = head_terms.reshape(micro_count, row_count, n_y, n_c, chunk_width)
    head_terms = jnp.transpose(head_terms, (3, 2, 0, 1, 4))
    pair_sum = jnp.sum(
        lax.all_to_all(head_terms, "tc", 0, 0, tiled=False).astype(jnp.float32), axis=0
    ).astype(jnp.bfloat16)
    heads_total = jnp.sum(
        lax.all_to_all(pair_sum, "ty", 0, 0, tiled=False).astype(jnp.float32), axis=0
    )
    heads_total = jnp.where(seg > 0, heads_total, jnp.zeros_like(heads_total))
    sections = seg_reduce(heads_total, n_hi, n_x)
    encoder_grad = (sections + cotangent[0].astype(jnp.float32)).astype(jnp.bfloat16)
    result = jnp.where(seg == 0, encoder_grad, context)
    return result[None]


def solution(mesh):
    n_seg, n_dp, n_tensor = (mesh.shape[a] for a in ("segment", "dp", "tensor"))
    sub = Mesh(
        mesh.devices.reshape(n_seg // X_SIZE, X_SIZE, n_dp, n_tensor // 2, 2),
        SEG + ("dp",) + TEN,
    )
    placed = (
        P(SEG, None, "dp", None),
        P(SEG, None, None, TEN),
        P(SEG, None, "dp", TEN),
    )
    return jax.shard_map(
        shards,
        mesh=sub,
        in_specs=placed,
        out_specs=P(SEG, None, "dp", TEN),
        check_vma=False,
    )
```

time: 261 us -> 252 us (0.966)
  the two profiles are of different devices: /device:TPU:64 before, /device:TPU:128 now
where the time goes in v4:
time: 252 us; the launch traced here: 251 us
  waiting for transfers between devices  108 us (43%)
  starting transfers between devices  58 us (23%)
  blocking collectives  32.9 us (13%)
  local copies, waits for them, and re-layouts  31.3 us (12%)
  matrix products  13.5 us (5%)
  other arithmetic  6.7 us (3%)
    ppermute x3, waiting for transfers between devices, seg_reduce(): got = lax.ppermute(mine, 'zh', [(b, a)])  39 us
    all_to_all x1, waiting for transfers between devices, shards(): lax.all_to_all(pair_sum, 'ty', 0, 0, tiled=False).astype(jnp.float32)  29.3 us
    all_to_all x3, blocking collectives, gather_axis(): return lax.all_to_all(spread, axis, 0, 0, tiled=False)  26.6 us
    all_to_all x2, waiting for transfers between devices, gather_axis(): return lax.all_to_all(spread, axis, 0, 0, tiled=False)  25.3 us
    ppermute x3, starting transfers between devices, seg_broadcast(): got = lax.ppermute(mine, 'zh', [(a, b)])  18.3 us
    all_to_all x2, starting transfers between devices, gather_axis(): return lax.all_to_all(spread, axis, 0, 0, tiled=False)  12.5 us
    ppermute x3, starting transfers between devices, seg_broadcast(): got = lax.ppermute(pieces[:, k], 'x', [(0, k)])  7.25 us
    reshape x2, local copies, waits for them, and re-layouts, shards(): head_terms.reshape(micro_count, row_count, n_y, n_c, chunk_width)  6.33 us
  transfers between devices with their start and end apart: 17, of which 12 were waited for; matrix products, arithmetic and copies ran while one was open for 11% of the time, Pallas kernels for 0%

profile of v4, /device:TPU:128, one launch (start us, length us, event | category | flops | bytes accessed | tf_op | source)
XLA Modules:
  0.0 251.2 jit_solution(9544859990011985804)
XLA Ops:
  0.0 1.6 copy-done
  1.6 4.7 %collective-permute-start = (bf16[2,32,256]{2,1,0:T(8,128)(2,1)S(1)}, bf16[2,32,256]{2,1,0:T(8,128)(2,1)S(1)}, u32[]{:S(2)}, u32[]{:S(2)}) collective-permute-start(bf16[2,32,256]{2,1,0:T(8,128)(2,1)S(1)} %get-tuple-element.15), channel_id=1, source_target_pairs={{0,192},{1,193},{2,194},{3,195},{4,196},{5,197},{6,198},{7,199},{8... | collective-permute-start | bytes 98312 | tf_op jit(solution)/shard_map/ppermute | solution.py:31
  6.3 1.3 collective-permute-start.1
  7.6 1.3 collective-permute-start.2
  9.2 1.3 collective-permute-done.2
  10.5 16.4 %collective-permute-start.3 = (bf16[2,32,256]{2,1,0:T(8,128)(2,1)S(1)}, bf16[2,32,256]{2,1,0:T(8,128)(2,1)S(1)}, u32[]{:S(2)}, u32[]{:S(2)}) collective-permute-start(bf16[2,32,256]{2,1,0:T(8,128)(2,1)S(1)} %fusion.37), channel_id=1, source_target_pairs={{0,768},{1,769},{2,770},{3,771},{4,772},{5,773},{6,774},{7,775},{8... | collective-permute-start | bytes 98312 | tf_op jit(solution)/shard_map/ppermute | solution.py:36
  26.9 1.3 collective-permute-start.4
  28.5 1.8 collective-permute-done.4
  30.3 0.7 collective-permute-start.5
  31.1 9.8 %all_to_all.45 = bf16[4,2,32,256]{3,2,1,0:T(8,128)(2,1)S(1)} all-to-all(bf16[4,2,32,256]{3,2,1,0:T(8,128)(2,1)S(1)} %broadcast_in_dim.15), channel_id=1, replica_groups=mesh['zh'=4,'x'=4,'dp'=4,'ty'=8,'tc'=2] {'x'}, dimensions={0} | all-to-all | bytes 262144 | tf_op jit(solution)/shard_map/all_to_all | solution.py:21
  40.8 1.1 broadcast_in_dim.17
  41.9 7.1 %all-to-all-start.2 = ((bf16[8,2,128,256]{3,2,1,0:T(8,128)(2,1)}), bf16[8,2,128,256]{3,2,1,0:T(8,128)(2,1)S(1)}, u32[]{:S(2)}, u32[]{:S(2)}) async-start(bf16[8,2,128,256]{3,2,1,0:T(8,128)(2,1)} %broadcast_in_dim.17), calls=%async_computation.2 | async-start | bytes 2097152 | tf_op jit(solution)/shard_map/all_to_all | solution.py:21
  49.0 2.3 fusion.8
  51.4 0.7 pad_maximum_fusion
  52.1 1.1 copy.185
  53.2 20.9 %all-to-all-done.2 = bf16[8,2,128,256]{3,2,1,0:T(8,128)(2,1)S(1)} async-done(((bf16[8,2,128,256]{3,2,1,0:T(8,128)(2,1)}), bf16[8,2,128,256]{3,2,1,0:T(8,128)(2,1)S(1)}, u32[]{:S(2)}, u32[]{:S(2)}) %all-to-all-start.2) | async-done | bytes 1048608 | tf_op jit(solution)/shard_map/all_to_all | solution.py:21
  74.1 0.6 copy.191
  74.9 6.3 %all_to_all.46 = bf16[2,8,2,128,256]{4,1,3,2,0:T(8,128)(2,1)} all-to-all(bf16[2,8,2,128,256]{4,1,3,2,0:T(8,128)(2,1)S(1)} %broadcast_in_dim.18), channel_id=1, replica_groups=mesh['zh'=4,'x'=4,'dp'=4,'ty'=8,'tc'=2] {'tc'}, dimensions={0} | all-to-all | bytes 4194304 | tf_op jit(solution)/shard_map/all_to_all | solution.py:21
  81.1 1.2 broadcast_in_dim.14
  82.3 5.4 %all-to-all-start = ((bf16[4,2,2,128,256]{3,4,2,1,0:T(8,128)(2,1)}), bf16[4,2,2,128,256]{3,4,2,1,0:T(8,128)(2,1)S(1)}, u32[]{:S(2)}, u32[]{:S(2)}) async-start(bf16[4,2,2,128,256]{3,4,2,1,0:T(8,128)(2,1)} %broadcast_in_dim.14), calls=%async_computation | async-start | bytes 2097152 | tf_op jit(solution)/shard_map/all_to_all | solution.py:21
  87.8 6.1 %copy.192 = bf16[2,128,8,2,256]{4,3,2,1,0:T(2,128)(2,1)} copy(bf16[2,128,8,2,256]{4,2,1,0,3:T(8,128)(2,1)} %bitcast.135) | data formatting | bytes 4194304 | tf_op jit(solution)/shard_map/transpose | solution.py:92
  93.9 4.5 %reshape_reshape.3 = bf16[256,4096]{1,0:T(8,128)(2,1)} reshape(bf16[2,128,8,2,256]{4,3,2,1,0:T(2,128)(2,1)} %copy.192) | data formatting | bytes 4194304 | tf_op jit(solution)/shard_map/reshape;reshape | solution.py:94
  98.4 2.9 %fusion.7 = bf16[256,256]{1,0:T(8,128)(2,1)S(1)} fusion(bf16[256,4096]{1,0:T(8,128)(2,1)} %reshape_reshape.3, bf16[4096,3,256]{2,0,1:T(8,128)(2,1)} %bitcast.138), kind=kOutput, calls=%fused_computation.19 | convolution fusion | flops 536936448 | bytes 4325376 | tf_op jit(solution)/shard_map/dot_general | solution.py:95
  101.5 2.9 %fusion.6 = bf16[256,256]{1,0:T(8,128)(2,1)S(1)} fusion(bf16[256,4096]{1,0:T(8,128)(2,1)} %reshape_reshape.3, bf16[4096,3,256]{2,0,1:T(8,128)(2,1)} %bitcast.139), kind=kOutput, calls=%fused_computation.18 | convolution fusion | flops 536936448 | bytes 4325376 | tf_op jit(solution)/shard_map/dot_general | solution.py:98
  104.4 0.8 copy.197
  105.2 0.9 reshape.56
  106.1 4.4 %all-to-all-done = bf16[4,2,2,128,256]{3,4,2,1,0:T(8,128)(2,1)S(1)} async-done(((bf16[4,2,2,128,256]{3,4,2,1,0:T(8,128)(2,1)}), bf16[4,2,2,128,256]{3,4,2,1,0:T(8,128)(2,1)S(1)}, u32[]{:S(2)}, u32[]{:S(2)}) %all-to-all-start) | async-done | bytes 1048608 | tf_op jit(solution)/shard_map/all_to_all | solution.py:21
  110.6 0.4 multiply_reduce_fusion.1
  111.0 0.7 fusion.2
  111.8 10.5 %all_to_all.47 = f32[4,3,2,4,4,128]{5,4,3,2,1,0:T(4,128)S(1)} all-to-all(f32[4,3,2,4,4,128]{5,4,3,2,1,0:T(4,128)S(1)} %broadcast_in_dim.19), channel_id=1, replica_groups=mesh['zh'=4,'x'=4,'dp'=4,'ty'=8,'tc'=2] {'dp'}, dimensions={0} | all-to-all | bytes 393216 | tf_op jit(solution)/shard_map/all_to_all | solution.py:21
  122.5 0.9 fusion.19
  123.3 0.5 fusion.11
  124.1 0.8 fusion.3
  124.8 0.5 fusion.9
  125.5 2.1 fusion
  127.6 4.5 %reshape.59 = bf16[2,128,8,2,256]{4,3,2,1,0:T(2,128)(2,1)} reshape(bf16[256,4096]{1,0:T(8,128)(2,1)} %fusion) | data formatting | bytes 4194304 | tf_op jit(solution)/shard_map/reshape | solution.py:143
  132.1 1.9 copy.288
  133.9 6.3 %all_to_all.48 = bf16[2,8,2,128,256]{4,1,3,2,0:T(8,128)(2,1)} all-to-all(bf16[2,8,2,128,256]{4,1,3,2,0:T(8,128)(2,1)S(1)} %bitcast.136), channel_id=1, replica_groups=mesh['zh'=4,'x'=4,'dp'=4,'ty'=8,'tc'=2] {'tc'}, dimensions={0} | all-to-all | bytes 4194304 | tf_op jit(solution)/shard_map/all_to_all | solution.py:146
  140.2 2.3 reduce_sum.79
  142.5 1.2 copy.208
  143.7 3.6 %all-to-all-start.6 = ((bf16[8,2,128,256]{3,2,1,0:T(8,128)(2,1)}), bf16[8,2,128,256]{3,2,1,0:T(8,128)(2,1)S(1)}, u32[]{:S(2)}, u32[]{:S(2)}) async-start(bf16[8,2,128,256]{3,2,1,0:T(8,128)(2,1)} %copy.208), calls=%async_computation.6 | async-start | bytes 2097152 | tf_op jit(solution)/shard_map/all_to_all | solution.py:149
  147.3 29.3 %all-to-all-done.6 = bf16[8,2,128,256]{3,2,1,0:T(8,128)(2,1)S(1)} async-done(((bf16[8,2,128,256]{3,2,1,0:T(8,128)(2,1)}), bf16[8,2,128,256]{3,2,1,0:T(8,128)(2,1)S(1)}, u32[]{:S(2)}, u32[]{:S(2)}) %all-to-all-start.6) | async-done | bytes 1048608 | tf_op jit(solution)/shard_map/all_to_all | solution.py:149
  176.8 0.7 copy.209
  177.5 3.4 %all-to-all-start.7 = ((f32[4,2,32,256]{3,2,1,0:T(8,128)}), f32[4,2,32,256]{3,2,1,0:T(8,128)S(1)}, u32[]{:S(2)}, u32[]{:S(2)}) async-start(f32[4,2,32,256]{3,2,1,0:T(8,128)} %copy.209), calls=%async_computation.7 | async-start | bytes 524288 | tf_op jit(solution)/shard_map/all_to_all | solution.py:47
  181.2 1.1 copy.215
  182.3 5.7 %all-to-all-done.7 = f32[4,2,32,256]{3,2,1,0:T(8,128)S(1)} async-done(((f32[4,2,32,256]{3,2,1,0:T(8,128)}), f32[4,2,32,256]{3,2,1,0:T(8,128)S(1)}, u32[]{:S(2)}, u32[]{:S(2)}) %all-to-all-start.7) | async-done | bytes 262176 | tf_op jit(solution)/shard_map/all_to_all | solution.py:47
  188.0 5.8 %all-to-all-start.8 = ((f32[4,2,128,256]{2,3,1,0:T(8,128)}), f32[4,2,128,256]{2,3,1,0:T(8,128)S(1)}, u32[]{:S(2)}, u32[]{:S(2)}) async-start(f32[4,2,128,256]{2,3,1,0:T(8,128)} %bitcast.38), calls=%async_computation.8 | async-start | bytes 2097152 | tf_op jit(solution)/shard_map/all_to_all | solution.py:128
  193.8 0.6 reduce_sum.81
  194.4 0.7 collective-permute-start.6
  195.1 0.9 select_add_fusion.1
  195.9 1.3 collective-permute-start.7
  197.2 1.3 collective-permute-start.8
  198.6 39.0 %collective-permute-done.7 = f32[2,32,256]{2,1,0:T(8,128)S(1)} collective-permute-done((f32[2,32,256]{2,1,0:T(8,128)S(1)}, f32[2,32,256]{2,1,0:T(8,128)S(1)}, u32[]{:S(2)}, u32[]{:S(2)}) %collective-permute-start.7) | collective-permute-done | bytes 65568 | tf_op jit(solution)/shard_map/ppermute | solution.py:51
  237.6 1.3 collective-permute-start.9
  238.9 1.3 collective-permute-start.10
  240.2 1.3 collective-permute-start.11
  241.5 0.8 copy.211
  242.3 1.5 collective-permute-done.9
  243.7 2.8 %collective-permute-done.10 = f32[2,32,256]{2,1,0:T(8,128)S(1)} collective-permute-done((f32[2,32,256]{2,1,0:T(8,128)S(1)}, f32[2,32,256]{2,1,0:T(8,128)S(1)}, u32[]{:S(2)}, u32[]{:S(2)}) %collective-permute-start.10) | collective-permute-done | bytes 65568 | tf_op jit(solution)/shard_map/ppermute | solution.py:56
  246.5 1.0 collective-permute-done.11
  247.6 0.7 copy.210
  248.3 1.1 copy.212
  249.4 1.0 fusion.21
  250.4 0.8 copy.216
  (46 shorter events, 2.1 us)
Async XLA Ops:
  0.0 1.6 copy-start
  1.6 7.3 %collective-permute-start = (bf16[2,32,256]{2,1,0:T(8,128)(2,1)S(1)}, bf16[2,32,256]{2,1,0:T(8,128)(2,1)S(1)}, u32[]{:S(2)}, u32[]{:S(2)}) collective-permute-start(bf16[2,32,256]{2,1,0:T(8,128)(2,1)S(1)} %get-tuple-element.15), channel_id=1, source_target_pairs={{0,192},{1,193},{2,194},{3,195},{4,196},{5,197},{6,198},{7,199},{8... | collective-permute-start | bytes 98312 | tf_op jit(solution)/shard_map/ppermute | solution.py:31
  6.3 2.9 %collective-permute-start.1 = (bf16[2,32,256]{2,1,0:T(8,128)(2,1)S(1)}, bf16[2,32,256]{2,1,0:T(8,128)(2,1)S(1)}, u32[]{:S(2)}, u32[]{:S(2)}) collective-permute-start(bf16[2,32,256]{2,1,0:T(8,128)(2,1)S(1)} %get-tuple-element.14), channel_id=1, source_target_pairs={{0,128},{1,129},{2,130},{3,131},{4,132},{5,133},{6,134},{7,135},{8... | collective-permute-start | bytes 98312 | tf_op jit(solution)/shard_map/ppermute | solution.py:31
  7.6 2.9 %collective-permute-start.2 = (bf16[2,32,256]{2,1,0:T(8,128)(2,1)S(1)}, bf16[2,32,256]{2,1,0:T(8,128)(2,1)S(1)}, u32[]{:S(2)}, u32[]{:S(2)}) collective-permute-start(bf16[2,32,256]{2,1,0:T(8,128)(2,1)S(1)} %get-tuple-element.13), channel_id=1, source_target_pairs={{0,64},{1,65},{2,66},{3,67},{4,68},{5,69},{6,70},{7,71},{8,72},{9,... | collective-permute-start | bytes 98312 | tf_op jit(solution)/shard_map/ppermute | solution.py:31
  10.5 18.0 %collective-permute-start.3 = (bf16[2,32,256]{2,1,0:T(8,128)(2,1)S(1)}, bf16[2,32,256]{2,1,0:T(8,128)(2,1)S(1)}, u32[]{:S(2)}, u32[]{:S(2)}) collective-permute-start(bf16[2,32,256]{2,1,0:T(8,128)(2,1)S(1)} %fusion.37), channel_id=1, source_target_pairs={{0,768},{1,769},{2,770},{3,771},{4,772},{5,773},{6,774},{7,775},{8... | collective-permute-start | bytes 98312 | tf_op jit(solution)/shard_map/ppermute | solution.py:36
  26.9 3.4 %collective-permute-start.4 = (bf16[2,32,256]{2,1,0:T(8,128)(2,1)S(1)}, bf16[2,32,256]{2,1,0:T(8,128)(2,1)S(1)}, u32[]{:S(2)}, u32[]{:S(2)}) collective-permute-start(bf16[2,32,256]{2,1,0:T(8,128)(2,1)S(1)} %fusion.37), channel_id=1, source_target_pairs={{0,256},{1,257},{2,258},{3,259},{4,260},{5,261},{6,262},{7,263},{8... | collective-permute-start | bytes 98312 | tf_op jit(solution)/shard_map/ppermute | solution.py:36
  30.3 0.7 collective-permute-start.5
  41.9 32.2 %all-to-all-start.2 = ((bf16[8,2,128,256]{3,2,1,0:T(8,128)(2,1)}), bf16[8,2,128,256]{3,2,1,0:T(8,128)(2,1)S(1)}, u32[]{:S(2)}, u32[]{:S(2)}) async-start(bf16[8,2,128,256]{3,2,1,0:T(8,128)(2,1)} %broadcast_in_dim.17), calls=%async_computation.2 | async-start | bytes 2097152 | tf_op jit(solution)/shard_map/all_to_all | solution.py:21
  49.0 2.3 copy-start.3
  82.3 28.2 %all-to-all-start = ((bf16[4,2,2,128,256]{3,4,2,1,0:T(8,128)(2,1)}), bf16[4,2,2,128,256]{3,4,2,1,0:T(8,128)(2,1)S(1)}, u32[]{:S(2)}, u32[]{:S(2)}) async-start(bf16[4,2,2,128,256]{3,4,2,1,0:T(8,128)(2,1)} %broadcast_in_dim.14), calls=%async_computation | async-start | bytes 2097152 | tf_op jit(solution)/shard_map/all_to_all | solution.py:21
  111.0 13.0 %slice-start = ((s8[6291456]{0:T(1024)(128)(4,1)}), s8[4194304]{0:T(1024)(128)(4,1)S(1)}, s32[]{:S(2)}) async-start(s8[6291456]{0:T(1024)(128)(4,1)} %bitcast.140), calls=%async_computation.9 | async-start | bytes 8388608
  122.5 1.6 slice-start.1
  123.3 1.5 copy-start.1
  143.7 32.9 %all-to-all-start.6 = ((bf16[8,2,128,256]{3,2,1,0:T(8,128)(2,1)}), bf16[8,2,128,256]{3,2,1,0:T(8,128)(2,1)S(1)}, u32[]{:S(2)}, u32[]{:S(2)}) async-start(bf16[8,2,128,256]{3,2,1,0:T(8,128)(2,1)} %copy.208), calls=%async_computation.6 | async-start | bytes 2097152 | tf_op jit(solution)/shard_map/all_to_all | solution.py:149
  176.7 4.2 %copy-start.2 = (bf16[2,4,4,128,128]{3,4,2,1,0:T(8,128)(2,1)S(1)}, bf16[2,4,4,128,128]{3,4,2,1,0:T(8,128)(2,1)}, u32[]{:S(2)}) copy-start(bf16[2,4,4,128,128]{3,4,2,1,0:T(8,128)(2,1)} %copy-done.1) | copy-start | bytes 3145732
  177.5 10.5 %all-to-all-start.7 = ((f32[4,2,32,256]{3,2,1,0:T(8,128)}), f32[4,2,32,256]{3,2,1,0:T(8,128)S(1)}, u32[]{:S(2)}, u32[]{:S(2)}) async-start(f32[4,2,32,256]{3,2,1,0:T(8,128)} %copy.209), calls=%async_computation.7 | async-start | bytes 524288 | tf_op jit(solution)/shard_map/all_to_all | solution.py:47
  181.2 60.3 %copy-start.4 = (bf16[1,2,128,256]{3,2,1,0:T(8,128)(2,1)S(1)}, bf16[1,2,128,256]{3,2,1,0:T(8,128)(2,1)}, u32[]{:S(2)}) copy-start(bf16[1,2,128,256]{3,2,1,0:T(8,128)(2,1)} %param.5) | copy-start | bytes 393220
  188.0 61.4 %all-to-all-start.8 = ((f32[4,2,128,256]{2,3,1,0:T(8,128)}), f32[4,2,128,256]{2,3,1,0:T(8,128)S(1)}, u32[]{:S(2)}, u32[]{:S(2)}) async-start(f32[4,2,128,256]{2,3,1,0:T(8,128)} %bitcast.38), calls=%async_computation.8 | async-start | bytes 2097152 | tf_op jit(solution)/shard_map/all_to_all | solution.py:128
  194.4 0.7 collective-permute-start.6
  195.9 41.6 %collective-permute-start.7 = (f32[2,32,256]{2,1,0:T(8,128)S(1)}, f32[2,32,256]{2,1,0:T(8,128)S(1)}, u32[]{:S(2)}, u32[]{:S(2)}) collective-permute-start(f32[2,32,256]{2,1,0:T(8,128)S(1)} %select_add_fusion.1), channel_id=1, source_target_pairs={{256,0},{257,1},{258,2},{259,3},{260,4},{261,5},{262,6},{263,7},{2... | collective-permute-start | bytes 196616 | tf_op jit(solution)/shard_map/ppermute | solution.py:51
  197.2 40.3 %collective-permute-start.8 = (f32[2,32,256]{2,1,0:T(8,128)S(1)}, f32[2,32,256]{2,1,0:T(8,128)S(1)}, u32[]{:S(2)}, u32[]{:S(2)}) collective-permute-start(f32[2,32,256]{2,1,0:T(8,128)S(1)} %select_add_fusion.1), channel_id=1, source_target_pairs={{768,0},{769,1},{770,2},{771,3},{772,4},{773,5},{774,6},{775,7},{7... | collective-permute-start | bytes 196616 | tf_op jit(solution)/shard_map/ppermute | solution.py:51
  237.6 6.2 %collective-permute-start.9 = (f32[2,32,256]{2,1,0:T(8,128)S(1)}, f32[2,32,256]{2,1,0:T(8,128)S(1)}, u32[]{:S(2)}, u32[]{:S(2)}) collective-permute-start(f32[2,32,256]{2,1,0:T(8,128)S(1)} %select_add_fusion), channel_id=1, source_target_pairs={{64,0},{65,1},{66,2},{67,3},{68,4},{69,5},{70,6},{71,7},{72,8},{73... | collective-permute-start | bytes 196616 | tf_op jit(solution)/shard_map/ppermute | solution.py:56
  238.9 7.7 %collective-permute-start.10 = (f32[2,32,256]{2,1,0:T(8,128)S(1)}, f32[2,32,256]{2,1,0:T(8,128)S(1)}, u32[]{:S(2)}, u32[]{:S(2)}) collective-permute-start(f32[2,32,256]{2,1,0:T(8,128)S(1)} %select_add_fusion), channel_id=1, source_target_pairs={{128,0},{129,1},{130,2},{131,3},{132,4},{133,5},{134,6},{135,7},{1... | collective-permute-start | bytes 196616 | tf_op jit(solution)/shard_map/ppermute | solution.py:56
  240.2 7.4 %collective-permute-start.11 = (f32[2,32,256]{2,1,0:T(8,128)S(1)}, f32[2,32,256]{2,1,0:T(8,128)S(1)}, u32[]{:S(2)}, u32[]{:S(2)}) collective-permute-start(f32[2,32,256]{2,1,0:T(8,128)S(1)} %select_add_fusion), channel_id=1, source_target_pairs={{192,0},{193,1},{194,2},{195,3},{196,4},{197,5},{198,6},{199,7},{2... | collective-permute-start | bytes 196616 | tf_op jit(solution)/shard_map/ppermute | solution.py:56

commit v5 on v4

--- a/solution.py
+++ b/solution.py
@@ -30,31 +30,25 @@
     for k in range(1, n_x):
         got = lax.ppermute(pieces[:, k], "x", [(0, k)])
         mine = jnp.where(x == k, got, mine)
-    for pairs in hi_rounds(n_hi):
-        nxt = mine
-        for a, b in pairs:
-            got = lax.ppermute(mine, "zh", [(a, b)])
-            nxt = jnp.where(zh == b, got, nxt)
-        mine = nxt
-    full = gather_axis(mine, "x", n_x)
-    return jnp.moveaxis(full, 0, 1).reshape(value.shape)
+    out = mine
+    for b in range(1, n_hi):
+        got = lax.ppermute(mine, "zh", [(0, b)])
+        out = jnp.where(zh == b, got, out)
+    return out
 
 
-def seg_reduce(value, n_hi, n_x):
+def seg_reduce(mine, n_hi, n_x):
     zh = lax.axis_index("zh")
-    quarter = value.shape[1] // n_x
-    pieces = jnp.moveaxis(value.reshape(value.shape[0], n_x, quarter, value.shape[2]), 1, 0)
-    mine = jnp.sum(lax.all_to_all(pieces, "x", 0, 0, tiled=False), axis=0)
-    for pairs in reversed(hi_rounds(n_hi)):
-        acc = mine
-        for a, b in pairs:
-            got = lax.ppermute(mine, "zh", [(b, a)])
-            acc = acc + jnp.where(zh == a, got, jnp.zeros_like(got))
-        mine = acc
-    parts = [mine]
+    acc = mine
+    for b in range(1, n_hi):
+        got = lax.ppermute(mine, "zh", [(b, 0)])
+        acc = acc + got
+    acc = jnp.where(zh == 0, acc, mine)
+    parts = [acc]
     for k in range(1, n_x):
-        parts.append(lax.ppermute(mine, "x", [(k, 0)]))
-    return jnp.stack(parts, axis=1).reshape(value.shape)
+        parts.append(lax.ppermute(acc, "x", [(k, 0)]))
+    stacked = jnp.stack(parts, axis=1)
+    return stacked.reshape(stacked.shape[0], -1, stacked.shape[-1])
 
 
 def shards(inbound, weights, cotangent):
@@ -86,10 +80,11 @@
     grad_heads = slots[:, 1].reshape(n_dp, micro_count, row_count, head_count, HD)
 
     chunk = lax.dynamic_slice_in_dim(states, tix * chunk_width, chunk_width, axis=2)
-    chunk = seg_broadcast(chunk, n_hi, n_x)
-    own = gather_axis(chunk, "ty", n_y)
+    piece = seg_broadcast(chunk, n_hi, n_x)
+    own = gather_axis(piece, ("x", "ty"), n_x * n_y)
     both = gather_axis(own, "tc", n_c)
-    encoded = jnp.transpose(both, (2, 3, 1, 0, 4)).reshape(micro_count, row_count, model_width)
+    both = both.reshape(n_c, n_x, n_y, micro_count, row_count // n_x, chunk_width)
+    encoded = jnp.transpose(both, (3, 1, 4, 2, 0, 5)).reshape(micro_count, row_count, model_width)
 
     flat_enc = encoded.reshape(rows, model_width)
     key_heads = jnp.dot(flat_enc, layer[:, 1, :], preferred_element_type=jnp.float32).astype(
@@ -145,10 +140,13 @@
     pair_sum = jnp.sum(
         lax.all_to_all(head_terms, "tc", 0, 0, tiled=False).astype(jnp.float32), axis=0
     ).astype(jnp.bfloat16)
+    pair_sum = jnp.where(seg > 0, pair_sum, jnp.zeros_like(pair_sum))
+    quarter = row_count // n_x
+    pair_sum = pair_sum.reshape(n_y, micro_count, n_x, quarter, chunk_width)
+    pair_sum = jnp.transpose(pair_sum, (2, 0, 1, 3, 4)).reshape(n_x * n_y, micro_count, quarter, chunk_width)
     heads_total = jnp.sum(
-        lax.all_to_all(pair_sum, "ty", 0, 0, tiled=False).astype(jnp.float32), axis=0
+        lax.all_to_all(pair_sum, ("x", "ty"), 0, 0, tiled=False).astype(jnp.float32), axis=0
     )
-    heads_total = jnp.where(seg > 0, heads_total, jnp.zeros_like(heads_total))
     sections = seg_reduce(heads_total, n_hi, n_x)
     encoder_grad = (sections + cotangent[0].astype(jnp.float32)).astype(jnp.bfloat16)
     result = jnp.where(seg == 0, encoder_grad, context)

time: 252 us -> 241 us (0.956)
  the two profiles are of different devices: /device:TPU:128 before, /device:TPU:136 now
where the time goes in v5:
time: 241 us; the launch traced here: 239 us
  waiting for transfers between devices  97.5 us (40%)
  starting transfers between devices  68.3 us (28%)
  local copies, waits for them, and re-layouts  30.8 us (13%)
  matrix products  19.1 us (8%)
  blocking collectives  12.6 us (5%)
  other arithmetic  10.3 us (4%)
    all_to_all x3, waiting for transfers between devices, gather_axis(): return lax.all_to_all(spread, axis, 0, 0, tiled=False)  32.4 us
    ppermute x3, waiting for transfers between devices, seg_reduce(): got = lax.ppermute(mine, 'zh', [(b, 0)])  30 us
    all_to_all x1, waiting for transfers between devices, shards(): lax.all_to_all(pair_sum, ('x', 'ty'), 0, 0, tiled=False).astype(jnp.float32)  26.2 us
    all_to_all x3, starting transfers between devices, gather_axis(): return lax.all_to_all(spread, axis, 0, 0, tiled=False)  22.2 us
    ppermute x3, starting transfers between devices, seg_broadcast(): got = lax.ppermute(mine, 'zh', [(0, b)])  19.5 us
    ppermute x3, starting transfers between devices, seg_broadcast(): got = lax.ppermute(pieces[:, k], 'x', [(0, k)])  7.25 us
    all_to_all x1, starting transfers between devices, shards(): lax.all_to_all(context_part, 'dp', 0, 0, tiled=False)  6.53 us
    reshape x2, local copies, waits for them, and re-layouts, shards(): head_terms.reshape(micro_count, row_count, n_y, n_c, chunk_width)  6.33 us
  transfers between devices with their start and end apart: 17, of which 12 were waited for; matrix products, arithmetic and copies ran while one was open for 12% of the time, Pallas kernels for 0%

profile of v5, /device:TPU:136, one launch (start us, length us, event | category | flops | bytes accessed | tf_op | source)
XLA Modules:
  0.0 239.1 jit_solution(12335630336591514748)
XLA Ops:
  0.0 1.6 copy-done
  1.6 4.7 %collective-permute-start = (bf16[2,32,256]{2,1,0:T(8,128)(2,1)S(1)}, bf16[2,32,256]{2,1,0:T(8,128)(2,1)S(1)}, u32[]{:S(2)}, u32[]{:S(2)}) collective-permute-start(bf16[2,32,256]{2,1,0:T(8,128)(2,1)S(1)} %get-tuple-element.15), channel_id=1, source_target_pairs={{0,192},{1,193},{2,194},{3,195},{4,196},{5,197},{6,198},{7,199},{8... | collective-permute-start | bytes 98312 | tf_op jit(solution)/shard_map/ppermute | solution.py:31
  6.3 1.3 collective-permute-start.1
  7.6 1.3 collective-permute-start.2
  9.2 1.3 collective-permute-done.2
  10.5 16.4 %collective-permute-start.3 = (bf16[2,32,256]{2,1,0:T(8,128)(2,1)S(1)}, bf16[2,32,256]{2,1,0:T(8,128)(2,1)S(1)}, u32[]{:S(2)}, u32[]{:S(2)}) collective-permute-start(bf16[2,32,256]{2,1,0:T(8,128)(2,1)S(1)} %fusion.35), channel_id=1, source_target_pairs={{0,768},{1,769},{2,770},{3,771},{4,772},{5,773},{6,774},{7,775},{8... | collective-permute-start | bytes 98312 | tf_op jit(solution)/shard_map/ppermute | solution.py:35
  26.9 1.8 collective-permute-start.4
  28.7 1.3 collective-permute-start.5
  30.1 0.9 collective-permute-done.4
  30.9 1.2 collective-permute-done.5
  32.2 1.1 broadcast_in_dim.11
  33.3 9.9 %all-to-all-start.1 = ((bf16[32,2,32,256]{3,2,1,0:T(8,128)(2,1)}), bf16[32,2,32,256]{3,2,1,0:T(8,128)(2,1)S(1)}, u32[]{:S(2)}, u32[]{:S(2)}) async-start(bf16[32,2,32,256]{3,2,1,0:T(8,128)(2,1)} %broadcast_in_dim.11), calls=%async_computation.1 | async-start | bytes 2097152 | tf_op jit(solution)/shard_map/all_to_all | solution.py:21
  43.1 2.3 fusion.8
  45.5 0.7 pad_maximum_fusion
  46.2 1.1 copy.161
  47.3 22.6 %all-to-all-done.1 = bf16[32,2,32,256]{3,2,1,0:T(8,128)(2,1)S(1)} async-done(((bf16[32,2,32,256]{3,2,1,0:T(8,128)(2,1)}), bf16[32,2,32,256]{3,2,1,0:T(8,128)(2,1)S(1)}, u32[]{:S(2)}, u32[]{:S(2)}) %all-to-all-start.1) | async-done | bytes 1048608 | tf_op jit(solution)/shard_map/all_to_all | solution.py:21
  70.2 6.3 %all_to_all.35 = bf16[2,32,2,32,256]{4,3,2,1,0:T(8,128)(2,1)} all-to-all(bf16[2,32,2,32,256]{4,3,2,1,0:T(8,128)(2,1)S(1)} %broadcast_in_dim.12), channel_id=1, replica_groups=mesh['zh'=4,'x'=4,'dp'=4,'ty'=8,'tc'=2] {'tc'}, dimensions={0} | all-to-all | bytes 4194304 | tf_op jit(solution)/shard_map/all_to_all | solution.py:21
  76.5 1.2 broadcast_in_dim.10
  77.7 5.7 %all-to-all-start = ((bf16[4,2,2,128,256]{3,4,2,1,0:T(8,128)(2,1)}), bf16[4,2,2,128,256]{3,4,2,1,0:T(8,128)(2,1)S(1)}, u32[]{:S(2)}, u32[]{:S(2)}) async-start(bf16[4,2,2,128,256]{3,4,2,1,0:T(8,128)(2,1)} %broadcast_in_dim.10), calls=%async_computation | async-start | bytes 2097152 | tf_op jit(solution)/shard_map/all_to_all | solution.py:21
  83.4 5.1 %copy.166 = bf16[2,4,32,8,2,256]{5,4,3,2,1,0:T(2,128)(2,1)} copy(bf16[2,4,32,8,2,256]{5,2,0,3,1,4:T(8,128)(2,1)} %bitcast.143) | data formatting | bytes 4194304 | tf_op jit(solution)/shard_map/transpose | solution.py:87
  88.5 4.5 %reshape_reshape.3 = bf16[256,4096]{1,0:T(8,128)(2,1)} reshape(bf16[2,4,32,8,2,256]{5,4,3,2,1,0:T(2,128)(2,1)} %copy.166) | data formatting | bytes 4194304 | tf_op jit(solution)/shard_map/reshape;reshape | solution.py:89
  92.9 2.9 %fusion.7 = bf16[256,256]{1,0:T(8,128)(2,1)S(1)} fusion(bf16[256,4096]{1,0:T(8,128)(2,1)} %reshape_reshape.3, bf16[4096,3,256]{2,0,1:T(8,128)(2,1)} %bitcast.148), kind=kOutput, calls=%fused_computation.19 | convolution fusion | flops 536936448 | bytes 4325376 | tf_op jit(solution)/shard_map/dot_general | solution.py:90
  96.0 2.9 %fusion.6 = bf16[256,256]{1,0:T(8,128)(2,1)S(1)} fusion(bf16[256,4096]{1,0:T(8,128)(2,1)} %reshape_reshape.3, bf16[4096,3,256]{2,0,1:T(8,128)(2,1)} %bitcast.149), kind=kOutput, calls=%fused_computation.18 | convolution fusion | flops 536936448 | bytes 4325376 | tf_op jit(solution)/shard_map/dot_general | solution.py:93
  99.0 0.8 copy.171
  99.7 0.9 reshape.62
  100.7 5.5 %all-to-all-done = bf16[4,2,2,128,256]{3,4,2,1,0:T(8,128)(2,1)S(1)} async-done(((bf16[4,2,2,128,256]{3,4,2,1,0:T(8,128)(2,1)}), bf16[4,2,2,128,256]{3,4,2,1,0:T(8,128)(2,1)S(1)}, u32[]{:S(2)}, u32[]{:S(2)}) %all-to-all-start) | async-done | bytes 1048608 | tf_op jit(solution)/shard_map/all_to_all | solution.py:21
  106.2 0.8 copy-done.6
  107.5 2.0 fusion.2
  109.5 0.7 broadcast_in_dim.13
  110.2 6.6 %all-to-all-start.3 = ((f32[4,3,2,4,4,128]{5,4,3,2,1,0:T(4,128)}), f32[4,3,2,4,4,128]{5,4,3,2,1,0:T(4,128)S(1)}, u32[]{:S(2)}, u32[]{:S(2)}) async-start(f32[4,3,2,4,4,128]{5,4,3,2,1,0:T(4,128)} %broadcast_in_dim.13), calls=%async_computation.3 | async-start | bytes 393216 | tf_op jit(solution)/shard_map/all_to_all | solution.py:21
  116.8 4.3 %all-to-all-done.3 = f32[4,3,2,4,4,128]{5,4,3,2,1,0:T(4,128)S(1)} async-done(((f32[4,3,2,4,4,128]{5,4,3,2,1,0:T(4,128)}), f32[4,3,2,4,4,128]{5,4,3,2,1,0:T(4,128)S(1)}, u32[]{:S(2)}, u32[]{:S(2)}) %all-to-all-start.3) | async-done | bytes 196640 | tf_op jit(solution)/shard_map/all_to_all | solution.py:21
  121.2 3.1 %fusion.17 = (bf16[2,4,4,128,128]{3,4,2,1,0:T(8,128)(2,1)S(1)}, bf16[2,4,4,128,128]{3,4,2,1,0:T(8,128)(2,1)S(1)}) fusion(f32[2,4,4,128]{3,2,1,0:T(4,128)S(1)} %get-tuple-element.7, f32[2,4,4,128]{3,2,1,0:T(4,128)S(1)} %bitcast_reduce_fusion, f32[2,4,4,128,128]{3,4,2,1,0:T(8,128)} %copy-done.1, f32[2,4,4,128,128]{3,4,2,1,0:T(8,128)} %get-tuple-element.18, ...), kind=kLoop, calls=%fused_computation.30 | loop fusion | flops 4194304 | bytes 6340608 | tf_op jit(solution)/shard_map/convert_element_type | solution.py:117
  124.3 0.5 fusion.11
  125.0 2.4 %fusion.3 = f32[256,4096]{1,0:T(8,128)S(1)} fusion(bf16[4096,3,256]{2,0,1:T(8,128)(2,1)} %bitcast.150, bf16[32,8,2,128]{3,2,1,0:T(2,128)(2,1)S(1)} %bitcast.161), kind=kOutput, calls=%fused_computation.13 | convolution fusion | flops 536870912 | bytes 6422528 | tf_op jit(solution)/shard_map/rc,dc->rd/dot_general | solution.py:133
  127.4 0.5 fusion.9
  128.0 3.7 %fusion = bf16[256,4096]{1,0:T(8,128)(2,1)} fusion(f32[256,4096]{1,0:T(8,128)S(1)} %fusion.3, bf16[4096,3,256]{2,0,1:T(8,128)(2,1)} %bitcast.151, bf16[32,8,2,128]{3,2,1,0:T(2,128)(2,1)S(1)} %bitcast.160), kind=kOutput, calls=%fused_computation.1 | convolution fusion | flops 538968064 | bytes 8519680 | tf_op jit(solution)/shard_map/rc,dc->rd/dot_general | solution.py:135
  131.7 4.5 %reshape.65 = bf16[2,128,8,2,256]{4,3,2,1,0:T(2,128)(2,1)} reshape(bf16[256,4096]{1,0:T(8,128)(2,1)} %fusion) | data formatting | bytes 4194304 | tf_op jit(solution)/shard_map/reshape | solution.py:138
  136.2 1.9 copy.263
  138.1 6.3 %all_to_all.36 = bf16[2,8,2,128,256]{4,1,3,2,0:T(8,128)(2,1)} all-to-all(bf16[2,8,2,128,256]{4,1,3,2,0:T(8,128)(2,1)S(1)} %bitcast.144), channel_id=1, replica_groups=mesh['zh'=4,'x'=4,'dp'=4,'ty'=8,'tc'=2] {'tc'}, dimensions={0} | all-to-all | bytes 4194304 | tf_op jit(solution)/shard_map/all_to_all | solution.py:141
  144.4 2.3 reduce_sum.70
  146.7 1.2 copy.185
  148.0 5.1 %all-to-all-start.5 = ((bf16[32,2,32,256]{3,2,1,0:T(8,128)(2,1)}), bf16[32,2,32,256]{3,2,1,0:T(8,128)(2,1)S(1)}, u32[]{:S(2)}, u32[]{:S(2)}) async-start(bf16[32,2,32,256]{3,2,1,0:T(8,128)(2,1)} %bitcast.146), calls=%async_computation.5 | async-start | bytes 2097152 | tf_op jit(solution)/shard_map/all_to_all | solution.py:148
  153.1 1.5 convolution_bitcast_fusion
  154.6 1.1 copy.193
  155.7 26.2 %all-to-all-done.5 = bf16[32,2,32,256]{3,2,1,0:T(8,128)(2,1)S(1)} async-done(((bf16[32,2,32,256]{3,2,1,0:T(8,128)(2,1)}), bf16[32,2,32,256]{3,2,1,0:T(8,128)(2,1)S(1)}, u32[]{:S(2)}, u32[]{:S(2)}) %all-to-all-start.5) | async-done | bytes 1048608 | tf_op jit(solution)/shard_map/all_to_all | solution.py:148
  181.9 1.0 copy-done.2
  182.9 6.5 %all-to-all-start.6 = ((f32[4,2,128,256]{2,3,1,0:T(8,128)}), f32[4,2,128,256]{2,3,1,0:T(8,128)S(1)}, u32[]{:S(2)}, u32[]{:S(2)}) async-start(f32[4,2,128,256]{2,3,1,0:T(8,128)} %bitcast.42), calls=%async_computation.6 | async-start | bytes 2097152 | tf_op jit(solution)/shard_map/all_to_all | solution.py:123
  189.4 1.4 convert_reduce_fusion
  190.8 1.3 collective-permute-start.6
  192.1 1.3 collective-permute-start.7
  193.4 1.3 collective-permute-start.8
  194.7 30.0 %collective-permute-done.6 = f32[2,32,256]{2,1,0:T(8,128)S(1)} collective-permute-done((f32[2,32,256]{2,1,0:T(8,128)S(1)}, f32[2,32,256]{2,1,0:T(8,128)S(1)}, u32[]{:S(2)}, u32[]{:S(2)}) %collective-permute-start.6) | collective-permute-done | bytes 65568 | tf_op jit(solution)/shard_map/ppermute | solution.py:44
  224.7 0.9 add_select_fusion
  225.5 1.3 collective-permute-start.9
  226.8 1.3 collective-permute-start.10
  228.1 1.3 collective-permute-start.11
  229.5 0.8 copy.189
  230.2 1.5 collective-permute-done.9
  231.7 2.8 %collective-permute-done.10 = f32[2,32,256]{2,1,0:T(8,128)S(1)} collective-permute-done((f32[2,32,256]{2,1,0:T(8,128)S(1)}, f32[2,32,256]{2,1,0:T(8,128)S(1)}, u32[]{:S(2)}, u32[]{:S(2)}) %collective-permute-start.10) | collective-permute-done | bytes 65568 | tf_op jit(solution)/shard_map/ppermute | solution.py:49
  234.5 1.0 collective-permute-done.11
  235.5 0.7 pad_maximum_fusion.1
  236.2 1.1 copy.190
  237.4 1.0 fusion.19
  238.3 0.8 copy.194
  (41 shorter events, 1.8 us)
Async XLA Ops:
  0.0 1.6 copy-start
  1.6 7.3 %collective-permute-start = (bf16[2,32,256]{2,1,0:T(8,128)(2,1)S(1)}, bf16[2,32,256]{2,1,0:T(8,128)(2,1)S(1)}, u32[]{:S(2)}, u32[]{:S(2)}) collective-permute-start(bf16[2,32,256]{2,1,0:T(8,128)(2,1)S(1)} %get-tuple-element.15), channel_id=1, source_target_pairs={{0,192},{1,193},{2,194},{3,195},{4,196},{5,197},{6,198},{7,199},{8... | collective-permute-start | bytes 98312 | tf_op jit(solution)/shard_map/ppermute | solution.py:31
  6.3 2.9 %collective-permute-start.1 = (bf16[2,32,256]{2,1,0:T(8,128)(2,1)S(1)}, bf16[2,32,256]{2,1,0:T(8,128)(2,1)S(1)}, u32[]{:S(2)}, u32[]{:S(2)}) collective-permute-start(bf16[2,32,256]{2,1,0:T(8,128)(2,1)S(1)} %get-tuple-element.14), channel_id=1, source_target_pairs={{0,128},{1,129},{2,130},{3,131},{4,132},{5,133},{6,134},{7,135},{8... | collective-permute-start | bytes 98312 | tf_op jit(solution)/shard_map/ppermute | solution.py:31
  7.6 2.9 %collective-permute-start.2 = (bf16[2,32,256]{2,1,0:T(8,128)(2,1)S(1)}, bf16[2,32,256]{2,1,0:T(8,128)(2,1)S(1)}, u32[]{:S(2)}, u32[]{:S(2)}) collective-permute-start(bf16[2,32,256]{2,1,0:T(8,128)(2,1)S(1)} %get-tuple-element.13), channel_id=1, source_target_pairs={{0,64},{1,65},{2,66},{3,67},{4,68},{5,69},{6,70},{7,71},{8,72},{9,... | collective-permute-start | bytes 98312 | tf_op jit(solution)/shard_map/ppermute | solution.py:31
  10.5 19.6 %collective-permute-start.3 = (bf16[2,32,256]{2,1,0:T(8,128)(2,1)S(1)}, bf16[2,32,256]{2,1,0:T(8,128)(2,1)S(1)}, u32[]{:S(2)}, u32[]{:S(2)}) collective-permute-start(bf16[2,32,256]{2,1,0:T(8,128)(2,1)S(1)} %fusion.35), channel_id=1, source_target_pairs={{0,768},{1,769},{2,770},{3,771},{4,772},{5,773},{6,774},{7,775},{8... | collective-permute-start | bytes 98312 | tf_op jit(solution)/shard_map/ppermute | solution.py:35
  26.9 4.0 %collective-permute-start.4 = (bf16[2,32,256]{2,1,0:T(8,128)(2,1)S(1)}, bf16[2,32,256]{2,1,0:T(8,128)(2,1)S(1)}, u32[]{:S(2)}, u32[]{:S(2)}) collective-permute-start(bf16[2,32,256]{2,1,0:T(8,128)(2,1)S(1)} %fusion.35), channel_id=1, source_target_pairs={{0,512},{1,513},{2,514},{3,515},{4,516},{5,517},{6,518},{7,519},{8... | collective-permute-start | bytes 98312 | tf_op jit(solution)/shard_map/ppermute | solution.py:35
  28.7 3.4 %collective-permute-start.5 = (bf16[2,32,256]{2,1,0:T(8,128)(2,1)S(1)}, bf16[2,32,256]{2,1,0:T(8,128)(2,1)S(1)}, u32[]{:S(2)}, u32[]{:S(2)}) collective-permute-start(bf16[2,32,256]{2,1,0:T(8,128)(2,1)S(1)} %fusion.35), channel_id=1, source_target_pairs={{0,256},{1,257},{2,258},{3,259},{4,260},{5,261},{6,262},{7,263},{8... | collective-permute-start | bytes 98312 | tf_op jit(solution)/shard_map/ppermute | solution.py:35
  33.3 36.7 %all-to-all-start.1 = ((bf16[32,2,32,256]{3,2,1,0:T(8,128)(2,1)}), bf16[32,2,32,256]{3,2,1,0:T(8,128)(2,1)S(1)}, u32[]{:S(2)}, u32[]{:S(2)}) async-start(bf16[32,2,32,256]{3,2,1,0:T(8,128)(2,1)} %broadcast_in_dim.11), calls=%async_computation.1 | async-start | bytes 2097152 | tf_op jit(solution)/shard_map/all_to_all | solution.py:21
  43.1 2.4 copy-start.8
  77.7 28.5 %all-to-all-start = ((bf16[4,2,2,128,256]{3,4,2,1,0:T(8,128)(2,1)}), bf16[4,2,2,128,256]{3,4,2,1,0:T(8,128)(2,1)S(1)}, u32[]{:S(2)}, u32[]{:S(2)}) async-start(bf16[4,2,2,128,256]{3,4,2,1,0:T(8,128)(2,1)} %broadcast_in_dim.10), calls=%async_computation | async-start | bytes 2097152 | tf_op jit(solution)/shard_map/all_to_all | solution.py:21
  106.2 0.8 copy-start.6
  106.2 3.2 %copy-start.4 = (bf16[4,1,2,128,256]{3,4,2,1,0:T(8,128)(2,1)}, bf16[4,1,2,128,256]{3,4,2,1,0:T(8,128)(2,1)S(1)}, u32[]{:S(2)}) copy-start(bf16[4,1,2,128,256]{3,4,2,1,0:T(8,128)(2,1)S(1)} %get-tuple-element.11) | copy-start | bytes 1572868
  107.5 2.0 copy-start.1
  110.2 10.9 %all-to-all-start.3 = ((f32[4,3,2,4,4,128]{5,4,3,2,1,0:T(4,128)}), f32[4,3,2,4,4,128]{5,4,3,2,1,0:T(4,128)S(1)}, u32[]{:S(2)}, u32[]{:S(2)}) async-start(f32[4,3,2,4,4,128]{5,4,3,2,1,0:T(4,128)} %broadcast_in_dim.13), calls=%async_computation.3 | async-start | bytes 393216 | tf_op jit(solution)/shard_map/all_to_all | solution.py:21
  121.2 3.1 %copy-start.7 = (bf16[4,1,2,128,256]{3,4,2,1,0:T(8,128)(2,1)S(1)}, bf16[4,1,2,128,256]{3,4,2,1,0:T(8,128)(2,1)}, u32[]{:S(2)}) copy-start(bf16[4,1,2,128,256]{3,4,2,1,0:T(8,128)(2,1)} %copy-done.6) | copy-start | bytes 1572868
  124.3 3.1 %copy-start.3 = (bf16[2,4,4,128,128]{3,4,2,1,0:T(8,128)(2,1)}, bf16[2,4,4,128,128]{3,4,2,1,0:T(8,128)(2,1)S(1)}, u32[]{:S(2)}) copy-start(bf16[2,4,4,128,128]{3,4,2,1,0:T(8,128)(2,1)S(1)} %get-tuple-element.9) | copy-start | bytes 3145732
  124.9 2.4 %copy-start.5 = (bf16[4,1,2,128,256]{3,4,2,1,0:T(8,128)(2,1)S(1)}, bf16[4,1,2,128,256]{3,4,2,1,0:T(8,128)(2,1)}, u32[]{:S(2)}) copy-start(bf16[4,1,2,128,256]{3,4,2,1,0:T(8,128)(2,1)} %copy-done.4) | copy-start | bytes 1572868
  148.0 33.9 %all-to-all-start.5 = ((bf16[32,2,32,256]{3,2,1,0:T(8,128)(2,1)}), bf16[32,2,32,256]{3,2,1,0:T(8,128)(2,1)S(1)}, u32[]{:S(2)}, u32[]{:S(2)}) async-start(bf16[32,2,32,256]{3,2,1,0:T(8,128)(2,1)} %bitcast.146), calls=%async_computation.5 | async-start | bytes 2097152 | tf_op jit(solution)/shard_map/all_to_all | solution.py:148
  155.7 73.7 %copy-start.9 = (bf16[1,2,128,256]{3,2,1,0:T(8,128)(2,1)S(1)}, bf16[1,2,128,256]{3,2,1,0:T(8,128)(2,1)}, u32[]{:S(2)}) copy-start(bf16[1,2,128,256]{3,2,1,0:T(8,128)(2,1)} %param.5) | copy-start | bytes 393220
  181.9 1.0 copy-start.2
  182.9 54.4 %all-to-all-start.6 = ((f32[4,2,128,256]{2,3,1,0:T(8,128)}), f32[4,2,128,256]{2,3,1,0:T(8,128)S(1)}, u32[]{:S(2)}, u32[]{:S(2)}) async-start(f32[4,2,128,256]{2,3,1,0:T(8,128)} %bitcast.42), calls=%async_computation.6 | async-start | bytes 2097152 | tf_op jit(solution)/shard_map/all_to_all | solution.py:123
  190.8 33.9 %collective-permute-start.6 = (f32[2,32,256]{2,1,0:T(8,128)S(1)}, f32[2,32,256]{2,1,0:T(8,128)S(1)}, u32[]{:S(2)}, u32[]{:S(2)}) collective-permute-start(f32[2,32,256]{2,1,0:T(8,128)S(1)} %convert_reduce_fusion), channel_id=1, source_target_pairs={{256,0},{257,1},{258,2},{259,3},{260,4},{261,5},{262,6},{263,7},{2... | collective-permute-start | bytes 196616 | tf_op jit(solution)/shard_map/ppermute | solution.py:44
  192.1 32.6 %collective-permute-start.7 = (f32[2,32,256]{2,1,0:T(8,128)S(1)}, f32[2,32,256]{2,1,0:T(8,128)S(1)}, u32[]{:S(2)}, u32[]{:S(2)}) collective-permute-start(f32[2,32,256]{2,1,0:T(8,128)S(1)} %convert_reduce_fusion), channel_id=1, source_target_pairs={{512,0},{513,1},{514,2},{515,3},{516,4},{517,5},{518,6},{519,7},{5... | collective-permute-start | bytes 196616 | tf_op jit(solution)/shard_map/ppermute | solution.py:44
  193.4 31.3 %collective-permute-start.8 = (f32[2,32,256]{2,1,0:T(8,128)S(1)}, f32[2,32,256]{2,1,0:T(8,128)}, u32[]{:S(2)}, u32[]{:S(2)}) collective-permute-start(f32[2,32,256]{2,1,0:T(8,128)S(1)} %convert_reduce_fusion), channel_id=1, source_target_pairs={{768,0},{769,1},{770,2},{771,3},{772,4},{773,5},{774,6},{775,7},{7... | collective-permute-start | bytes 196616 | tf_op jit(solution)/shard_map/ppermute | solution.py:44
  225.5 6.2 %collective-permute-start.9 = (f32[2,32,256]{2,1,0:T(8,128)S(1)}, f32[2,32,256]{2,1,0:T(8,128)S(1)}, u32[]{:S(2)}, u32[]{:S(2)}) collective-permute-start(f32[2,32,256]{2,1,0:T(8,128)S(1)} %add_select_fusion), channel_id=1, source_target_pairs={{64,0},{65,1},{66,2},{67,3},{68,4},{69,5},{70,6},{71,7},{72,8},{73... | collective-permute-start | bytes 196616 | tf_op jit(solution)/shard_map/ppermute | solution.py:49
  226.8 7.7 %collective-permute-start.10 = (f32[2,32,256]{2,1,0:T(8,128)S(1)}, f32[2,32,256]{2,1,0:T(8,128)S(1)}, u32[]{:S(2)}, u32[]{:S(2)}) collective-permute-start(f32[2,32,256]{2,1,0:T(8,128)S(1)} %add_select_fusion), channel_id=1, source_target_pairs={{128,0},{129,1},{130,2},{131,3},{132,4},{133,5},{134,6},{135,7},{1... | collective-permute-start | bytes 196616 | tf_op jit(solution)/shard_map/ppermute | solution.py:49
  228.1 7.4 %collective-permute-start.11 = (f32[2,32,256]{2,1,0:T(8,128)S(1)}, f32[2,32,256]{2,1,0:T(8,128)S(1)}, u32[]{:S(2)}, u32[]{:S(2)}) collective-permute-start(f32[2,32,256]{2,1,0:T(8,128)S(1)} %add_select_fusion), channel_id=1, source_target_pairs={{192,0},{193,1},{194,2},{195,3},{196,4},{197,5},{198,6},{199,7},{2... | collective-permute-start | bytes 196616 | tf_op jit(solution)/shard_map/ppermute | solution.py:49

commit v6 on v5

--- a/solution.py
+++ b/solution.py
@@ -39,14 +39,16 @@
 
 def seg_reduce(mine, n_hi, n_x):
     zh = lax.axis_index("zh")
+    sent = mine.astype(jnp.bfloat16)
     acc = mine
     for b in range(1, n_hi):
-        got = lax.ppermute(mine, "zh", [(b, 0)])
-        acc = acc + got
+        got = lax.ppermute(sent, "zh", [(b, 0)])
+        acc = acc + got.astype(jnp.float32)
     acc = jnp.where(zh == 0, acc, mine)
     parts = [acc]
+    sent = acc.astype(jnp.bfloat16)
     for k in range(1, n_x):
-        parts.append(lax.ppermute(acc, "x", [(k, 0)]))
+        parts.append(lax.ppermute(sent, "x", [(k, 0)]).astype(jnp.float32))
     stacked = jnp.stack(parts, axis=1)
     return stacked.reshape(stacked.shape[0], -1, stacked.shape[-1])
 
@@ -76,16 +78,17 @@
     ).astype(jnp.bfloat16)
     query = query.reshape(micro_count, row_count, feat_width)
     slots = gather_axis(jnp.stack([query, cotangent[0]]), "dp", n_dp)
-    query_heads = slots[:, 0].reshape(n_dp, micro_count, row_count, head_count, HD)
-    grad_heads = slots[:, 1].reshape(n_dp, micro_count, row_count, head_count, HD)
 
     chunk = lax.dynamic_slice_in_dim(states, tix * chunk_width, chunk_width, axis=2)
     piece = seg_broadcast(chunk, n_hi, n_x)
+    slots, piece = lax.optimization_barrier((slots, piece))
     own = gather_axis(piece, ("x", "ty"), n_x * n_y)
     both = gather_axis(own, "tc", n_c)
     both = both.reshape(n_c, n_x, n_y, micro_count, row_count // n_x, chunk_width)
     encoded = jnp.transpose(both, (3, 1, 4, 2, 0, 5)).reshape(micro_count, row_count, model_width)
 
+    query_heads = slots[:, 0].reshape(n_dp, micro_count, row_count, head_count, HD)
+    grad_heads = slots[:, 1].reshape(n_dp, micro_count, row_count, head_count, HD)
     flat_enc = encoded.reshape(rows, model_width)
     key_heads = jnp.dot(flat_enc, layer[:, 1, :], preferred_element_type=jnp.float32).astype(
         jnp.bfloat16
@@ -136,10 +139,10 @@
                      preferred_element_type=jnp.float32)
     ).astype(jnp.bfloat16)
     head_terms = head_terms.reshape(micro_count, row_count, n_y, n_c, chunk_width)
-    head_terms = jnp.transpose(head_terms, (3, 2, 0, 1, 4))
     pair_sum = jnp.sum(
-        lax.all_to_all(head_terms, "tc", 0, 0, tiled=False).astype(jnp.float32), axis=0
+        lax.all_to_all(head_terms, "tc", 3, 0, tiled=False).astype(jnp.float32), axis=0
     ).astype(jnp.bfloat16)
+    pair_sum = jnp.moveaxis(pair_sum, 2, 0)
     pair_sum = jnp.where(seg > 0, pair_sum, jnp.zeros_like(pair_sum))
     quarter = row_count // n_x
     pair_sum = pair_sum.reshape(n_y, micro_count, n_x, quarter, chunk_width)

time: 241 us -> 237 us (0.983)
  the two profiles are of different devices: /device:TPU:136 before, /device:TPU:72 now
where the time goes in v6:
time: 237 us; the launch traced here: 235 us
  waiting for transfers between devices  97.2 us (41%)
  starting transfers between devices  66.8 us (28%)
  local copies, waits for them, and re-layouts  30.9 us (13%)
  matrix products  19.3 us (8%)
  blocking collectives  11.7 us (5%)
  other arithmetic  8.77 us (4%)
    ppermute x3, waiting for transfers between devices, seg_reduce(): got = lax.ppermute(sent, 'zh', [(b, 0)])  31.9 us
    all_to_all x3, waiting for transfers between devices, gather_axis(): return lax.all_to_all(spread, axis, 0, 0, tiled=False)  30.3 us
    all_to_all x1, waiting for transfers between devices, shards(): lax.all_to_all(pair_sum, ('x', 'ty'), 0, 0, tiled=False).astype(jnp.float32)  26.2 us
    all_to_all x3, starting transfers between devices, gather_axis(): return lax.all_to_all(spread, axis, 0, 0, tiled=False)  23 us
    ppermute x3, starting transfers between devices, seg_broadcast(): got = lax.ppermute(mine, 'zh', [(0, b)])  18.6 us
    ppermute x3, starting transfers between devices, seg_broadcast(): got = lax.ppermute(pieces[:, k], 'x', [(0, k)])  7.25 us
    another operation x2, local copies, waits for them, and re-layouts, shards(): lax.all_to_all(head_terms, 'tc', 3, 0, tiled=False).astype(jnp.float32)  6.35 us
    all_to_all x1, blocking collectives, shards(): lax.all_to_all(head_terms, 'tc', 3, 0, tiled=False).astype(jnp.float32)  6.3 us
  transfers between devices with their start and end apart: 17, of which 13 were waited for; matrix products, arithmetic and copies ran while one was open for 4% of the time, Pallas kernels for 0%

profile of v6, /device:TPU:72, one launch (start us, length us, event | category | flops | bytes accessed | tf_op | source)
XLA Modules:
  0.0 235.1 jit_solution(12325807846588995002)
XLA Ops:
  0.0 1.6 copy-done
  1.6 2.3 fusion.8
  4.2 1.2 broadcast_in_dim.10
  5.3 6.9 %all-to-all-start = ((bf16[4,2,2,128,256]{3,4,2,1,0:T(8,128)(2,1)}), bf16[4,2,2,128,256]{3,4,2,1,0:T(8,128)(2,1)S(1)}, u32[]{:S(2)}, u32[]{:S(2)}) async-start(bf16[4,2,2,128,256]{3,4,2,1,0:T(8,128)(2,1)} %broadcast_in_dim.10), calls=%async_computation | async-start | bytes 2097152 | tf_op jit(solution)/shard_map/all_to_all | solution.py:21
  12.3 4.7 %collective-permute-start = (bf16[2,32,256]{2,1,0:T(8,128)(2,1)S(1)}, bf16[2,32,256]{2,1,0:T(8,128)(2,1)S(1)}, u32[]{:S(2)}, u32[]{:S(2)}) collective-permute-start(bf16[2,32,256]{2,1,0:T(8,128)(2,1)S(1)} %get-tuple-element.21), channel_id=1, source_target_pairs={{0,192},{1,193},{2,194},{3,195},{4,196},{5,197},{6,198},{7,199},{8... | collective-permute-start | bytes 98312 | tf_op jit(solution)/shard_map/ppermute | solution.py:31
  17.0 1.3 collective-permute-start.1
  18.3 1.3 collective-permute-start.2
  19.6 0.3 collective-permute-done.1
  19.8 1.3 collective-permute-done.2
  21.1 15.5 %collective-permute-start.3 = (bf16[2,32,256]{2,1,0:T(8,128)(2,1)S(1)}, bf16[2,32,256]{2,1,0:T(8,128)(2,1)S(1)}, u32[]{:S(2)}, u32[]{:S(2)}) collective-permute-start(bf16[2,32,256]{2,1,0:T(8,128)(2,1)S(1)} %fusion.35), channel_id=1, source_target_pairs={{0,768},{1,769},{2,770},{3,771},{4,772},{5,773},{6,774},{7,775},{8... | collective-permute-start | bytes 98312 | tf_op jit(solution)/shard_map/ppermute | solution.py:35
  36.6 1.8 collective-permute-start.4
  38.5 1.3 collective-permute-start.5
  39.8 0.4 collective-permute-done.4
  40.2 1.1 collective-permute-done.5
  41.4 1.2 broadcast_in_dim.11
  42.7 9.7 %all-to-all-start.1 = ((bf16[32,2,32,256]{3,2,1,0:T(8,128)(2,1)}), bf16[32,2,32,256]{3,2,1,0:T(8,128)(2,1)S(1)}, u32[]{:S(2)}, u32[]{:S(2)}) async-start(bf16[32,2,32,256]{3,2,1,0:T(8,128)(2,1)} %broadcast_in_dim.11), calls=%async_computation.1 | async-start | bytes 2097152 | tf_op jit(solution)/shard_map/all_to_all | solution.py:21
  52.4 2.3 fusion.38
  54.7 24.0 %all-to-all-done.1 = bf16[32,2,32,256]{3,2,1,0:T(8,128)(2,1)S(1)} async-done(((bf16[32,2,32,256]{3,2,1,0:T(8,128)(2,1)}), bf16[32,2,32,256]{3,2,1,0:T(8,128)(2,1)S(1)}, u32[]{:S(2)}, u32[]{:S(2)}) %all-to-all-start.1) | async-done | bytes 1048608 | tf_op jit(solution)/shard_map/all_to_all | solution.py:21
  78.9 5.4 %all_to_all.39 = bf16[2,32,2,32,256]{4,3,2,1,0:T(8,128)(2,1)S(1)} all-to-all(bf16[2,32,2,32,256]{4,3,2,1,0:T(8,128)(2,1)S(1)} %broadcast_in_dim.12), channel_id=1, replica_groups=mesh['zh'=4,'x'=4,'dp'=4,'ty'=8,'tc'=2] {'tc'}, dimensions={0} | all-to-all | bytes 4194304 | tf_op jit(solution)/shard_map/all_to_all | solution.py:21
  84.4 3.5 %copy.166 = bf16[2,4,32,8,2,256]{5,4,3,2,1,0:T(2,128)(2,1)} copy(bf16[2,4,32,8,2,256]{5,2,0,3,1,4:T(8,128)(2,1)S(1)} %bitcast.147) | data formatting | bytes 4194304 | tf_op jit(solution)/shard_map/transpose | solution.py:88
  87.9 4.5 %reshape_reshape.3 = bf16[256,4096]{1,0:T(8,128)(2,1)} reshape(bf16[2,4,32,8,2,256]{5,4,3,2,1,0:T(2,128)(2,1)} %copy.166) | data formatting | bytes 4194304 | tf_op jit(solution)/shard_map/reshape;reshape | solution.py:92
  92.3 3.1 %fusion.7 = bf16[256,256]{1,0:T(8,128)(2,1)S(1)} fusion(bf16[256,4096]{1,0:T(8,128)(2,1)} %reshape_reshape.3, bf16[4096,3,256]{2,0,1:T(8,128)(2,1)} %bitcast.151), kind=kOutput, calls=%fused_computation.18 | convolution fusion | flops 536936448 | bytes 4325376 | tf_op jit(solution)/shard_map/dot_general | solution.py:93
  95.4 3.0 %fusion.6 = bf16[256,256]{1,0:T(8,128)(2,1)} fusion(bf16[256,4096]{1,0:T(8,128)(2,1)S(1)} %copy-done.5, bf16[4096,3,256]{2,0,1:T(8,128)(2,1)} %bitcast.152), kind=kOutput, calls=%fused_computation.17 | convolution fusion | flops 536936448 | bytes 4325376 | tf_op jit(solution)/shard_map/dot_general | solution.py:96
  98.6 1.7 copy.171
  100.3 0.9 reshape.58
  101.3 0.4 multiply_reduce_fusion.1
  101.7 1.9 fusion.2
  103.7 0.7 broadcast_in_dim.13
  104.4 6.5 %all-to-all-start.3 = ((f32[4,3,2,4,4,128]{5,4,3,2,1,0:T(4,128)}), f32[4,3,2,4,4,128]{5,4,3,2,1,0:T(4,128)S(1)}, u32[]{:S(2)}, u32[]{:S(2)}) async-start(f32[4,3,2,4,4,128]{5,4,3,2,1,0:T(4,128)} %broadcast_in_dim.13), calls=%async_computation.3 | async-start | bytes 393216 | tf_op jit(solution)/shard_map/all_to_all | solution.py:21
  110.9 6.3 %all-to-all-done.3 = f32[4,3,2,4,4,128]{5,4,3,2,1,0:T(4,128)S(1)} async-done(((f32[4,3,2,4,4,128]{5,4,3,2,1,0:T(4,128)}), f32[4,3,2,4,4,128]{5,4,3,2,1,0:T(4,128)S(1)}, u32[]{:S(2)}, u32[]{:S(2)}) %all-to-all-start.3) | async-done | bytes 196640 | tf_op jit(solution)/shard_map/all_to_all | solution.py:21
  117.2 3.1 %fusion.17 = (bf16[2,4,4,128,128]{3,4,2,1,0:T(8,128)(2,1)S(1)}, bf16[2,4,4,128,128]{3,4,2,1,0:T(8,128)(2,1)S(1)}) fusion(f32[2,4,4,128]{3,2,1,0:T(4,128)S(1)} %get-tuple-element.11, f32[2,4,4,128]{3,2,1,0:T(4,128)S(1)} %bitcast_reduce_fusion, f32[2,4,4,128,128]{3,4,2,1,0:T(8,128)} %copy-done.1, f32[2,4,4,128,128]{3,4,2,1,0:T(8,128)} %get-tuple-element.24, ...), kind=kLoop, calls=%fused_computation.29 | loop fusion | flops 4194304 | bytes 6340608 | tf_op jit(solution)/shard_map/convert_element_type | solution.py:120
  120.3 0.5 fusion.11
  121.0 2.4 %fusion.3 = f32[256,4096]{1,0:T(8,128)S(1)} fusion(bf16[4096,3,256]{2,0,1:T(8,128)(2,1)} %bitcast.153, bf16[32,8,2,128]{3,2,1,0:T(2,128)(2,1)S(1)} %bitcast.164), kind=kOutput, calls=%fused_computation.12 | convolution fusion | flops 536870912 | bytes 6422528 | tf_op jit(solution)/shard_map/rc,dc->rd/dot_general | solution.py:136
  123.3 0.5 fusion.9
  124.0 3.7 %fusion = bf16[256,4096]{1,0:T(8,128)(2,1)} fusion(f32[256,4096]{1,0:T(8,128)S(1)} %fusion.3, bf16[4096,3,256]{2,0,1:T(8,128)(2,1)} %bitcast.154, bf16[32,8,2,128]{3,2,1,0:T(2,128)(2,1)S(1)} %bitcast.163), kind=kOutput, calls=%fused_computation.1 | convolution fusion | flops 538968064 | bytes 8519680 | tf_op jit(solution)/shard_map/rc,dc->rd/dot_general | solution.py:138
  127.7 4.5 %broadcast_in_dim_reshape.3 = bf16[1,2,128,8,2,256]{5,4,3,2,1,0:T(2,128)(2,1)} reshape(bf16[256,4096]{1,0:T(8,128)(2,1)} %fusion) | data formatting | bytes 4194304 | tf_op jit(solution)/shard_map/broadcast_in_dim;reshape | solution.py:143
  132.2 1.9 copy.182
  134.0 6.3 %all_to_all.40 = bf16[1,2,128,8,2,256]{5,3,2,1,0,4:T(8,128)(2,1)} all-to-all(bf16[1,2,128,8,2,256]{5,3,2,1,0,4:T(8,128)(2,1)S(1)} %copy.182), channel_id=1, replica_groups=mesh['zh'=4,'x'=4,'dp'=4,'ty'=8,'tc'=2] {'tc'}, dimensions={4} | all-to-all | bytes 4194304 | tf_op jit(solution)/shard_map/all_to_all | solution.py:143
  140.3 2.3 reduce_sum.70
  142.7 1.3 copy.185
  144.0 5.1 %all-to-all-start.5 = ((bf16[32,2,32,256]{3,2,1,0:T(8,128)(2,1)}), bf16[32,2,32,256]{3,2,1,0:T(8,128)(2,1)S(1)}, u32[]{:S(2)}, u32[]{:S(2)}) async-start(bf16[32,2,32,256]{3,2,1,0:T(8,128)(2,1)} %bitcast.149), calls=%async_computation.5 | async-start | bytes 2097152 | tf_op jit(solution)/shard_map/all_to_all | solution.py:151
  149.1 1.5 convolution_bitcast_fusion
  150.6 1.1 copy.193
  151.7 26.2 %all-to-all-done.5 = bf16[32,2,32,256]{3,2,1,0:T(8,128)(2,1)S(1)} async-done(((bf16[32,2,32,256]{3,2,1,0:T(8,128)(2,1)}), bf16[32,2,32,256]{3,2,1,0:T(8,128)(2,1)S(1)}, u32[]{:S(2)}, u32[]{:S(2)}) %all-to-all-start.5) | async-done | bytes 1048608 | tf_op jit(solution)/shard_map/all_to_all | solution.py:151
  177.8 1.0 copy-done.3
  178.8 5.0 %all-to-all-start.6 = ((f32[4,2,128,256]{2,3,1,0:T(8,128)}), f32[4,2,128,256]{2,3,1,0:T(8,128)S(1)}, u32[]{:S(2)}, u32[]{:S(2)}) async-start(f32[4,2,128,256]{2,3,1,0:T(8,128)} %bitcast.42), calls=%async_computation.6 | async-start | bytes 2097152 | tf_op jit(solution)/shard_map/all_to_all | solution.py:126
  183.9 1.4 convert_reduce_fusion
  185.3 1.3 collective-permute-start.6
  186.6 1.3 collective-permute-start.7
  187.9 1.3 collective-permute-start.8
  189.2 13.1 %collective-permute-done.6 = bf16[2,32,256]{2,1,0:T(8,128)(2,1)S(1)} collective-permute-done((bf16[2,32,256]{2,1,0:T(8,128)(2,1)S(1)}, bf16[2,32,256]{2,1,0:T(8,128)(2,1)S(1)}, u32[]{:S(2)}, u32[]{:S(2)}) %collective-permute-start.6) | collective-permute-done | bytes 32800 | tf_op jit(solution)/shard_map/ppermute | solution.py:45
  202.3 4.5 %collective-permute-done.7 = bf16[2,32,256]{2,1,0:T(8,128)(2,1)S(1)} collective-permute-done((bf16[2,32,256]{2,1,0:T(8,128)(2,1)S(1)}, bf16[2,32,256]{2,1,0:T(8,128)(2,1)S(1)}, u32[]{:S(2)}, u32[]{:S(2)}) %collective-permute-start.7) | collective-permute-done | bytes 32800 | tf_op jit(solution)/shard_map/ppermute | solution.py:45
  206.8 14.3 %collective-permute-done.8 = bf16[2,32,256]{2,1,0:T(8,128)(2,1)S(1)} collective-permute-done((bf16[2,32,256]{2,1,0:T(8,128)(2,1)S(1)}, bf16[2,32,256]{2,1,0:T(8,128)(2,1)S(1)}, u32[]{:S(2)}, u32[]{:S(2)}) %collective-permute-start.8) | collective-permute-done | bytes 32800 | tf_op jit(solution)/shard_map/ppermute | solution.py:45
  221.1 1.3 collective-permute-start.10
  222.4 0.8 copy.189
  223.2 1.3 collective-permute-start.9
  224.5 1.3 collective-permute-start.11
  225.8 2.7 %collective-permute-done.10 = bf16[2,32,256]{2,1,0:T(8,128)(2,1)S(1)} collective-permute-done((bf16[2,32,256]{2,1,0:T(8,128)(2,1)S(1)}, bf16[2,32,256]{2,1,0:T(8,128)(2,1)S(1)}, u32[]{:S(2)}, u32[]{:S(2)}) %collective-permute-start.10) | collective-permute-done | bytes 32800 | tf_op jit(solution)/shard_map/ppermute | solution.py:51
  228.5 0.5 collective-permute-done.9
  229.0 2.5 %collective-permute-done.11 = bf16[2,32,256]{2,1,0:T(8,128)(2,1)S(1)} collective-permute-done((bf16[2,32,256]{2,1,0:T(8,128)(2,1)S(1)}, bf16[2,32,256]{2,1,0:T(8,128)(2,1)S(1)}, u32[]{:S(2)}, u32[]{:S(2)}) %collective-permute-start.11) | collective-permute-done | bytes 32800 | tf_op jit(solution)/shard_map/ppermute | solution.py:51
  231.5 0.7 pad_maximum_fusion.1
  232.3 1.1 copy.190
  233.4 1.0 fusion.19
  234.4 0.8 copy.194
  (45 shorter events, 1.3 us)
Async XLA Ops:
  0.0 1.6 copy-start
  1.6 2.3 copy-start.8
  5.3 36.0 %all-to-all-start = ((bf16[4,2,2,128,256]{3,4,2,1,0:T(8,128)(2,1)}), bf16[4,2,2,128,256]{3,4,2,1,0:T(8,128)(2,1)S(1)}, u32[]{:S(2)}, u32[]{:S(2)}) async-start(bf16[4,2,2,128,256]{3,4,2,1,0:T(8,128)(2,1)} %broadcast_in_dim.10), calls=%async_computation | async-start | bytes 2097152 | tf_op jit(solution)/shard_map/all_to_all | solution.py:21
  12.3 7.3 %collective-permute-start = (bf16[2,32,256]{2,1,0:T(8,128)(2,1)S(1)}, bf16[2,32,256]{2,1,0:T(8,128)(2,1)S(1)}, u32[]{:S(2)}, u32[]{:S(2)}) collective-permute-start(bf16[2,32,256]{2,1,0:T(8,128)(2,1)S(1)} %get-tuple-element.21), channel_id=1, source_target_pairs={{0,192},{1,193},{2,194},{3,195},{4,196},{5,197},{6,198},{7,199},{8... | collective-permute-start | bytes 98312 | tf_op jit(solution)/shard_map/ppermute | solution.py:31
  17.0 2.9 %collective-permute-start.1 = (bf16[2,32,256]{2,1,0:T(8,128)(2,1)S(1)}, bf16[2,32,256]{2,1,0:T(8,128)(2,1)S(1)}, u32[]{:S(2)}, u32[]{:S(2)}) collective-permute-start(bf16[2,32,256]{2,1,0:T(8,128)(2,1)S(1)} %get-tuple-element.20), channel_id=1, source_target_pairs={{0,128},{1,129},{2,130},{3,131},{4,132},{5,133},{6,134},{7,135},{8... | collective-permute-start | bytes 98312 | tf_op jit(solution)/shard_map/ppermute | solution.py:31
  18.3 2.9 %collective-permute-start.2 = (bf16[2,32,256]{2,1,0:T(8,128)(2,1)S(1)}, bf16[2,32,256]{2,1,0:T(8,128)(2,1)S(1)}, u32[]{:S(2)}, u32[]{:S(2)}) collective-permute-start(bf16[2,32,256]{2,1,0:T(8,128)(2,1)S(1)} %get-tuple-element.19), channel_id=1, source_target_pairs={{0,64},{1,65},{2,66},{3,67},{4,68},{5,69},{6,70},{7,71},{8,72},{9,... | collective-permute-start | bytes 98312 | tf_op jit(solution)/shard_map/ppermute | solution.py:31
  21.1 18.7 %collective-permute-start.3 = (bf16[2,32,256]{2,1,0:T(8,128)(2,1)S(1)}, bf16[2,32,256]{2,1,0:T(8,128)(2,1)S(1)}, u32[]{:S(2)}, u32[]{:S(2)}) collective-permute-start(bf16[2,32,256]{2,1,0:T(8,128)(2,1)S(1)} %fusion.35), channel_id=1, source_target_pairs={{0,768},{1,769},{2,770},{3,771},{4,772},{5,773},{6,774},{7,775},{8... | collective-permute-start | bytes 98312 | tf_op jit(solution)/shard_map/ppermute | solution.py:35
  36.6 3.6 %collective-permute-start.4 = (bf16[2,32,256]{2,1,0:T(8,128)(2,1)S(1)}, bf16[2,32,256]{2,1,0:T(8,128)(2,1)S(1)}, u32[]{:S(2)}, u32[]{:S(2)}) collective-permute-start(bf16[2,32,256]{2,1,0:T(8,128)(2,1)S(1)} %fusion.35), channel_id=1, source_target_pairs={{0,512},{1,513},{2,514},{3,515},{4,516},{5,517},{6,518},{7,519},{8... | collective-permute-start | bytes 98312 | tf_op jit(solution)/shard_map/ppermute | solution.py:35
  38.5 2.9 %collective-permute-start.5 = (bf16[2,32,256]{2,1,0:T(8,128)(2,1)S(1)}, bf16[2,32,256]{2,1,0:T(8,128)(2,1)S(1)}, u32[]{:S(2)}, u32[]{:S(2)}) collective-permute-start(bf16[2,32,256]{2,1,0:T(8,128)(2,1)S(1)} %fusion.35), channel_id=1, source_target_pairs={{0,256},{1,257},{2,258},{3,259},{4,260},{5,261},{6,262},{7,263},{8... | collective-permute-start | bytes 98312 | tf_op jit(solution)/shard_map/ppermute | solution.py:35
  41.4 1.3 copy-start.2
  42.7 36.0 %all-to-all-start.1 = ((bf16[32,2,32,256]{3,2,1,0:T(8,128)(2,1)}), bf16[32,2,32,256]{3,2,1,0:T(8,128)(2,1)S(1)}, u32[]{:S(2)}, u32[]{:S(2)}) async-start(bf16[32,2,32,256]{3,2,1,0:T(8,128)(2,1)} %broadcast_in_dim.11), calls=%async_computation.1 | async-start | bytes 2097152 | tf_op jit(solution)/shard_map/all_to_all | solution.py:21
  92.3 3.1 %copy-start.5 = (bf16[256,4096]{1,0:T(8,128)(2,1)S(1)}, bf16[256,4096]{1,0:T(8,128)(2,1)}, u32[]{:S(2)}) copy-start(bf16[256,4096]{1,0:T(8,128)(2,1)} %reshape_reshape.3) | copy-start | bytes 6291460
  95.4 5.8 %copy-start.7 = (bf16[4,1,2,128,256]{3,4,2,0,1:T(8,128)(2,1)S(1)}, bf16[4,1,2,128,256]{3,4,2,0,1:T(8,128)(2,1)}, u32[]{:S(2)}) copy-start(bf16[4,1,2,128,256]{3,4,2,0,1:T(8,128)(2,1)} %get-tuple-element.16) | copy-start | bytes 1572868
  98.5 3.2 %copy-start.6 = (bf16[4,1,2,128,256]{3,4,2,0,1:T(8,128)(2,1)S(1)}, bf16[4,1,2,128,256]{3,4,2,0,1:T(8,128)(2,1)}, u32[]{:S(2)}) copy-start(bf16[4,1,2,128,256]{3,4,2,0,1:T(8,128)(2,1)} %get-tuple-element.15) | copy-start | bytes 1572868
  101.7 2.0 copy-start.1
  104.4 12.7 %all-to-all-start.3 = ((f32[4,3,2,4,4,128]{5,4,3,2,1,0:T(4,128)}), f32[4,3,2,4,4,128]{5,4,3,2,1,0:T(4,128)S(1)}, u32[]{:S(2)}, u32[]{:S(2)}) async-start(f32[4,3,2,4,4,128]{5,4,3,2,1,0:T(4,128)} %broadcast_in_dim.13), calls=%async_computation.3 | async-start | bytes 393216 | tf_op jit(solution)/shard_map/all_to_all | solution.py:21
  120.3 3.0 %copy-start.4 = (bf16[2,4,4,128,128]{3,4,2,1,0:T(8,128)(2,1)}, bf16[2,4,4,128,128]{3,4,2,1,0:T(8,128)(2,1)S(1)}, u32[]{:S(2)}) copy-start(bf16[2,4,4,128,128]{3,4,2,1,0:T(8,128)(2,1)S(1)} %get-tuple-element.13) | copy-start | bytes 3145732
  144.0 33.9 %all-to-all-start.5 = ((bf16[32,2,32,256]{3,2,1,0:T(8,128)(2,1)}), bf16[32,2,32,256]{3,2,1,0:T(8,128)(2,1)S(1)}, u32[]{:S(2)}, u32[]{:S(2)}) async-start(bf16[32,2,32,256]{3,2,1,0:T(8,128)(2,1)} %bitcast.149), calls=%async_computation.5 | async-start | bytes 2097152 | tf_op jit(solution)/shard_map/all_to_all | solution.py:151
  151.7 70.8 %copy-start.9 = (bf16[1,2,128,256]{3,2,1,0:T(8,128)(2,1)S(1)}, bf16[1,2,128,256]{3,2,1,0:T(8,128)(2,1)}, u32[]{:S(2)}) copy-start(bf16[1,2,128,256]{3,2,1,0:T(8,128)(2,1)} %param.5) | copy-start | bytes 393220
  177.8 1.0 copy-start.3
  178.8 54.5 %all-to-all-start.6 = ((f32[4,2,128,256]{2,3,1,0:T(8,128)}), f32[4,2,128,256]{2,3,1,0:T(8,128)S(1)}, u32[]{:S(2)}, u32[]{:S(2)}) async-start(f32[4,2,128,256]{2,3,1,0:T(8,128)} %bitcast.42), calls=%async_computation.6 | async-start | bytes 2097152 | tf_op jit(solution)/shard_map/all_to_all | solution.py:126
  185.3 17.0 %collective-permute-start.6 = (bf16[2,32,256]{2,1,0:T(8,128)(2,1)S(1)}, bf16[2,32,256]{2,1,0:T(8,128)(2,1)S(1)}, u32[]{:S(2)}, u32[]{:S(2)}) collective-permute-start(bf16[2,32,256]{2,1,0:T(8,128)(2,1)S(1)} %convert_element_type.85), channel_id=1, source_target_pairs={{256,0},{257,1},{258,2},{259,3},{260,4},{261,5},{262,6},{263,7},{2... | collective-permute-start | bytes 98312 | tf_op jit(solution)/shard_map/ppermute | solution.py:45
  186.6 20.3 %collective-permute-start.7 = (bf16[2,32,256]{2,1,0:T(8,128)(2,1)S(1)}, bf16[2,32,256]{2,1,0:T(8,128)(2,1)S(1)}, u32[]{:S(2)}, u32[]{:S(2)}) collective-permute-start(bf16[2,32,256]{2,1,0:T(8,128)(2,1)S(1)} %convert_element_type.85), channel_id=1, source_target_pairs={{512,0},{513,1},{514,2},{515,3},{516,4},{517,5},{518,6},{519,7},{5... | collective-permute-start | bytes 98312 | tf_op jit(solution)/shard_map/ppermute | solution.py:45
  187.9 33.2 %collective-permute-start.8 = (bf16[2,32,256]{2,1,0:T(8,128)(2,1)S(1)}, bf16[2,32,256]{2,1,0:T(8,128)(2,1)S(1)}, u32[]{:S(2)}, u32[]{:S(2)}) collective-permute-start(bf16[2,32,256]{2,1,0:T(8,128)(2,1)S(1)} %convert_element_type.85), channel_id=1, source_target_pairs={{768,0},{769,1},{770,2},{771,3},{772,4},{773,5},{774,6},{775,7},{7... | collective-permute-start | bytes 98312 | tf_op jit(solution)/shard_map/ppermute | solution.py:45
  221.1 7.4 %collective-permute-start.10 = (bf16[2,32,256]{2,1,0:T(8,128)(2,1)S(1)}, bf16[2,32,256]{2,1,0:T(8,128)(2,1)S(1)}, u32[]{:S(2)}, u32[]{:S(2)}) collective-permute-start(bf16[2,32,256]{2,1,0:T(8,128)(2,1)S(1)} %get-tuple-element.18), channel_id=1, source_target_pairs={{128,0},{129,1},{130,2},{131,3},{132,4},{133,5},{134,6},{135,7},{1... | collective-permute-start | bytes 98312 | tf_op jit(solution)/shard_map/ppermute | solution.py:51
  223.2 5.8 %collective-permute-start.9 = (bf16[2,32,256]{2,1,0:T(8,128)(2,1)S(1)}, bf16[2,32,256]{2,1,0:T(8,128)(2,1)S(1)}, u32[]{:S(2)}, u32[]{:S(2)}) collective-permute-start(bf16[2,32,256]{2,1,0:T(8,128)(2,1)S(1)} %get-tuple-element.18), channel_id=1, source_target_pairs={{64,0},{65,1},{66,2},{67,3},{68,4},{69,5},{70,6},{71,7},{72,8},{73... | collective-permute-start | bytes 98312 | tf_op jit(solution)/shard_map/ppermute | solution.py:51
  224.5 7.0 %collective-permute-start.11 = (bf16[2,32,256]{2,1,0:T(8,128)(2,1)S(1)}, bf16[2,32,256]{2,1,0:T(8,128)(2,1)S(1)}, u32[]{:S(2)}, u32[]{:S(2)}) collective-permute-start(bf16[2,32,256]{2,1,0:T(8,128)(2,1)S(1)} %get-tuple-element.18), channel_id=1, source_target_pairs={{192,0},{193,1},{194,2},{195,3},{196,4},{197,5},{198,6},{199,7},{2... | collective-permute-start | bytes 98312 | tf_op jit(solution)/shard_map/ppermute | solution.py:51

commit v7 on v6

v7 whole, which is shorter than its diff:
```python
import jax
import jax.numpy as jnp
from jax import lax
from jax.sharding import Mesh, PartitionSpec as P

HD = 64
X_SIZE = 4
SEG = ("zh", "x")
TEN = ("ty", "tc")


def hi_rounds(n_hi):
    rounds = [[(0, 1)] + ([(0, n_hi - 1)] if n_hi > 2 else [])]
    if n_hi > 3:
        rounds.append([(1, 2)])
    return rounds


def gather_axis(value, axis, n):
    spread = jnp.broadcast_to(value[None], (n,) + value.shape)
    return lax.all_to_all(spread, axis, 0, 0, tiled=False)


def seg_broadcast(value, n_hi, n_x):
    x = lax.axis_index("x")
    zh = lax.axis_index("zh")
    quarter = value.shape[1] // n_x
    pieces = value.reshape(value.shape[0], n_x, quarter, value.shape[2])
    mine = pieces[:, 0]
    for k in range(1, n_x):
        got = lax.ppermute(pieces[:, k], "x", [(0, k)])
        mine = jnp.where(x == k, got, mine)
    out = mine
    for b in range(1, n_hi):
        got = lax.ppermute(mine, "zh", [(0, b)])
        out = jnp.where(zh == b, got, out)
    return out


def seg_reduce(mine, n_hi, n_x):
    zh = lax.axis_index("zh")
    sent = mine.astype(jnp.bfloat16)
    acc = mine
    for b in range(1, n_hi):
        got = lax.ppermute(sent, "zh", [(b, 0)])
        acc = acc + got.astype(jnp.float32)
    acc = jnp.where(zh == 0, acc, mine)
    parts = [acc]
    sent = acc.astype(jnp.bfloat16)
    for k in range(1, n_x):
        parts.append(lax.ppermute(sent, "x", [(k, 0)]).astype(jnp.float32))
    stacked = jnp.stack(parts, axis=1)
    return stacked.reshape(stacked.shape[0], -1, stacked.shape[-1])


def shards(inbound, weights, cotangent):
    n_hi = lax.axis_size("zh")
    n_x = lax.axis_size("x")
    n_dp = lax.axis_size("dp")
    n_y = lax.axis_size("ty")
    n_c = lax.axis_size("tc")
    n_tensor = n_y * n_c
    seg = lax.axis_index("zh") * n_x + lax.axis_index("x")
    core = lax.axis_index("tc")
    tix = lax.axis_index("ty") * n_c + core

    states = inbound[0]
    micro_count, row_count, model_width = states.shape
    layer = weights[0]
    feat_width = layer.shape[2]
    head_count = feat_width // HD
    scale = HD ** (-0.5)
    rows = micro_count * row_count
    chunk_width = model_width // n_tensor

    query = jnp.dot(
        states.reshape(rows, model_width), layer[:, 0, :], preferred_element_type=jnp.float32
    ).astype(jnp.bfloat16)
    query = query.reshape(micro_count, row_count, feat_width)
    slots = gather_axis(jnp.stack([query, cotangent[0]]), "dp", n_dp)

    chunk = lax.dynamic_slice_in_dim(states, tix * chunk_width, chunk_width, axis=2)
    piece = seg_broadcast(chunk, n_hi, n_x)
    slots, piece = lax.optimization_barrier((slots, piece))
    def chain(piece, slots, upstream):
        micro_count = 1
        rows = row_count
        own = gather_axis(piece, ("x", "ty"), n_x * n_y)
        both = gather_axis(own, "tc", n_c)
        both = both.reshape(n_c, n_x, n_y, micro_count, row_count // n_x, chunk_width)
        encoded = jnp.transpose(both, (3, 1, 4, 2, 0, 5)).reshape(micro_count, row_count, model_width)

        query_heads = slots[:, 0].reshape(n_dp, micro_count, row_count, head_count, HD)
        grad_heads = slots[:, 1].reshape(n_dp, micro_count, row_count, head_count, HD)
        flat_enc = encoded.reshape(rows, model_width)
        key_heads = jnp.dot(flat_enc, layer[:, 1, :], preferred_element_type=jnp.float32).astype(
            jnp.bfloat16
        ).reshape(micro_count, row_count, head_count, HD)
        value_heads = jnp.dot(flat_enc, layer[:, 2, :], preferred_element_type=jnp.float32).astype(
            jnp.bfloat16
        ).reshape(micro_count, row_count, head_count, HD)

        scores = (
            jnp.einsum("jmqhe,mkhe->mhjqk", query_heads, key_heads, preferred_element_type=jnp.float32)
            * scale
        )
        prob_grad = jnp.einsum(
            "jmqhe,mkhe->mhjqk", grad_heads, value_heads, preferred_element_type=jnp.float32
        )
        local_peak = jnp.max(scores, axis=-1)
        local_exp = jnp.exp(scores - local_peak[..., None])
        local_sum = jnp.sum(local_exp, axis=-1)
        local_delta = jnp.sum(local_exp * prob_grad, axis=-1)
        stats = jnp.stack([local_peak, local_sum, local_delta])
        all_stats = gather_axis(stats, "dp", n_dp)
        peaks = all_stats[:, 0]
        peak = jnp.max(peaks, axis=0)
        weight = jnp.exp(peaks - peak[None])
        total = jnp.sum(all_stats[:, 1] * weight, axis=0)
        row_delta = jnp.sum(all_stats[:, 2] * weight, axis=0) / total

        attend_prob = jnp.exp(scores - peak[..., None]) / total[..., None]
        prob_rounded = attend_prob.astype(jnp.bfloat16)
        score_grad = (attend_prob * (prob_grad - row_delta[..., None]) * scale).astype(jnp.bfloat16)

        context_part = jnp.einsum(
            "mhjqk,mkhe->jmqhe", prob_rounded, value_heads, preferred_element_type=jnp.float32
        ).reshape(n_dp, micro_count, row_count, feat_width)
        context = jnp.sum(lax.all_to_all(context_part, "dp", 0, 0, tiled=False), axis=0)
        context = context.astype(jnp.bfloat16)

        key_grad = jnp.einsum(
            "mhjqk,jmqhe->mkhe", score_grad, query_heads, preferred_element_type=jnp.float32
        ).astype(jnp.bfloat16)
        value_grad = jnp.einsum(
            "mhjqk,jmqhe->mkhe", prob_rounded, grad_heads, preferred_element_type=jnp.float32
        ).astype(jnp.bfloat16)
        head_terms = (
            jnp.einsum("rc,dc->rd", key_grad.reshape(rows, feat_width), layer[:, 1, :],
                       preferred_element_type=jnp.float32)
            + jnp.einsum("rc,dc->rd", value_grad.reshape(rows, feat_width), layer[:, 2, :],
                         preferred_element_type=jnp.float32)
        ).astype(jnp.bfloat16)
        head_terms = head_terms.reshape(micro_count, row_count, n_y, n_c, chunk_width)
        pair_sum = jnp.sum(
            lax.all_to_all(head_terms, "tc", 3, 0, tiled=False).astype(jnp.float32), axis=0
        ).astype(jnp.bfloat16)
        pair_sum = jnp.moveaxis(pair_sum, 2, 0)
        pair_sum = jnp.where(seg > 0, pair_sum, jnp.zeros_like(pair_sum))
        quarter = row_count // n_x
        pair_sum = pair_sum.reshape(n_y, micro_count, n_x, quarter, chunk_width)
        pair_sum = jnp.transpose(pair_sum, (2, 0, 1, 3, 4)).reshape(n_x * n_y, micro_count, quarter, chunk_width)
        heads_total = jnp.sum(
            lax.all_to_all(pair_sum, ("x", "ty"), 0, 0, tiled=False).astype(jnp.float32), axis=0
        )
        sections = seg_reduce(heads_total, n_hi, n_x)
        encoder_grad = (sections + upstream.astype(jnp.float32)).astype(jnp.bfloat16)
        return jnp.where(seg == 0, encoder_grad, context)

    outs = [
        chain(piece[m:m + 1], slots[:, :, m:m + 1], cotangent[0][m:m + 1])
        for m in range(micro_count)
    ]
    return jnp.concatenate(outs, axis=0)[None]


def solution(mesh):
    n_seg, n_dp, n_tensor = (mesh.shape[a] for a in ("segment", "dp", "tensor"))
    sub = Mesh(
        mesh.devices.reshape(n_seg // X_SIZE, X_SIZE, n_dp, n_tensor // 2, 2),
        SEG + ("dp",) + TEN,
    )
    placed = (
        P(SEG, None, "dp", None),
        P(SEG, None, None, TEN),
        P(SEG, None, "dp", TEN),
    )
    return jax.shard_map(
        shards,
        mesh=sub,
        in_specs=placed,
        out_specs=P(SEG, None, "dp", TEN),
        check_vma=False,
    )
```

time: 237 us -> 275 us (1.16)
  the two profiles are of different devices: /device:TPU:72 before, /device:TPU:10 now
where the time goes in v7:
time: 275 us; the launch traced here: 272 us
  starting transfers between devices  83.2 us (30%)
  waiting for transfers between devices  67.6 us (25%)
  blocking collectives  43.3 us (16%)
  matrix products  30.7 us (11%)
  local copies, waits for them, and re-layouts  27.7 us (10%)
  other arithmetic  19.1 us (7%)
    all_to_all x3, blocking collectives, gather_axis(): return lax.all_to_all(spread, axis, 0, 0, tiled=False)  33.3 us
    all_to_all x2, waiting for transfers between devices, chain(): lax.all_to_all(pair_sum, ('x', 'ty'), 0, 0, tiled=False).astype(jnp.float32)  29.4 us
    all_to_all x4, starting transfers between devices, gather_axis(): return lax.all_to_all(spread, axis, 0, 0, tiled=False)  23.2 us
    ppermute x3, starting transfers between devices, seg_broadcast(): got = lax.ppermute(mine, 'zh', [(0, b)])  18.6 us
    all_to_all x2, starting transfers between devices, chain(): lax.all_to_all(pair_sum, ('x', 'ty'), 0, 0, tiled=False).astype(jnp.float32)  11.6 us
    all_to_all x4, waiting for transfers between devices, gather_axis(): return lax.all_to_all(spread, axis, 0, 0, tiled=False)  11.1 us
    all_to_all x2, blocking collectives, chain(): lax.all_to_all(head_terms, 'tc', 3, 0, tiled=False).astype(jnp.float32)  9.97 us
    all_to_all x2, starting transfers between devices, chain(): lax.all_to_all(context_part, 'dp', 0, 0, tiled=False)  9.77 us
  transfers between devices with their start and end apart: 26, of which 12 were waited for; matrix products, arithmetic and copies ran while one was open for 11% of the time, Pallas kernels for 0%

profile of v7, /device:TPU:10, one launch (start us, length us, event | category | flops | bytes accessed | tf_op | source)
XLA Modules:
  0.0 272.4 jit_solution(14829139439442146184)
XLA Ops:
  0.0 1.6 copy-done
  1.6 2.3 fusion.9
  4.2 1.2 broadcast_in_dim.28
  5.3 7.3 %all-to-all-start = ((bf16[4,2,2,128,256]{3,4,2,1,0:T(8,128)(2,1)}), bf16[4,2,2,128,256]{3,4,2,1,0:T(8,128)(2,1)S(1)}, u32[]{:S(2)}, u32[]{:S(2)}) async-start(bf16[4,2,2,128,256]{3,4,2,1,0:T(8,128)(2,1)} %broadcast_in_dim.28), calls=%async_computation | async-start | bytes 2097152 | tf_op jit(solution)/shard_map/all_to_all | solution.py:21
  14.0 1.3 collective-permute-start.2
  15.3 7.0 %collective-permute-done.2 = bf16[2,32,256]{2,1,0:T(8,128)(2,1)S(1)} collective-permute-done((bf16[2,32,256]{2,1,0:T(8,128)(2,1)S(1)}, bf16[2,32,256]{2,1,0:T(8,128)(2,1)S(1)}, u32[]{:S(2)}, u32[]{:S(2)}) %collective-permute-start.2) | collective-permute-done | bytes 32800 | tf_op jit(solution)/shard_map/ppermute | solution.py:31
  22.3 15.5 %collective-permute-start.3 = (bf16[2,32,256]{2,1,0:T(8,128)(2,1)S(1)}, bf16[2,32,256]{2,1,0:T(8,128)(2,1)S(1)}, u32[]{:S(2)}, u32[]{:S(2)}) collective-permute-start(bf16[2,32,256]{2,1,0:T(8,128)(2,1)S(1)} %fusion.46), channel_id=1, source_target_pairs={{0,768},{1,769},{2,770},{3,771},{4,772},{5,773},{6,774},{7,775},{8... | collective-permute-start | bytes 98312 | tf_op jit(solution)/shard_map/ppermute | solution.py:35
  37.8 1.8 collective-permute-start.4
  39.7 1.3 collective-permute-start.5
  41.2 1.3 collective-permute-done.5
  42.6 23.4 %all_to_all.73 = bf16[32,1,32,256]{3,2,1,0:T(8,128)(2,1)S(1)} all-to-all(bf16[32,1,32,256]{3,2,1,0:T(8,128)(2,1)S(1)} %broadcast_in_dim.30), channel_id=1, replica_groups=mesh['zh'=4,'x'=4,'dp'=4,'ty'=8,'tc'=2] {'x','ty'}, dimensions={0} | all-to-all | bytes 1048576 | tf_op jit(solution)/shard_map/all_to_all | solution.py:21
  66.2 5.4 %all_to_all.74 = bf16[2,32,1,32,256]{4,3,1,2,0:T(8,128)(2,1)} all-to-all(bf16[2,32,1,32,256]{4,3,1,2,0:T(8,128)(2,1)S(1)} %broadcast_in_dim.32), channel_id=1, replica_groups=mesh['zh'=4,'x'=4,'dp'=4,'ty'=8,'tc'=2] {'tc'}, dimensions={0} | all-to-all | bytes 2097152 | tf_op jit(solution)/shard_map/all_to_all | solution.py:21
  72.4 5.8 %all-to-all-start.7 = ((bf16[32,1,32,256]{3,2,1,0:T(8,128)(2,1)}), bf16[32,1,32,256]{3,2,1,0:T(8,128)(2,1)}, u32[]{:S(2)}, u32[]{:S(2)}) async-start(bf16[32,1,32,256]{3,2,1,0:T(8,128)(2,1)} %broadcast_in_dim.36), calls=%async_computation.7 | async-start | bytes 1048576 | tf_op jit(solution)/shard_map/all_to_all | solution.py:21
  79.7 1.1 copy.227
  80.8 1.6 reshape_reshape.6
  82.4 2.4 fusion.12
  84.8 2.7 fusion.10
  87.5 7.8 %all-to-all-done.7 = bf16[32,1,32,256]{3,2,1,0:T(8,128)(2,1)} async-done(((bf16[32,1,32,256]{3,2,1,0:T(8,128)(2,1)}), bf16[32,1,32,256]{3,2,1,0:T(8,128)(2,1)}, u32[]{:S(2)}, u32[]{:S(2)}) %all-to-all-start.7) | async-done | bytes 524320 | tf_op jit(solution)/shard_map/all_to_all | solution.py:21
  95.3 1.2 broadcast_in_dim.38
  96.5 4.6 %all_to_all.75 = bf16[2,32,1,32,256]{4,3,1,2,0:T(8,128)(2,1)S(1)} all-to-all(bf16[2,32,1,32,256]{4,3,1,2,0:T(8,128)(2,1)S(1)} %broadcast_in_dim.38), channel_id=1, replica_groups=mesh['zh'=4,'x'=4,'dp'=4,'ty'=8,'tc'=2] {'tc'}, dimensions={0} | all-to-all | bytes 2097152 | tf_op jit(solution)/shard_map/all_to_all | solution.py:21
  102.1 1.6 reshape_reshape.7
  103.7 2.4 fusion.13
  106.2 2.1 fusion.11
  109.9 1.4 fusion.18
  111.9 6.1 %all-to-all-start.3 = ((f32[4,3,1,4,4,128]{5,4,3,2,1,0:T(4,128)}), f32[4,3,1,4,4,128]{5,4,3,2,1,0:T(4,128)}, u32[]{:S(2)}, u32[]{:S(2)}) async-start(f32[4,3,1,4,4,128]{5,4,3,2,1,0:T(4,128)} %broadcast_in_dim.34), calls=%async_computation.3 | async-start | bytes 196608 | tf_op jit(solution)/shard_map/all_to_all | solution.py:21
  118.9 1.3 fusion.59
  120.2 1.3 fusion.19
  122.1 1.8 all-to-all-done.3
  125.7 2.0 fusion.24
  128.5 2.4 fusion.5
  131.0 3.5 %fusion = bf16[128,4096]{1,0:T(8,128)(2,1)} fusion(f32[128,4096]{1,0:T(8,128)S(1)} %fusion.5, bf16[128,256]{0,1:T(8,128)(2,1)S(1)} %bitcast.343, bf16[4096,3,256]{2,0,1:T(8,128)(2,1)} %bitcast.311), kind=kOutput, calls=%fused_computation.2 | convolution fusion | flops 269484032 | bytes 5308416 | tf_op jit(solution)/shard_map/rc,dc->rd/dot_general | solution.py:141
  134.4 2.6 broadcast_in_dim_reshape.6
  137.0 1.4 copy.237
  138.4 5.4 %all_to_all.76 = bf16[1,1,128,8,2,256]{5,3,2,1,0,4:T(8,128)(2,1)} all-to-all(bf16[1,1,128,8,2,256]{5,3,2,1,0,4:T(8,128)(2,1)S(1)} %copy.237), channel_id=1, replica_groups=mesh['zh'=4,'x'=4,'dp'=4,'ty'=8,'tc'=2] {'tc'}, dimensions={4} | all-to-all | bytes 2097152 | tf_op jit(solution)/shard_map/all_to_all | solution.py:146
  144.5 4.1 %all-to-all-start.9 = ((f32[4,3,1,4,4,128]{5,4,3,2,1,0:T(4,128)}), f32[4,3,1,4,4,128]{5,4,3,2,1,0:T(4,128)}, u32[]{:S(2)}, u32[]{:S(2)}) async-start(f32[4,3,1,4,4,128]{5,4,3,2,1,0:T(4,128)} %broadcast_in_dim.79), calls=%async_computation.9 | async-start | bytes 196608 | tf_op jit(solution)/shard_map/all_to_all | solution.py:21
  148.6 2.3 reduce_sum.140
  152.9 1.5 all-to-all-done.9
  156.1 1.7 fusion.25
  158.6 2.4 fusion.3
  161.0 3.4 %fusion.1 = bf16[128,4096]{1,0:T(8,128)(2,1)} fusion(f32[128,4096]{1,0:T(8,128)S(1)} %fusion.3, bf16[128,256]{0,1:T(8,128)(2,1)S(1)} %bitcast.344, bf16[4096,3,256]{2,0,1:T(8,128)(2,1)} %bitcast.313), kind=kOutput, calls=%fused_computation.3 | convolution fusion | flops 269484032 | bytes 5308416 | tf_op jit(solution)/shard_map/rc,dc->rd/dot_general | solution.py:141
  164.5 1.8 broadcast_in_dim_reshape.7
  166.5 4.6 %all_to_all.77 = bf16[1,1,128,8,2,256]{5,3,2,1,0,4:T(8,128)(2,1)S(1)} all-to-all(bf16[1,1,128,8,2,256]{5,3,2,1,0,4:T(8,128)(2,1)S(1)} %copy.259), channel_id=1, replica_groups=mesh['zh'=4,'x'=4,'dp'=4,'ty'=8,'tc'=2] {'tc'}, dimensions={4} | all-to-all | bytes 2097152 | tf_op jit(solution)/shard_map/all_to_all | solution.py:146
  171.0 5.8 %all-to-all-start.5 = ((bf16[32,1,32,256]{3,2,1,0:T(8,128)(2,1)}), bf16[32,1,32,256]{3,2,1,0:T(8,128)(2,1)}, u32[]{:S(2)}, u32[]{:S(2)}) async-start(bf16[32,1,32,256]{3,2,1,0:T(8,128)(2,1)} %bitcast.317), calls=%async_computation.5 | async-start | bytes 1048576 | tf_op jit(solution)/shard_map/all_to_all | solution.py:154
  176.8 1.1 reduce_sum.148
  177.9 1.1 select_bitcast_fusion
  180.0 13.9 %all-to-all-done.5 = bf16[32,1,32,256]{3,2,1,0:T(8,128)(2,1)} async-done(((bf16[32,1,32,256]{3,2,1,0:T(8,128)(2,1)}), bf16[32,1,32,256]{3,2,1,0:T(8,128)(2,1)}, u32[]{:S(2)}, u32[]{:S(2)}) %all-to-all-start.5) | async-done | bytes 524320 | tf_op jit(solution)/shard_map/all_to_all | solution.py:154
  193.9 5.8 %all-to-all-start.11 = ((bf16[32,1,32,256]{3,2,1,0:T(8,128)(2,1)}), bf16[32,1,32,256]{3,2,1,0:T(8,128)(2,1)S(1)}, u32[]{:S(2)}, u32[]{:S(2)}) async-start(bf16[32,1,32,256]{3,2,1,0:T(8,128)(2,1)} %bitcast.91), calls=%async_computation.11 | async-start | bytes 1048576 | tf_op jit(solution)/shard_map/all_to_all | solution.py:154
  200.8 15.5 %all-to-all-done.11 = bf16[32,1,32,256]{3,2,1,0:T(8,128)(2,1)S(1)} async-done(((bf16[32,1,32,256]{3,2,1,0:T(8,128)(2,1)}), bf16[32,1,32,256]{3,2,1,0:T(8,128)(2,1)S(1)}, u32[]{:S(2)}, u32[]{:S(2)}) %all-to-all-start.11) | async-done | bytes 524320 | tf_op jit(solution)/shard_map/all_to_all | solution.py:154
  216.3 3.5 %all-to-all-start.6 = ((f32[4,1,128,256]{2,3,1,0:T(8,128)}), f32[4,1,128,256]{2,3,1,0:T(8,128)S(1)}, u32[]{:S(2)}, u32[]{:S(2)}) async-start(f32[4,1,128,256]{2,3,1,0:T(8,128)} %bitcast.56), calls=%async_computation.6 | async-start | bytes 1048576 | tf_op jit(solution)/shard_map/all_to_all | solution.py:129
  221.3 1.3 convolution_bitcast_fusion
  223.4 1.1 convert_reduce_fusion.1
  224.5 1.3 collective-permute-start.6
  225.8 1.3 collective-permute-start.7
  227.1 1.3 collective-permute-start.8
  228.5 1.3 collective-permute-start.12
  229.8 1.3 collective-permute-start.13
  231.1 3.0 %collective-permute-done.6 = bf16[1,32,256]{2,1,0:T(8,128)(2,1)S(1)} collective-permute-done((bf16[1,32,256]{2,1,0:T(8,128)(2,1)S(1)}, bf16[1,32,256]{2,1,0:T(8,128)(2,1)S(1)}, u32[]{:S(2)}, u32[]{:S(2)}) %collective-permute-start.6) | collective-permute-done | bytes 16416 | tf_op jit(solution)/shard_map/ppermute | solution.py:45
  234.1 1.3 collective-permute-start.14
  235.4 4.9 %collective-permute-done.7 = bf16[1,32,256]{2,1,0:T(8,128)(2,1)S(1)} collective-permute-done((bf16[1,32,256]{2,1,0:T(8,128)(2,1)S(1)}, bf16[1,32,256]{2,1,0:T(8,128)(2,1)S(1)}, u32[]{:S(2)}, u32[]{:S(2)}) %collective-permute-start.7) | collective-permute-done | bytes 16416 | tf_op jit(solution)/shard_map/ppermute | solution.py:45
  240.3 1.5 collective-permute-done.8
  243.1 4.4 %collective-permute-start.9 = (bf16[1,32,256]{2,1,0:T(8,128)(2,1)S(1)}, bf16[1,32,256]{2,1,0:T(8,128)(2,1)S(1)}, u32[]{:S(2)}, u32[]{:S(2)}) collective-permute-start(bf16[1,32,256]{2,1,0:T(8,128)(2,1)S(1)} %get-tuple-element.31), channel_id=1, source_target_pairs={{64,0},{65,1},{66,2},{67,3},{68,4},{69,5},{70,6},{71,7},{72,8},{73... | collective-permute-start | bytes 49160 | tf_op jit(solution)/shard_map/ppermute | solution.py:51
  249.5 2.6 collective-permute-start.15
  252.1 6.3 %all-to-all-start.12 = ((f32[4,1,128,256]{2,3,1,0:T(8,128)}), f32[4,1,128,256]{2,3,1,0:T(8,128)S(1)}, u32[]{:S(2)}, u32[]{:S(2)}) async-start(f32[4,1,128,256]{2,3,1,0:T(8,128)} %bitcast.104), calls=%async_computation.12 | async-start | bytes 1048576 | tf_op jit(solution)/shard_map/all_to_all | solution.py:129
  261.6 9.1 %all-to-all-done.12 = f32[4,1,128,256]{2,3,1,0:T(8,128)S(1)} async-done(((f32[4,1,128,256]{2,3,1,0:T(8,128)}), f32[4,1,128,256]{2,3,1,0:T(8,128)S(1)}, u32[]{:S(2)}, u32[]{:S(2)}) %all-to-all-start.12) | async-done | bytes 524320 | tf_op jit(solution)/shard_map/all_to_all | solution.py:129
  (118 shorter events, 29.4 us)
Async XLA Ops:
  0.0 1.6 copy-start
  1.6 2.3 copy-start.13
  5.3 37.2 %all-to-all-start = ((bf16[4,2,2,128,256]{3,4,2,1,0:T(8,128)(2,1)}), bf16[4,2,2,128,256]{3,4,2,1,0:T(8,128)(2,1)S(1)}, u32[]{:S(2)}, u32[]{:S(2)}) async-start(bf16[4,2,2,128,256]{3,4,2,1,0:T(8,128)(2,1)} %broadcast_in_dim.28), calls=%async_computation | async-start | bytes 2097152 | tf_op jit(solution)/shard_map/all_to_all | solution.py:21
  12.6 2.7 collective-permute-start
  13.3 2.0 collective-permute-start.1
  14.0 8.3 %collective-permute-start.2 = (bf16[2,32,256]{2,1,0:T(8,128)(2,1)S(1)}, bf16[2,32,256]{2,1,0:T(8,128)(2,1)S(1)}, u32[]{:S(2)}, u32[]{:S(2)}) collective-permute-start(bf16[2,32,256]{2,1,0:T(8,128)(2,1)S(1)} %get-tuple-element.27), channel_id=1, source_target_pairs={{0,64},{1,65},{2,66},{3,67},{4,68},{5,69},{6,70},{7,71},{8,72},{9,... | collective-permute-start | bytes 98312 | tf_op jit(solution)/shard_map/ppermute | solution.py:31
  22.3 18.7 %collective-permute-start.3 = (bf16[2,32,256]{2,1,0:T(8,128)(2,1)S(1)}, bf16[2,32,256]{2,1,0:T(8,128)(2,1)S(1)}, u32[]{:S(2)}, u32[]{:S(2)}) collective-permute-start(bf16[2,32,256]{2,1,0:T(8,128)(2,1)S(1)} %fusion.46), channel_id=1, source_target_pairs={{0,768},{1,769},{2,770},{3,771},{4,772},{5,773},{6,774},{7,775},{8... | collective-permute-start | bytes 98312 | tf_op jit(solution)/shard_map/ppermute | solution.py:35
  37.8 3.4 %collective-permute-start.4 = (bf16[2,32,256]{2,1,0:T(8,128)(2,1)S(1)}, bf16[2,32,256]{2,1,0:T(8,128)(2,1)S(1)}, u32[]{:S(2)}, u32[]{:S(2)}) collective-permute-start(bf16[2,32,256]{2,1,0:T(8,128)(2,1)S(1)} %fusion.46), channel_id=1, source_target_pairs={{0,512},{1,513},{2,514},{3,515},{4,516},{5,517},{6,518},{7,519},{8... | collective-permute-start | bytes 98312 | tf_op jit(solution)/shard_map/ppermute | solution.py:35
  39.7 2.9 %collective-permute-start.5 = (bf16[2,32,256]{2,1,0:T(8,128)(2,1)S(1)}, bf16[2,32,256]{2,1,0:T(8,128)(2,1)S(1)}, u32[]{:S(2)}, u32[]{:S(2)}) collective-permute-start(bf16[2,32,256]{2,1,0:T(8,128)(2,1)S(1)} %fusion.46), channel_id=1, source_target_pairs={{0,256},{1,257},{2,258},{3,259},{4,260},{5,261},{6,262},{7,263},{8... | collective-permute-start | bytes 98312 | tf_op jit(solution)/shard_map/ppermute | solution.py:35
  72.4 22.9 %all-to-all-start.7 = ((bf16[32,1,32,256]{3,2,1,0:T(8,128)(2,1)}), bf16[32,1,32,256]{3,2,1,0:T(8,128)(2,1)}, u32[]{:S(2)}, u32[]{:S(2)}) async-start(bf16[32,1,32,256]{3,2,1,0:T(8,128)(2,1)} %broadcast_in_dim.36), calls=%async_computation.7 | async-start | bytes 1048576 | tf_op jit(solution)/shard_map/all_to_all | solution.py:21
  78.2 1.5 copy-start.2
  82.4 2.4 copy-start.6
  103.7 2.4 copy-start.7
  106.2 2.3 copy-start.16
  106.2 2.4 copy-start.11
  106.2 3.7 %copy-start.8 = (bf16[4,1,1,128,256]{3,4,0,2,1:T(8,128)(2,1)S(1)}, bf16[4,1,1,128,256]{3,4,0,2,1:T(8,128)(2,1)}, u32[]{:S(2)}) copy-start(bf16[4,1,1,128,256]{3,4,0,2,1:T(8,128)(2,1)} %get-tuple-element.21) | copy-start | bytes 786436
  108.9 1.0 copy-start.1
  111.9 12.1 %all-to-all-start.3 = ((f32[4,3,1,4,4,128]{5,4,3,2,1,0:T(4,128)}), f32[4,3,1,4,4,128]{5,4,3,2,1,0:T(4,128)}, u32[]{:S(2)}, u32[]{:S(2)}) async-start(f32[4,3,1,4,4,128]{5,4,3,2,1,0:T(4,128)} %broadcast_in_dim.34), calls=%async_computation.3 | async-start | bytes 196608 | tf_op jit(solution)/shard_map/all_to_all | solution.py:21
  124.0 3.7 %copy-start.9 = (bf16[4,1,1,128,256]{3,4,0,2,1:T(8,128)(2,1)S(1)}, bf16[4,1,1,128,256]{3,4,0,2,1:T(8,128)(2,1)}, u32[]{:S(2)}) copy-start(bf16[4,1,1,128,256]{3,4,0,2,1:T(8,128)(2,1)} %get-tuple-element.21) | copy-start | bytes 786436
  124.8 3.2 %copy-start.12 = (bf16[4,1,1,128,256]{3,4,0,2,1:T(8,128)(2,1)S(1)}, bf16[4,1,1,128,256]{3,4,0,2,1:T(8,128)(2,1)}, u32[]{:S(2)}) copy-start(bf16[4,1,1,128,256]{3,4,0,2,1:T(8,128)(2,1)} %get-tuple-element.24) | copy-start | bytes 786436
  127.7 0.8 copy-start.3
  137.0 6.8 %copy-start.15 = (f32[3,4,4,128]{3,2,1,0:T(4,128)S(1)}, f32[3,4,4,128]{3,2,1,0:T(4,128)}, u32[]{:S(2)}) copy-start(f32[3,4,4,128]{3,2,1,0:T(4,128)} %maximum_bitcast_fusion.2) | copy-start | bytes 73732
  144.5 10.0 %all-to-all-start.9 = ((f32[4,3,1,4,4,128]{5,4,3,2,1,0:T(4,128)}), f32[4,3,1,4,4,128]{5,4,3,2,1,0:T(4,128)}, u32[]{:S(2)}, u32[]{:S(2)}) async-start(f32[4,3,1,4,4,128]{5,4,3,2,1,0:T(4,128)} %broadcast_in_dim.79), calls=%async_computation.9 | async-start | bytes 196608 | tf_op jit(solution)/shard_map/all_to_all | solution.py:21
  155.2 2.9 %copy-start.10 = (bf16[4,1,1,128,256]{3,4,0,2,1:T(8,128)(2,1)S(1)}, bf16[4,1,1,128,256]{3,4,0,2,1:T(8,128)(2,1)}, u32[]{:S(2)}) copy-start(bf16[4,1,1,128,256]{3,4,0,2,1:T(8,128)(2,1)} %get-tuple-element.23) | copy-start | bytes 786436
  157.8 0.8 copy-start.5
  171.0 22.9 %all-to-all-start.5 = ((bf16[32,1,32,256]{3,2,1,0:T(8,128)(2,1)}), bf16[32,1,32,256]{3,2,1,0:T(8,128)(2,1)}, u32[]{:S(2)}, u32[]{:S(2)}) async-start(bf16[32,1,32,256]{3,2,1,0:T(8,128)(2,1)} %bitcast.317), calls=%async_computation.5 | async-start | bytes 1048576 | tf_op jit(solution)/shard_map/all_to_all | solution.py:154
  177.9 21.9 %copy-start.4 = (bf16[4,4,128,128]{2,3,1,0:T(8,128)(2,1)S(1)}, bf16[4,4,128,128]{2,3,1,0:T(8,128)(2,1)}, u32[]{:S(2)}) copy-start(bf16[4,4,128,128]{2,3,1,0:T(8,128)(2,1)} %copy-done.3) | copy-start | bytes 1572868
  193.9 25.9 %copy-start.14 = (bf16[1,2,128,256]{3,2,1,0:T(8,128)(2,1)S(1)}, bf16[1,2,128,256]{3,2,1,0:T(8,128)(2,1)}, u32[]{:S(2)}) copy-start(bf16[1,2,128,256]{3,2,1,0:T(8,128)(2,1)} %param.5) | copy-start | bytes 393220
  193.9 22.4 %all-to-all-start.11 = ((bf16[32,1,32,256]{3,2,1,0:T(8,128)(2,1)}), bf16[32,1,32,256]{3,2,1,0:T(8,128)(2,1)S(1)}, u32[]{:S(2)}, u32[]{:S(2)}) async-start(bf16[32,1,32,256]{3,2,1,0:T(8,128)(2,1)} %bitcast.91), calls=%async_computation.11 | async-start | bytes 1048576 | tf_op jit(solution)/shard_map/all_to_all | solution.py:154
  216.3 35.7 %all-to-all-start.6 = ((f32[4,1,128,256]{2,3,1,0:T(8,128)}), f32[4,1,128,256]{2,3,1,0:T(8,128)S(1)}, u32[]{:S(2)}, u32[]{:S(2)}) async-start(f32[4,1,128,256]{2,3,1,0:T(8,128)} %bitcast.56), calls=%async_computation.6 | async-start | bytes 1048576 | tf_op jit(solution)/shard_map/all_to_all | solution.py:129
  224.5 9.6 %collective-permute-start.6 = (bf16[1,32,256]{2,1,0:T(8,128)(2,1)S(1)}, bf16[1,32,256]{2,1,0:T(8,128)(2,1)S(1)}, u32[]{:S(2)}, u32[]{:S(2)}) collective-permute-start(bf16[1,32,256]{2,1,0:T(8,128)(2,1)S(1)} %bitcast_convert_fusion.1), channel_id=1, source_target_pairs={{256,0},{257,1},{258,2},{259,3},{260,4},{261,5},{262,6},{263,7},{2... | collective-permute-start | bytes 49160 | tf_op jit(solution)/shard_map/ppermute | solution.py:45
  225.8 14.5 %collective-permute-start.7 = (bf16[1,32,256]{2,1,0:T(8,128)(2,1)S(1)}, bf16[1,32,256]{2,1,0:T(8,128)(2,1)S(1)}, u32[]{:S(2)}, u32[]{:S(2)}) collective-permute-start(bf16[1,32,256]{2,1,0:T(8,128)(2,1)S(1)} %bitcast_convert_fusion.1), channel_id=1, source_target_pairs={{512,0},{513,1},{514,2},{515,3},{516,4},{517,5},{518,6},{519,7},{5... | collective-permute-start | bytes 49160 | tf_op jit(solution)/shard_map/ppermute | solution.py:45
  227.1 14.6 %collective-permute-start.8 = (bf16[1,32,256]{2,1,0:T(8,128)(2,1)S(1)}, bf16[1,32,256]{2,1,0:T(8,128)(2,1)S(1)}, u32[]{:S(2)}, u32[]{:S(2)}) collective-permute-start(bf16[1,32,256]{2,1,0:T(8,128)(2,1)S(1)} %bitcast_convert_fusion.1), channel_id=1, source_target_pairs={{768,0},{769,1},{770,2},{771,3},{772,4},{773,5},{774,6},{775,7},{7... | collective-permute-start | bytes 49160 | tf_op jit(solution)/shard_map/ppermute | solution.py:45
  228.5 14.6 %collective-permute-start.12 = (bf16[1,32,256]{2,1,0:T(8,128)(2,1)S(1)}, bf16[1,32,256]{2,1,0:T(8,128)(2,1)S(1)}, u32[]{:S(2)}, u32[]{:S(2)}) collective-permute-start(bf16[1,32,256]{2,1,0:T(8,128)(2,1)S(1)} %bitcast_convert_fusion), channel_id=1, source_target_pairs={{256,0},{257,1},{258,2},{259,3},{260,4},{261,5},{262,6},{263,7},{2... | collective-permute-start | bytes 49160 | tf_op jit(solution)/shard_map/ppermute | solution.py:45
  229.8 17.7 %collective-permute-start.13 = (bf16[1,32,256]{2,1,0:T(8,128)(2,1)S(1)}, bf16[1,32,256]{2,1,0:T(8,128)(2,1)S(1)}, u32[]{:S(2)}, u32[]{:S(2)}) collective-permute-start(bf16[1,32,256]{2,1,0:T(8,128)(2,1)S(1)} %bitcast_convert_fusion), channel_id=1, source_target_pairs={{512,0},{513,1},{514,2},{515,3},{516,4},{517,5},{518,6},{519,7},{5... | collective-permute-start | bytes 49160 | tf_op jit(solution)/shard_map/ppermute | solution.py:45
  234.1 13.4 %collective-permute-start.14 = (bf16[1,32,256]{2,1,0:T(8,128)(2,1)S(1)}, bf16[1,32,256]{2,1,0:T(8,128)(2,1)S(1)}, u32[]{:S(2)}, u32[]{:S(2)}) collective-permute-start(bf16[1,32,256]{2,1,0:T(8,128)(2,1)S(1)} %bitcast_convert_fusion), channel_id=1, source_target_pairs={{768,0},{769,1},{770,2},{771,3},{772,4},{773,5},{774,6},{775,7},{7... | collective-permute-start | bytes 49160 | tf_op jit(solution)/shard_map/ppermute | solution.py:45
  241.8 7.7 %collective-permute-start.11 = (bf16[1,32,256]{2,1,0:T(8,128)(2,1)S(1)}, bf16[1,32,256]{2,1,0:T(8,128)(2,1)S(1)}, u32[]{:S(2)}, u32[]{:S(2)}) collective-permute-start(bf16[1,32,256]{2,1,0:T(8,128)(2,1)S(1)} %get-tuple-element.31), channel_id=1, source_target_pairs={{192,0},{193,1},{194,2},{195,3},{196,4},{197,5},{198,6},{199,7},{2... | collective-permute-start | bytes 49160 | tf_op jit(solution)/shard_map/ppermute | solution.py:51
  242.4 15.9 %collective-permute-start.10 = (bf16[1,32,256]{2,1,0:T(8,128)(2,1)S(1)}, bf16[1,32,256]{2,1,0:T(8,128)(2,1)S(1)}, u32[]{:S(2)}, u32[]{:S(2)}) collective-permute-start(bf16[1,32,256]{2,1,0:T(8,128)(2,1)S(1)} %get-tuple-element.31), channel_id=1, source_target_pairs={{128,0},{129,1},{130,2},{131,3},{132,4},{133,5},{134,6},{135,7},{1... | collective-permute-start | bytes 49160 | tf_op jit(solution)/shard_map/ppermute | solution.py:51
  243.1 15.3 %collective-permute-start.9 = (bf16[1,32,256]{2,1,0:T(8,128)(2,1)S(1)}, bf16[1,32,256]{2,1,0:T(8,128)(2,1)S(1)}, u32[]{:S(2)}, u32[]{:S(2)}) collective-permute-start(bf16[1,32,256]{2,1,0:T(8,128)(2,1)S(1)} %get-tuple-element.31), channel_id=1, source_target_pairs={{64,0},{65,1},{66,2},{67,3},{68,4},{69,5},{70,6},{71,7},{72,8},{73... | collective-permute-start | bytes 49160 | tf_op jit(solution)/shard_map/ppermute | solution.py:51
  248.1 10.3 %collective-permute-start.17 = (bf16[1,32,256]{2,1,0:T(8,128)(2,1)S(1)}, bf16[1,32,256]{2,1,0:T(8,128)(2,1)S(1)}, u32[]{:S(2)}, u32[]{:S(2)}) collective-permute-start(bf16[1,32,256]{2,1,0:T(8,128)(2,1)S(1)} %get-tuple-element.33), channel_id=1, source_target_pairs={{192,0},{193,1},{194,2},{195,3},{196,4},{197,5},{198,6},{199,7},{2... | collective-permute-start | bytes 49160 | tf_op jit(solution)/shard_map/ppermute | solution.py:51
  248.8 10.2 %collective-permute-start.16 = (bf16[1,32,256]{2,1,0:T(8,128)(2,1)S(1)}, bf16[1,32,256]{2,1,0:T(8,128)(2,1)S(1)}, u32[]{:S(2)}, u32[]{:S(2)}) collective-permute-start(bf16[1,32,256]{2,1,0:T(8,128)(2,1)S(1)} %get-tuple-element.33), channel_id=1, source_target_pairs={{128,0},{129,1},{130,2},{131,3},{132,4},{133,5},{134,6},{135,7},{1... | collective-permute-start | bytes 49160 | tf_op jit(solution)/shard_map/ppermute | solution.py:51
  249.5 10.3 %collective-permute-start.15 = (bf16[1,32,256]{2,1,0:T(8,128)(2,1)S(1)}, bf16[1,32,256]{2,1,0:T(8,128)(2,1)S(1)}, u32[]{:S(2)}, u32[]{:S(2)}) collective-permute-start(bf16[1,32,256]{2,1,0:T(8,128)(2,1)S(1)} %get-tuple-element.33), channel_id=1, source_target_pairs={{64,0},{65,1},{66,2},{67,3},{68,4},{69,5},{70,6},{71,7},{72,8},{73... | collective-permute-start | bytes 49160 | tf_op jit(solution)/shard_map/ppermute | solution.py:51
  252.1 18.6 %all-to-all-start.12 = ((f32[4,1,128,256]{2,3,1,0:T(8,128)}), f32[4,1,128,256]{2,3,1,0:T(8,128)S(1)}, u32[]{:S(2)}, u32[]{:S(2)}) async-start(f32[4,1,128,256]{2,3,1,0:T(8,128)} %bitcast.104), calls=%async_computation.12 | async-start | bytes 1048576 | tf_op jit(solution)/shard_map/all_to_all | solution.py:129

commit v8 on v6

--- a/solution.py
+++ b/solution.py
@@ -85,17 +85,15 @@
     own = gather_axis(piece, ("x", "ty"), n_x * n_y)
     both = gather_axis(own, "tc", n_c)
     both = both.reshape(n_c, n_x, n_y, micro_count, row_count // n_x, chunk_width)
-    encoded = jnp.transpose(both, (3, 1, 4, 2, 0, 5)).reshape(micro_count, row_count, model_width)
-
     query_heads = slots[:, 0].reshape(n_dp, micro_count, row_count, head_count, HD)
     grad_heads = slots[:, 1].reshape(n_dp, micro_count, row_count, head_count, HD)
-    flat_enc = encoded.reshape(rows, model_width)
-    key_heads = jnp.dot(flat_enc, layer[:, 1, :], preferred_element_type=jnp.float32).astype(
-        jnp.bfloat16
-    ).reshape(micro_count, row_count, head_count, HD)
-    value_heads = jnp.dot(flat_enc, layer[:, 2, :], preferred_element_type=jnp.float32).astype(
-        jnp.bfloat16
-    ).reshape(micro_count, row_count, head_count, HD)
+    def project(kind):
+        grid = layer[:, kind, :].reshape(n_y, n_c, chunk_width, feat_width)
+        out = jnp.einsum("cxymrf,ycfn->mxrn", both, grid, preferred_element_type=jnp.float32)
+        return out.astype(jnp.bfloat16).reshape(micro_count, row_count, head_count, HD)
+
+    key_heads = project(1)
+    value_heads = project(2)
 
     scores = (
         jnp.einsum("jmqhe,mkhe->mhjqk", query_heads, key_heads, preferred_element_type=jnp.float32)
@@ -132,15 +130,14 @@
     value_grad = jnp.einsum(
         "mhjqk,jmqhe->mkhe", prob_rounded, grad_heads, preferred_element_type=jnp.float32
     ).astype(jnp.bfloat16)
-    head_terms = (
-        jnp.einsum("rc,dc->rd", key_grad.reshape(rows, feat_width), layer[:, 1, :],
-                   preferred_element_type=jnp.float32)
-        + jnp.einsum("rc,dc->rd", value_grad.reshape(rows, feat_width), layer[:, 2, :],
-                     preferred_element_type=jnp.float32)
-    ).astype(jnp.bfloat16)
-    head_terms = head_terms.reshape(micro_count, row_count, n_y, n_c, chunk_width)
+    def back(grad, kind):
+        grid = layer[:, kind, :].reshape(n_y, n_c, chunk_width, feat_width)
+        return jnp.einsum("mrn,ycfn->cmryf", grad.reshape(micro_count, row_count, feat_width), grid,
+                          preferred_element_type=jnp.float32)
+
+    head_terms = (back(key_grad, 1) + back(value_grad, 2)).astype(jnp.bfloat16)
     pair_sum = jnp.sum(
-        lax.all_to_all(head_terms, "tc", 3, 0, tiled=False).astype(jnp.float32), axis=0
+        lax.all_to_all(head_terms, "tc", 0, 0, tiled=False).astype(jnp.float32), axis=0
     ).astype(jnp.bfloat16)
     pair_sum = jnp.moveaxis(pair_sum, 2, 0)
     pair_sum = jnp.where(seg > 0, pair_sum, jnp.zeros_like(pair_sum))

time: 237 us -> 216 us (0.911)
  local copies, waits for them, and re-layouts: 30.9 us -> 20.5 us
  matrix products: 19.3 us -> 13.4 us
  waiting for transfers between devices: 97.2 us -> 93.6 us
    another operation x3 -> x0, local copies, waits for them, and re-layouts: 10.8 us -> none  [the longest x2 6.35 us: shards(): lax.all_to_all(head_terms, 'tc', 3, 0, tiled=False).astype(jnp.float32)]
    dot_general x4, matrix products: 12.2 us -> 5.23 us  [the longest x2 3.7 us: project(): jnp.einsum('cxymrf,ycfn->mxrn', both, grid, preferred_element_type=jnp.fl...]
    transpose x1 -> x0, local copies, waits for them, and re-layouts: 3.49 us -> none  [shards(): jnp.transpose(both, (3, 1, 4, 2, 0, 5))]
    all_to_all x3, waiting for transfers between devices: 30.3 us -> 26.9 us  [gather_axis(): return lax.all_to_all(spread, axis, 0, 0, tiled=False)]
    slice x1 -> x2, local copies, waits for them, and re-layouts: 2.27 us -> 5.65 us  [the longest x1 4.55 us: back(): grid = layer[:, kind, :].reshape(n_y, n_c, chunk_width, feat_width)]
    unnamed x21 -> x29, local copies, waits for them, and re-layouts: 3.46 us -> 5.85 us
  transfers between devices with their start and end apart: 17 -> 17, of which waited for: 13 -> 13; matrix products, arithmetic and copies ran while one was open for 4% -> 6% of each run, Pallas kernels for 0% -> 0%
where the time goes in v8:
time: 216 us; the launch traced here: 215 us
  waiting for transfers between devices  93.6 us (43%)
  starting transfers between devices  66.8 us (31%)
  local copies, waits for them, and re-layouts  20.5 us (9%)
  matrix products  13.4 us (6%)
  blocking collectives  11.9 us (6%)
  other arithmetic  8.58 us (4%)
    ppermute x3, waiting for transfers between devices, seg_reduce(): got = lax.ppermute(sent, 'zh', [(b, 0)])  31.7 us
    all_to_all x3, waiting for transfers between devices, gather_axis(): return lax.all_to_all(spread, axis, 0, 0, tiled=False)  26.9 us
    all_to_all x1, waiting for transfers between devices, shards(): lax.all_to_all(pair_sum, ('x', 'ty'), 0, 0, tiled=False).astype(jnp.float32)  26.2 us
    all_to_all x3, starting transfers between devices, gather_axis(): return lax.all_to_all(spread, axis, 0, 0, tiled=False)  23 us
    ppermute x3, starting transfers between devices, seg_broadcast(): got = lax.ppermute(mine, 'zh', [(0, b)])  18.6 us
    ppermute x3, starting transfers between devices, seg_broadcast(): got = lax.ppermute(pieces[:, k], 'x', [(0, k)])  7.25 us
    all_to_all x1, blocking collectives, shards(): lax.all_to_all(head_terms, 'tc', 0, 0, tiled=False).astype(jnp.float32)  6.31 us
    unnamed x29, local copies, waits for them, and re-layouts  5.85 us
  transfers between devices with their start and end apart: 17, of which 13 were waited for; matrix products, arithmetic and copies ran while one was open for 6% of the time, Pallas kernels for 0%

profile of v8, /device:TPU:72, one launch (start us, length us, event | category | flops | bytes accessed | tf_op | source)
XLA Modules:
  0.0 215.2 jit_solution(8653892701491233234)
XLA Ops:
  0.0 1.6 copy-done
  1.6 2.3 %fusion.9 = bf16[256,256]{1,0:T(8,128)(2,1)S(1)} fusion(bf16[256,4096]{1,0:T(8,128)(2,1)S(1)} %bitcast.154, bf16[4096,3,256]{2,0,1:T(8,128)(2,1)} %bitcast.161), kind=kOutput, calls=%fused_computation.18 | convolution fusion | flops 536936448 | bytes 4325376 | tf_op jit(solution)/shard_map/dot_general | solution.py:76
  4.2 1.2 broadcast_in_dim.10
  5.3 6.9 %all-to-all-start = ((bf16[4,2,2,128,256]{3,4,2,1,0:T(8,128)(2,1)}), bf16[4,2,2,128,256]{3,4,2,1,0:T(8,128)(2,1)S(1)}, u32[]{:S(2)}, u32[]{:S(2)}) async-start(bf16[4,2,2,128,256]{3,4,2,1,0:T(8,128)(2,1)} %broadcast_in_dim.10), calls=%async_computation | async-start | bytes 2097152 | tf_op jit(solution)/shard_map/all_to_all | solution.py:21
  12.3 4.7 %collective-permute-start = (bf16[2,32,256]{2,1,0:T(8,128)(2,1)S(1)}, bf16[2,32,256]{2,1,0:T(8,128)(2,1)S(1)}, u32[]{:S(2)}, u32[]{:S(2)}) collective-permute-start(bf16[2,32,256]{2,1,0:T(8,128)(2,1)S(1)} %get-tuple-element.23), channel_id=1, source_target_pairs={{0,192},{1,193},{2,194},{3,195},{4,196},{5,197},{6,198},{7,199},{8... | collective-permute-start | bytes 98312 | tf_op jit(solution)/shard_map/ppermute | solution.py:31
  17.0 1.3 collective-permute-start.1
  18.3 1.3 collective-permute-start.2
  19.6 0.3 collective-permute-done.1
  19.8 1.3 collective-permute-done.2
  21.2 15.5 %collective-permute-start.3 = (bf16[2,32,256]{2,1,0:T(8,128)(2,1)S(1)}, bf16[2,32,256]{2,1,0:T(8,128)(2,1)S(1)}, u32[]{:S(2)}, u32[]{:S(2)}) collective-permute-start(bf16[2,32,256]{2,1,0:T(8,128)(2,1)S(1)} %fusion.32), channel_id=1, source_target_pairs={{0,768},{1,769},{2,770},{3,771},{4,772},{5,773},{6,774},{7,775},{8... | collective-permute-start | bytes 98312 | tf_op jit(solution)/shard_map/ppermute | solution.py:35
  36.7 1.8 collective-permute-start.4
  38.5 1.3 collective-permute-start.5
  39.8 0.4 collective-permute-done.4
  40.3 1.1 collective-permute-done.5
  41.4 1.2 broadcast_in_dim.11
  42.7 9.7 %all-to-all-start.1 = ((bf16[32,2,32,256]{3,2,1,0:T(8,128)(2,1)}), bf16[32,2,32,256]{3,2,1,0:T(8,128)(2,1)S(1)}, u32[]{:S(2)}, u32[]{:S(2)}) async-start(bf16[32,2,32,256]{3,2,1,0:T(8,128)(2,1)} %broadcast_in_dim.11), calls=%async_computation.1 | async-start | bytes 2097152 | tf_op jit(solution)/shard_map/all_to_all | solution.py:21
  52.4 4.5 %fusion.35 = (bf16[4096,1,256]{2,0,1:T(8,128)(2,1)}, bf16[4096,1,256]{2,0,1:T(8,128)(2,1)}) fusion(bf16[4096,3,256]{2,0,1:T(8,128)(2,1)} %bitcast.162), kind=kLoop, calls=%fused_computation.67 | loop fusion | bytes 8388608 | tf_op jit(solution)/shard_map/slice | solution.py:134
  56.9 1.1 fusion.36
  58.0 20.6 %all-to-all-done.1 = bf16[32,2,32,256]{3,2,1,0:T(8,128)(2,1)S(1)} async-done(((bf16[32,2,32,256]{3,2,1,0:T(8,128)(2,1)}), bf16[32,2,32,256]{3,2,1,0:T(8,128)(2,1)S(1)}, u32[]{:S(2)}, u32[]{:S(2)}) %all-to-all-start.1) | async-done | bytes 1048608 | tf_op jit(solution)/shard_map/all_to_all | solution.py:21
  78.7 0.3 broadcast_in_dim.12
  78.9 5.5 %all_to_all.35 = bf16[2,32,2,32,256]{4,3,2,1,0:T(8,128)(2,1)S(1)} all-to-all(bf16[2,32,2,32,256]{4,3,2,1,0:T(8,128)(2,1)S(1)} %broadcast_in_dim.12), channel_id=1, replica_groups=mesh['zh'=4,'x'=4,'dp'=4,'ty'=8,'tc'=2] {'tc'}, dimensions={0} | all-to-all | bytes 4194304 | tf_op jit(solution)/shard_map/all_to_all | solution.py:21
  84.5 0.7 fusion.3
  85.2 0.6 copy-done.9
  85.9 0.9 reshape.56
  86.7 3.0 %fusion.1 = bf16[4,2,32,256,1,1]{3,2,5,0,1,4:T(8,128)(2,1)S(1)} fusion(bf16[8,2,256,256,1,1]{3,2,1,0,5,4:T(8,128)(2,1)} %bitcast.157, bf16[2,4,8,2,32,256]{5,4,3,2,1,0:T(8,128)(2,1)} %bitcast.164), kind=kOutput, calls=%fused_computation.3 | convolution fusion | flops 536870912 | bytes 4325376 | tf_op jit(solution)/shard_map/cxymrf,ycfn->mxrn/dot_general | solution.py:92
  90.1 1.4 multiply_reduce_fusion.1
  91.5 2.0 fusion.5
  93.5 0.7 broadcast_in_dim.13
  94.2 6.5 %all-to-all-start.3 = ((f32[4,3,2,4,4,128]{5,4,3,2,1,0:T(4,128)}), f32[4,3,2,4,4,128]{5,4,3,2,1,0:T(4,128)S(1)}, u32[]{:S(2)}, u32[]{:S(2)}) async-start(f32[4,3,2,4,4,128]{5,4,3,2,1,0:T(4,128)} %broadcast_in_dim.13), calls=%async_computation.3 | async-start | bytes 393216 | tf_op jit(solution)/shard_map/all_to_all | solution.py:21
  100.7 6.3 %all-to-all-done.3 = f32[4,3,2,4,4,128]{5,4,3,2,1,0:T(4,128)S(1)} async-done(((f32[4,3,2,4,4,128]{5,4,3,2,1,0:T(4,128)}), f32[4,3,2,4,4,128]{5,4,3,2,1,0:T(4,128)S(1)}, u32[]{:S(2)}, u32[]{:S(2)}) %all-to-all-start.3) | async-done | bytes 196640 | tf_op jit(solution)/shard_map/all_to_all | solution.py:21
  107.1 3.1 %fusion.20 = (bf16[2,4,4,128,128]{3,4,2,1,0:T(8,128)(2,1)S(1)}, bf16[2,4,4,128,128]{3,4,2,1,0:T(8,128)(2,1)S(1)}) fusion(f32[2,4,4,128]{3,2,1,0:T(4,128)S(1)} %get-tuple-element.11, f32[2,4,4,128]{3,2,1,0:T(4,128)S(1)} %bitcast_reduce_fusion, f32[2,4,4,128,128]{3,4,2,1,0:T(8,128)} %copy-done.1, f32[2,4,4,128,128]{3,4,2,1,0:T(8,128)} %get-tuple-element.26, ...), kind=kLoop, calls=%fused_computation.30 | loop fusion | flops 4194304 | bytes 6340608 | tf_op jit(solution)/shard_map/convert_element_type | solution.py:118
  110.2 0.5 fusion.12
  110.7 0.5 fusion.10
  111.2 0.9 copy-done.3
  112.1 0.8 fusion.37
  112.9 0.8 copy-done.4
  113.7 0.8 fusion.8
  114.6 6.3 %all_to_all.36 = bf16[2,2,128,8,256]{4,2,3,1,0:T(8,128)(2,1)} all-to-all(bf16[2,2,128,8,256]{4,2,3,1,0:T(8,128)(2,1)S(1)} %copy.225), channel_id=1, replica_groups=mesh['zh'=4,'x'=4,'dp'=4,'ty'=8,'tc'=2] {'tc'}, dimensions={0} | all-to-all | bytes 4194304 | tf_op jit(solution)/shard_map/all_to_all | solution.py:140
  120.9 2.1 reduce_sum.70
  123.1 1.1 copy.228
  124.2 5.1 %all-to-all-start.5 = ((bf16[32,2,32,256]{3,2,1,0:T(8,128)(2,1)}), bf16[32,2,32,256]{3,2,1,0:T(8,128)(2,1)S(1)}, u32[]{:S(2)}, u32[]{:S(2)}) async-start(bf16[32,2,32,256]{3,2,1,0:T(8,128)(2,1)} %bitcast.160), calls=%async_computation.5 | async-start | bytes 2097152 | tf_op jit(solution)/shard_map/all_to_all | solution.py:148
  129.3 1.5 convolution_bitcast_fusion
  130.9 1.1 copy.236
  132.0 26.2 %all-to-all-done.5 = bf16[32,2,32,256]{3,2,1,0:T(8,128)(2,1)S(1)} async-done(((bf16[32,2,32,256]{3,2,1,0:T(8,128)(2,1)}), bf16[32,2,32,256]{3,2,1,0:T(8,128)(2,1)S(1)}, u32[]{:S(2)}, u32[]{:S(2)}) %all-to-all-start.5) | async-done | bytes 1048608 | tf_op jit(solution)/shard_map/all_to_all | solution.py:148
  158.1 1.0 copy-done.7
  159.1 5.0 %all-to-all-start.6 = ((f32[4,2,128,256]{2,3,1,0:T(8,128)}), f32[4,2,128,256]{2,3,1,0:T(8,128)S(1)}, u32[]{:S(2)}, u32[]{:S(2)}) async-start(f32[4,2,128,256]{2,3,1,0:T(8,128)} %bitcast.54), calls=%async_computation.6 | async-start | bytes 2097152 | tf_op jit(solution)/shard_map/all_to_all | solution.py:124
  164.2 1.4 convert_reduce_fusion
  165.5 1.3 collective-permute-start.6
  166.8 1.3 collective-permute-start.7
  168.1 1.3 collective-permute-start.8
  169.5 12.9 %collective-permute-done.6 = bf16[2,32,256]{2,1,0:T(8,128)(2,1)S(1)} collective-permute-done((bf16[2,32,256]{2,1,0:T(8,128)(2,1)S(1)}, bf16[2,32,256]{2,1,0:T(8,128)(2,1)S(1)}, u32[]{:S(2)}, u32[]{:S(2)}) %collective-permute-start.6) | collective-permute-done | bytes 32800 | tf_op jit(solution)/shard_map/ppermute | solution.py:45
  182.3 4.5 %collective-permute-done.7 = bf16[2,32,256]{2,1,0:T(8,128)(2,1)S(1)} collective-permute-done((bf16[2,32,256]{2,1,0:T(8,128)(2,1)S(1)}, bf16[2,32,256]{2,1,0:T(8,128)(2,1)S(1)}, u32[]{:S(2)}, u32[]{:S(2)}) %collective-permute-start.7) | collective-permute-done | bytes 32800 | tf_op jit(solution)/shard_map/ppermute | solution.py:45
  186.9 14.3 %collective-permute-done.8 = bf16[2,32,256]{2,1,0:T(8,128)(2,1)S(1)} collective-permute-done((bf16[2,32,256]{2,1,0:T(8,128)(2,1)S(1)}, bf16[2,32,256]{2,1,0:T(8,128)(2,1)S(1)}, u32[]{:S(2)}, u32[]{:S(2)}) %collective-permute-start.8) | collective-permute-done | bytes 32800 | tf_op jit(solution)/shard_map/ppermute | solution.py:45
  201.2 1.3 collective-permute-start.10
  202.5 0.8 copy.232
  203.3 1.3 collective-permute-start.9
  204.6 1.3 collective-permute-start.11
  205.9 2.7 %collective-permute-done.10 = bf16[2,32,256]{2,1,0:T(8,128)(2,1)S(1)} collective-permute-done((bf16[2,32,256]{2,1,0:T(8,128)(2,1)S(1)}, bf16[2,32,256]{2,1,0:T(8,128)(2,1)S(1)}, u32[]{:S(2)}, u32[]{:S(2)}) %collective-permute-start.10) | collective-permute-done | bytes 32800 | tf_op jit(solution)/shard_map/ppermute | solution.py:51
  208.6 0.5 collective-permute-done.9
  209.1 2.5 %collective-permute-done.11 = bf16[2,32,256]{2,1,0:T(8,128)(2,1)S(1)} collective-permute-done((bf16[2,32,256]{2,1,0:T(8,128)(2,1)S(1)}, bf16[2,32,256]{2,1,0:T(8,128)(2,1)S(1)}, u32[]{:S(2)}, u32[]{:S(2)}) %collective-permute-start.11) | collective-permute-done | bytes 32800 | tf_op jit(solution)/shard_map/ppermute | solution.py:51
  211.6 0.7 pad_maximum_fusion.1
  212.3 1.1 copy.233
  213.5 1.0 fusion.22
  214.5 0.8 copy.237
  (53 shorter events, 1.2 us)
Async XLA Ops:
  0.0 1.6 copy-start
  1.6 2.3 %copy-start.12 = (bf16[1,2,128,256]{3,2,1,0:T(8,128)(2,1)S(1)}, bf16[1,2,128,256]{3,2,1,0:T(8,128)(2,1)}, u32[]{:S(2)}) copy-start(bf16[1,2,128,256]{3,2,1,0:T(8,128)(2,1)} %param.5) | copy-start | bytes 393220
  5.3 36.0 %all-to-all-start = ((bf16[4,2,2,128,256]{3,4,2,1,0:T(8,128)(2,1)}), bf16[4,2,2,128,256]{3,4,2,1,0:T(8,128)(2,1)S(1)}, u32[]{:S(2)}, u32[]{:S(2)}) async-start(bf16[4,2,2,128,256]{3,4,2,1,0:T(8,128)(2,1)} %broadcast_in_dim.10), calls=%async_computation | async-start | bytes 2097152 | tf_op jit(solution)/shard_map/all_to_all | solution.py:21
  12.3 7.3 %collective-permute-start = (bf16[2,32,256]{2,1,0:T(8,128)(2,1)S(1)}, bf16[2,32,256]{2,1,0:T(8,128)(2,1)S(1)}, u32[]{:S(2)}, u32[]{:S(2)}) collective-permute-start(bf16[2,32,256]{2,1,0:T(8,128)(2,1)S(1)} %get-tuple-element.23), channel_id=1, source_target_pairs={{0,192},{1,193},{2,194},{3,195},{4,196},{5,197},{6,198},{7,199},{8... | collective-permute-start | bytes 98312 | tf_op jit(solution)/shard_map/ppermute | solution.py:31
  17.0 2.9 %collective-permute-start.1 = (bf16[2,32,256]{2,1,0:T(8,128)(2,1)S(1)}, bf16[2,32,256]{2,1,0:T(8,128)(2,1)S(1)}, u32[]{:S(2)}, u32[]{:S(2)}) collective-permute-start(bf16[2,32,256]{2,1,0:T(8,128)(2,1)S(1)} %get-tuple-element.22), channel_id=1, source_target_pairs={{0,128},{1,129},{2,130},{3,131},{4,132},{5,133},{6,134},{7,135},{8... | collective-permute-start | bytes 98312 | tf_op jit(solution)/shard_map/ppermute | solution.py:31
  18.3 2.9 %collective-permute-start.2 = (bf16[2,32,256]{2,1,0:T(8,128)(2,1)S(1)}, bf16[2,32,256]{2,1,0:T(8,128)(2,1)S(1)}, u32[]{:S(2)}, u32[]{:S(2)}) collective-permute-start(bf16[2,32,256]{2,1,0:T(8,128)(2,1)S(1)} %get-tuple-element.21), channel_id=1, source_target_pairs={{0,64},{1,65},{2,66},{3,67},{4,68},{5,69},{6,70},{7,71},{8,72},{9,... | collective-permute-start | bytes 98312 | tf_op jit(solution)/shard_map/ppermute | solution.py:31
  21.2 18.7 %collective-permute-start.3 = (bf16[2,32,256]{2,1,0:T(8,128)(2,1)S(1)}, bf16[2,32,256]{2,1,0:T(8,128)(2,1)S(1)}, u32[]{:S(2)}, u32[]{:S(2)}) collective-permute-start(bf16[2,32,256]{2,1,0:T(8,128)(2,1)S(1)} %fusion.32), channel_id=1, source_target_pairs={{0,768},{1,769},{2,770},{3,771},{4,772},{5,773},{6,774},{7,775},{8... | collective-permute-start | bytes 98312 | tf_op jit(solution)/shard_map/ppermute | solution.py:35
  36.7 3.6 %collective-permute-start.4 = (bf16[2,32,256]{2,1,0:T(8,128)(2,1)S(1)}, bf16[2,32,256]{2,1,0:T(8,128)(2,1)S(1)}, u32[]{:S(2)}, u32[]{:S(2)}) collective-permute-start(bf16[2,32,256]{2,1,0:T(8,128)(2,1)S(1)} %fusion.32), channel_id=1, source_target_pairs={{0,512},{1,513},{2,514},{3,515},{4,516},{5,517},{6,518},{7,519},{8... | collective-permute-start | bytes 98312 | tf_op jit(solution)/shard_map/ppermute | solution.py:35
  38.5 2.9 %collective-permute-start.5 = (bf16[2,32,256]{2,1,0:T(8,128)(2,1)S(1)}, bf16[2,32,256]{2,1,0:T(8,128)(2,1)S(1)}, u32[]{:S(2)}, u32[]{:S(2)}) collective-permute-start(bf16[2,32,256]{2,1,0:T(8,128)(2,1)S(1)} %fusion.32), channel_id=1, source_target_pairs={{0,256},{1,257},{2,258},{3,259},{4,260},{5,261},{6,262},{7,263},{8... | collective-permute-start | bytes 98312 | tf_op jit(solution)/shard_map/ppermute | solution.py:35
  41.4 1.3 copy-start.5
  42.7 36.0 %all-to-all-start.1 = ((bf16[32,2,32,256]{3,2,1,0:T(8,128)(2,1)}), bf16[32,2,32,256]{3,2,1,0:T(8,128)(2,1)S(1)}, u32[]{:S(2)}, u32[]{:S(2)}) async-start(bf16[32,2,32,256]{3,2,1,0:T(8,128)(2,1)} %broadcast_in_dim.11), calls=%async_computation.1 | async-start | bytes 2097152 | tf_op jit(solution)/shard_map/all_to_all | solution.py:21
  52.4 4.6 %copy-start.6 = (bf16[4,2,2,128,256]{3,4,2,1,0:T(8,128)(2,1)S(1)}, bf16[4,2,2,128,256]{3,4,2,1,0:T(8,128)(2,1)}, u32[]{:S(2)}) copy-start(bf16[4,2,2,128,256]{3,4,2,1,0:T(8,128)(2,1)} %copy-done.5) | copy-start | bytes 3145732
  78.9 5.6 %copy-start.2 = (bf16[4096,1,256]{2,0,1:T(8,128)(2,1)S(1)}, bf16[4096,1,256]{2,0,1:T(8,128)(2,1)}, u32[]{:S(2)}) copy-start(bf16[4096,1,256]{2,0,1:T(8,128)(2,1)} %get-tuple-element.13) | copy-start | bytes 6291460
  84.5 1.4 copy-start.9
  86.7 3.4 %copy-start.11 = (bf16[4,1,2,128,256]{3,4,2,0,1:T(8,128)(2,1)S(1)}, bf16[4,1,2,128,256]{3,4,2,0,1:T(8,128)(2,1)}, u32[]{:S(2)}) copy-start(bf16[4,1,2,128,256]{3,4,2,0,1:T(8,128)(2,1)} %get-tuple-element.17) | copy-start | bytes 1572868
  89.7 1.8 copy-start.10
  91.5 2.0 copy-start.1
  94.2 12.7 %all-to-all-start.3 = ((f32[4,3,2,4,4,128]{5,4,3,2,1,0:T(4,128)}), f32[4,3,2,4,4,128]{5,4,3,2,1,0:T(4,128)S(1)}, u32[]{:S(2)}, u32[]{:S(2)}) async-start(f32[4,3,2,4,4,128]{5,4,3,2,1,0:T(4,128)} %broadcast_in_dim.13), calls=%async_computation.3 | async-start | bytes 393216 | tf_op jit(solution)/shard_map/all_to_all | solution.py:21
  110.1 1.0 copy-start.8
  110.2 2.0 copy-start.3
  112.1 1.6 copy-start.4
  124.2 33.9 %all-to-all-start.5 = ((bf16[32,2,32,256]{3,2,1,0:T(8,128)(2,1)}), bf16[32,2,32,256]{3,2,1,0:T(8,128)(2,1)S(1)}, u32[]{:S(2)}, u32[]{:S(2)}) async-start(bf16[32,2,32,256]{3,2,1,0:T(8,128)(2,1)} %bitcast.160), calls=%async_computation.5 | async-start | bytes 2097152 | tf_op jit(solution)/shard_map/all_to_all | solution.py:148
  132.0 70.6 %copy-start.13 = (bf16[1,2,128,256]{3,2,1,0:T(8,128)(2,1)S(1)}, bf16[1,2,128,256]{3,2,1,0:T(8,128)(2,1)}, u32[]{:S(2)}) copy-start(bf16[1,2,128,256]{3,2,1,0:T(8,128)(2,1)} %param.5) | copy-start | bytes 393220
  158.1 1.0 copy-start.7
  159.1 54.3 %all-to-all-start.6 = ((f32[4,2,128,256]{2,3,1,0:T(8,128)}), f32[4,2,128,256]{2,3,1,0:T(8,128)S(1)}, u32[]{:S(2)}, u32[]{:S(2)}) async-start(f32[4,2,128,256]{2,3,1,0:T(8,128)} %bitcast.54), calls=%async_computation.6 | async-start | bytes 2097152 | tf_op jit(solution)/shard_map/all_to_all | solution.py:124
  165.5 16.8 %collective-permute-start.6 = (bf16[2,32,256]{2,1,0:T(8,128)(2,1)S(1)}, bf16[2,32,256]{2,1,0:T(8,128)(2,1)S(1)}, u32[]{:S(2)}, u32[]{:S(2)}) collective-permute-start(bf16[2,32,256]{2,1,0:T(8,128)(2,1)S(1)} %convert_element_type.97), channel_id=1, source_target_pairs={{256,0},{257,1},{258,2},{259,3},{260,4},{261,5},{262,6},{263,7},{2... | collective-permute-start | bytes 98312 | tf_op jit(solution)/shard_map/ppermute | solution.py:45
  166.8 20.0 %collective-permute-start.7 = (bf16[2,32,256]{2,1,0:T(8,128)(2,1)S(1)}, bf16[2,32,256]{2,1,0:T(8,128)(2,1)S(1)}, u32[]{:S(2)}, u32[]{:S(2)}) collective-permute-start(bf16[2,32,256]{2,1,0:T(8,128)(2,1)S(1)} %convert_element_type.97), channel_id=1, source_target_pairs={{512,0},{513,1},{514,2},{515,3},{516,4},{517,5},{518,6},{519,7},{5... | collective-permute-start | bytes 98312 | tf_op jit(solution)/shard_map/ppermute | solution.py:45
  168.1 33.1 %collective-permute-start.8 = (bf16[2,32,256]{2,1,0:T(8,128)(2,1)S(1)}, bf16[2,32,256]{2,1,0:T(8,128)(2,1)S(1)}, u32[]{:S(2)}, u32[]{:S(2)}) collective-permute-start(bf16[2,32,256]{2,1,0:T(8,128)(2,1)S(1)} %convert_element_type.97), channel_id=1, source_target_pairs={{768,0},{769,1},{770,2},{771,3},{772,4},{773,5},{774,6},{775,7},{7... | collective-permute-start | bytes 98312 | tf_op jit(solution)/shard_map/ppermute | solution.py:45
  201.2 7.4 %collective-permute-start.10 = (bf16[2,32,256]{2,1,0:T(8,128)(2,1)S(1)}, bf16[2,32,256]{2,1,0:T(8,128)(2,1)S(1)}, u32[]{:S(2)}, u32[]{:S(2)}) collective-permute-start(bf16[2,32,256]{2,1,0:T(8,128)(2,1)S(1)} %get-tuple-element.20), channel_id=1, source_target_pairs={{128,0},{129,1},{130,2},{131,3},{132,4},{133,5},{134,6},{135,7},{1... | collective-permute-start | bytes 98312 | tf_op jit(solution)/shard_map/ppermute | solution.py:51
  203.3 5.8 %collective-permute-start.9 = (bf16[2,32,256]{2,1,0:T(8,128)(2,1)S(1)}, bf16[2,32,256]{2,1,0:T(8,128)(2,1)S(1)}, u32[]{:S(2)}, u32[]{:S(2)}) collective-permute-start(bf16[2,32,256]{2,1,0:T(8,128)(2,1)S(1)} %get-tuple-element.20), channel_id=1, source_target_pairs={{64,0},{65,1},{66,2},{67,3},{68,4},{69,5},{70,6},{71,7},{72,8},{73... | collective-permute-start | bytes 98312 | tf_op jit(solution)/shard_map/ppermute | solution.py:51
  204.6 7.0 %collective-permute-start.11 = (bf16[2,32,256]{2,1,0:T(8,128)(2,1)S(1)}, bf16[2,32,256]{2,1,0:T(8,128)(2,1)S(1)}, u32[]{:S(2)}, u32[]{:S(2)}) collective-permute-start(bf16[2,32,256]{2,1,0:T(8,128)(2,1)S(1)} %get-tuple-element.20), channel_id=1, source_target_pairs={{192,0},{193,1},{194,2},{195,3},{196,4},{197,5},{198,6},{199,7},{2... | collective-permute-start | bytes 98312 | tf_op jit(solution)/shard_map/ppermute | solution.py:51

commit v9 on v8

--- a/solution.py
+++ b/solution.py
@@ -21,7 +21,7 @@
     return lax.all_to_all(spread, axis, 0, 0, tiled=False)
 
 
-def seg_broadcast(value, n_hi, n_x):
+def seg_broadcast(value, n_hi, n_x, held):
     x = lax.axis_index("x")
     zh = lax.axis_index("zh")
     quarter = value.shape[1] // n_x
@@ -30,11 +30,12 @@
     for k in range(1, n_x):
         got = lax.ppermute(pieces[:, k], "x", [(0, k)])
         mine = jnp.where(x == k, got, mine)
+    mine, held = lax.optimization_barrier((mine, held))
     out = mine
     for b in range(1, n_hi):
         got = lax.ppermute(mine, "zh", [(0, b)])
         out = jnp.where(zh == b, got, out)
-    return out
+    return out, held
 
 
 def seg_reduce(mine, n_hi, n_x):
@@ -73,15 +74,14 @@
     rows = micro_count * row_count
     chunk_width = model_width // n_tensor
 
+    chunk = lax.dynamic_slice_in_dim(states, tix * chunk_width, chunk_width, axis=2)
+    piece, held = seg_broadcast(chunk, n_hi, n_x, (states, layer[:, 0, :], cotangent[0]))
+    held_states, query_weights, upstream = held
     query = jnp.dot(
-        states.reshape(rows, model_width), layer[:, 0, :], preferred_element_type=jnp.float32
+        held_states.reshape(rows, model_width), query_weights, preferred_element_type=jnp.float32
     ).astype(jnp.bfloat16)
     query = query.reshape(micro_count, row_count, feat_width)
-    slots = gather_axis(jnp.stack([query, cotangent[0]]), "dp", n_dp)
-
-    chunk = lax.dynamic_slice_in_dim(states, tix * chunk_width, chunk_width, axis=2)
-    piece = seg_broadcast(chunk, n_hi, n_x)
-    slots, piece = lax.optimization_barrier((slots, piece))
+    slots = gather_axis(jnp.stack([query, upstream]), "dp", n_dp)
     own = gather_axis(piece, ("x", "ty"), n_x * n_y)
     both = gather_axis(own, "tc", n_c)
     both = both.reshape(n_c, n_x, n_y, micro_count, row_count // n_x, chunk_width)

time: 216 us -> 222 us (1.028)
  the two profiles are of different devices: /device:TPU:72 before, /device:TPU:136 now
where the time goes in v9:
time: 222 us; the launch traced here: 221 us
  waiting for transfers between devices  107 us (48%)
  starting transfers between devices  67.2 us (30%)
  local copies, waits for them, and re-layouts  17.3 us (8%)
  matrix products  13.4 us (6%)
  blocking collectives  11.7 us (5%)
  other arithmetic  4.4 us (2%)
    all_to_all x3, waiting for transfers between devices, gather_axis(): return lax.all_to_all(spread, axis, 0, 0, tiled=False)  44 us
    all_to_all x1, waiting for transfers between devices, shards(): lax.all_to_all(pair_sum, ('x', 'ty'), 0, 0, tiled=False).astype(jnp.float32)  27.4 us
    ppermute x3, waiting for transfers between devices, seg_reduce(): got = lax.ppermute(sent, 'zh', [(b, 0)])  27.3 us
    all_to_all x3, starting transfers between devices, gather_axis(): return lax.all_to_all(spread, axis, 0, 0, tiled=False)  21 us
    ppermute x3, starting transfers between devices, seg_broadcast(): got = lax.ppermute(mine, 'zh', [(0, b)])  19.5 us
    ppermute x3, starting transfers between devices, seg_broadcast(): got = lax.ppermute(pieces[:, k], 'x', [(0, k)])  7.25 us
    all_to_all x1, starting transfers between devices, shards(): lax.all_to_all(context_part, 'dp', 0, 0, tiled=False)  6.53 us
    all_to_all x1, blocking collectives, gather_axis(): return lax.all_to_all(spread, axis, 0, 0, tiled=False)  6.3 us
  transfers between devices with their start and end apart: 17, of which 9 were waited for; matrix products, arithmetic and copies ran while one was open for 8% of the time, Pallas kernels for 0%

profile of v9, /device:TPU:136, one launch (start us, length us, event | category | flops | bytes accessed | tf_op | source)
XLA Modules:
  0.0 221.3 jit_solution(12792260017229819585)
XLA Ops:
  0.0 0.9 constant_dynamic-slice_fusion
  0.9 4.7 %collective-permute-start = (bf16[2,32,256]{2,1,0:T(8,128)(2,1)S(1)}, bf16[2,32,256]{2,1,0:T(8,128)(2,1)S(1)}, u32[]{:S(2)}, u32[]{:S(2)}) collective-permute-start(bf16[2,32,256]{2,1,0:T(8,128)(2,1)S(1)} %get-tuple-element.28), channel_id=1, source_target_pairs={{0,192},{1,193},{2,194},{3,195},{4,196},{5,197},{6,198},{7,199},{8... | collective-permute-start | bytes 98312 | tf_op jit(solution)/shard_map/ppermute | solution.py:31
  5.6 1.3 collective-permute-start.1
  6.9 1.3 collective-permute-start.2
  8.2 5.2 %fusion.33 = (bf16[4096,1,256]{2,0,1:T(8,128)(2,1)S(1)}, bf16[4096,1,256]{2,0,1:T(8,128)(2,1)}, bf16[4096,256]{1,0:T(8,128)(2,1)}) fusion(bf16[4096,3,256]{2,0,1:T(8,128)(2,1)} %bitcast.163), kind=kLoop, calls=%fused_computation.66 | loop fusion | bytes 12582912 | tf_op jit(solution)/shard_map/slice | solution.py:134
  13.5 16.4 %collective-permute-start.3 = (bf16[2,32,256]{2,1,0:T(8,128)(2,1)S(1)}, bf16[2,32,256]{2,1,0:T(8,128)(2,1)S(1)}, u32[]{:S(2)}, u32[]{:S(2)}) collective-permute-start(bf16[2,32,256]{2,1,0:T(8,128)(2,1)S(1)} %fusion.30), channel_id=1, source_target_pairs={{0,768},{1,769},{2,770},{3,771},{4,772},{5,773},{6,774},{7,775},{8... | collective-permute-start | bytes 98312 | tf_op jit(solution)/shard_map/ppermute | solution.py:36
  29.9 1.8 collective-permute-start.4
  31.7 1.3 collective-permute-start.5
  33.0 2.1 collective-permute-done.4
  35.2 0.3 collective-permute-done.5
  35.5 1.1 broadcast_in_dim.11
  36.6 7.7 %all-to-all-start.1 = ((bf16[32,2,32,256]{3,2,1,0:T(8,128)(2,1)}), bf16[32,2,32,256]{3,2,1,0:T(8,128)(2,1)S(1)}, u32[]{:S(2)}, u32[]{:S(2)}) async-start(bf16[32,2,32,256]{3,2,1,0:T(8,128)(2,1)} %broadcast_in_dim.11), calls=%async_computation.1 | async-start | bytes 2097152 | tf_op jit(solution)/shard_map/all_to_all | solution.py:21
  44.4 3.0 %convolution_convert_fusion = bf16[256,256]{1,0:T(8,128)(2,1)S(1)} fusion(bf16[256,4096]{1,0:T(8,128)(2,1)} %bitcast.184, bf16[4096,256]{1,0:T(8,128)(2,1)} %get-tuple-element.10), kind=kOutput, calls=%fused_computation.17 | convolution fusion | flops 536936448 | bytes 4325376 | tf_op jit(solution)/shard_map/dot_general | solution.py:80
  47.3 0.7 pad_maximum_fusion
  48.1 1.1 copy.206
  49.2 22.8 %all-to-all-done.1 = bf16[32,2,32,256]{3,2,1,0:T(8,128)(2,1)S(1)} async-done(((bf16[32,2,32,256]{3,2,1,0:T(8,128)(2,1)}), bf16[32,2,32,256]{3,2,1,0:T(8,128)(2,1)S(1)}, u32[]{:S(2)}, u32[]{:S(2)}) %all-to-all-start.1) | async-done | bytes 1048608 | tf_op jit(solution)/shard_map/all_to_all | solution.py:21
  72.0 0.3 broadcast_in_dim.12
  72.2 6.3 %all_to_all.35 = bf16[2,32,2,32,256]{4,3,2,1,0:T(8,128)(2,1)} all-to-all(bf16[2,32,2,32,256]{4,3,2,1,0:T(8,128)(2,1)S(1)} %broadcast_in_dim.12), channel_id=1, replica_groups=mesh['zh'=4,'x'=4,'dp'=4,'ty'=8,'tc'=2] {'tc'}, dimensions={0} | all-to-all | bytes 4194304 | tf_op jit(solution)/shard_map/all_to_all | solution.py:21
  78.5 1.2 broadcast_in_dim.10
  79.7 6.7 %all-to-all-start = ((bf16[4,2,2,128,256]{3,4,2,1,0:T(8,128)(2,1)}), bf16[4,2,2,128,256]{3,4,2,1,0:T(8,128)(2,1)S(1)}, u32[]{:S(2)}, u32[]{:S(2)}) async-start(bf16[4,2,2,128,256]{3,4,2,1,0:T(8,128)(2,1)} %broadcast_in_dim.10), calls=%async_computation | async-start | bytes 2097152 | tf_op jit(solution)/shard_map/all_to_all | solution.py:21
  86.4 2.9 %fusion = bf16[4,2,32,256,1,1]{3,2,5,0,1,4:T(8,128)(2,1)S(1)} fusion(bf16[8,2,256,256,1,1]{3,2,1,0,5,4:T(8,128)(2,1)} %bitcast.161, bf16[2,4,8,2,32,256]{5,4,3,2,1,0:T(8,128)(2,1)} %bitcast.165), kind=kOutput, calls=%fused_computation.2 | convolution fusion | flops 536870912 | bytes 4325376 | tf_op jit(solution)/shard_map/cxymrf,ycfn->mxrn/dot_general | solution.py:92
  89.4 0.2 reshape.61
  89.6 0.2 copy.245
  89.7 2.3 %fusion.2 = bf16[4,2,32,256,1,1]{3,2,5,0,1,4:T(8,128)(2,1)S(1)} fusion(bf16[8,2,256,256,1,1]{3,2,1,0,5,4:T(8,128)(2,1)S(1)} %bitcast.159, bf16[2,4,8,2,32,256]{5,4,3,2,1,0:T(8,128)(2,1)} %bitcast.166), kind=kOutput, calls=%fused_computation.4 | convolution fusion | flops 536870912 | bytes 4325376 | tf_op jit(solution)/shard_map/cxymrf,ycfn->mxrn/dot_general | solution.py:92
  92.1 0.2 reshape.60
  92.2 16.9 %all-to-all-done = bf16[4,2,2,128,256]{3,4,2,1,0:T(8,128)(2,1)S(1)} async-done(((bf16[4,2,2,128,256]{3,4,2,1,0:T(8,128)(2,1)}), bf16[4,2,2,128,256]{3,4,2,1,0:T(8,128)(2,1)S(1)}, u32[]{:S(2)}, u32[]{:S(2)}) %all-to-all-start) | async-done | bytes 1048608 | tf_op jit(solution)/shard_map/all_to_all | solution.py:21
  109.2 0.1 fusion.34
  109.3 0.8 copy-done.7
  110.1 0.4 multiply_reduce_fusion.1
  110.5 2.0 fusion.4
  112.5 0.7 broadcast_in_dim.13
  113.2 6.6 %all-to-all-start.3 = ((f32[4,3,2,4,4,128]{5,4,3,2,1,0:T(4,128)}), f32[4,3,2,4,4,128]{5,4,3,2,1,0:T(4,128)S(1)}, u32[]{:S(2)}, u32[]{:S(2)}) async-start(f32[4,3,2,4,4,128]{5,4,3,2,1,0:T(4,128)} %broadcast_in_dim.13), calls=%async_computation.3 | async-start | bytes 393216 | tf_op jit(solution)/shard_map/all_to_all | solution.py:21
  119.8 4.3 %all-to-all-done.3 = f32[4,3,2,4,4,128]{5,4,3,2,1,0:T(4,128)S(1)} async-done(((f32[4,3,2,4,4,128]{5,4,3,2,1,0:T(4,128)}), f32[4,3,2,4,4,128]{5,4,3,2,1,0:T(4,128)S(1)}, u32[]{:S(2)}, u32[]{:S(2)}) %all-to-all-start.3) | async-done | bytes 196640 | tf_op jit(solution)/shard_map/all_to_all | solution.py:21
  124.2 2.5 %fusion.18 = (bf16[2,4,4,128,128]{3,4,2,1,0:T(8,128)(2,1)S(1)}, bf16[2,4,4,128,128]{3,4,2,1,0:T(8,128)(2,1)S(1)}) fusion(f32[2,4,4,128]{3,2,1,0:T(4,128)S(1)} %get-tuple-element.15, f32[2,4,4,128]{3,2,1,0:T(4,128)S(1)} %bitcast_reduce_fusion, f32[2,4,4,128,128]{3,4,2,1,0:T(8,128)S(1)} %get-tuple-element.30, f32[2,4,4,128,128]{3,4,2,1,0:T(8,128)} %get-tuple-element.31, ...), kind=kLoop, calls=%fused_computation.29 | loop fusion | flops 4194304 | bytes 6340608 | tf_op jit(solution)/shard_map/convert_element_type | solution.py:118
  126.7 0.5 fusion.8
  127.2 0.9 copy-done.8
  128.1 0.5 fusion.10
  128.6 0.2 copy-done.1
  128.8 0.8 fusion.35
  129.6 0.8 copy-done.2
  130.4 0.8 fusion.7
  131.2 0.1 copy.225
  131.3 5.4 %all_to_all.36 = bf16[2,2,128,8,256]{4,2,3,1,0:T(8,128)(2,1)S(1)} all-to-all(bf16[2,2,128,8,256]{4,2,3,1,0:T(8,128)(2,1)S(1)} %copy.225), channel_id=1, replica_groups=mesh['zh'=4,'x'=4,'dp'=4,'ty'=8,'tc'=2] {'tc'}, dimensions={0} | all-to-all | bytes 4194304 | tf_op jit(solution)/shard_map/all_to_all | solution.py:140
  136.7 0.7 reduce_sum.70
  137.4 0.1 broadcast_select_fusion
  137.5 1.1 copy.228
  138.6 5.2 %all-to-all-start.5 = ((bf16[32,2,32,256]{3,2,1,0:T(8,128)(2,1)}), bf16[32,2,32,256]{3,2,1,0:T(8,128)(2,1)S(1)}, u32[]{:S(2)}, u32[]{:S(2)}) async-start(bf16[32,2,32,256]{3,2,1,0:T(8,128)(2,1)} %bitcast.46), calls=%async_computation.5 | async-start | bytes 2097152 | tf_op jit(solution)/shard_map/all_to_all | solution.py:148
  143.8 0.3 convolution_bitcast_fusion
  144.1 1.1 copy.236
  145.2 27.4 %all-to-all-done.5 = bf16[32,2,32,256]{3,2,1,0:T(8,128)(2,1)S(1)} async-done(((bf16[32,2,32,256]{3,2,1,0:T(8,128)(2,1)}), bf16[32,2,32,256]{3,2,1,0:T(8,128)(2,1)S(1)}, u32[]{:S(2)}, u32[]{:S(2)}) %all-to-all-start.5) | async-done | bytes 1048608 | tf_op jit(solution)/shard_map/all_to_all | solution.py:148
  172.6 6.5 %all-to-all-start.6 = ((f32[4,2,128,256]{2,3,1,0:T(8,128)}), f32[4,2,128,256]{2,3,1,0:T(8,128)S(1)}, u32[]{:S(2)}, u32[]{:S(2)}) async-start(f32[4,2,128,256]{2,3,1,0:T(8,128)} %bitcast.57), calls=%async_computation.6 | async-start | bytes 2097152 | tf_op jit(solution)/shard_map/all_to_all | solution.py:124
  179.1 0.2 convert_reduce_fusion
  179.3 1.3 collective-permute-start.6
  180.6 1.3 collective-permute-start.7
  181.9 1.3 collective-permute-start.8
  183.2 27.3 %collective-permute-done.6 = bf16[2,32,256]{2,1,0:T(8,128)(2,1)S(1)} collective-permute-done((bf16[2,32,256]{2,1,0:T(8,128)(2,1)S(1)}, bf16[2,32,256]{2,1,0:T(8,128)(2,1)S(1)}, u32[]{:S(2)}, u32[]{:S(2)}) %collective-permute-start.6) | collective-permute-done | bytes 32800 | tf_op jit(solution)/shard_map/ppermute | solution.py:46
  210.5 1.3 collective-permute-start.10
  211.8 0.1 copy.232
  212.0 1.3 collective-permute-start.9
  213.3 1.3 collective-permute-start.11
  214.6 3.3 %collective-permute-done.10 = bf16[2,32,256]{2,1,0:T(8,128)(2,1)S(1)} collective-permute-done((bf16[2,32,256]{2,1,0:T(8,128)(2,1)S(1)}, bf16[2,32,256]{2,1,0:T(8,128)(2,1)S(1)}, u32[]{:S(2)}, u32[]{:S(2)}) %collective-permute-start.10) | collective-permute-done | bytes 32800 | tf_op jit(solution)/shard_map/ppermute | solution.py:52
  217.9 2.4 %collective-permute-done.11 = bf16[2,32,256]{2,1,0:T(8,128)(2,1)S(1)} collective-permute-done((bf16[2,32,256]{2,1,0:T(8,128)(2,1)S(1)}, bf16[2,32,256]{2,1,0:T(8,128)(2,1)S(1)}, u32[]{:S(2)}, u32[]{:S(2)}) %collective-permute-start.11) | collective-permute-done | bytes 32800 | tf_op jit(solution)/shard_map/ppermute | solution.py:52
  220.3 0.1 copy.233
  220.6 0.8 copy.237
  (47 shorter events, 0.4 us)
Async XLA Ops:
  0.9 12.5 %collective-permute-start = (bf16[2,32,256]{2,1,0:T(8,128)(2,1)S(1)}, bf16[2,32,256]{2,1,0:T(8,128)(2,1)S(1)}, u32[]{:S(2)}, u32[]{:S(2)}) collective-permute-start(bf16[2,32,256]{2,1,0:T(8,128)(2,1)S(1)} %get-tuple-element.28), channel_id=1, source_target_pairs={{0,192},{1,193},{2,194},{3,195},{4,196},{5,197},{6,198},{7,199},{8... | collective-permute-start | bytes 98312 | tf_op jit(solution)/shard_map/ppermute | solution.py:31
  5.6 7.8 %collective-permute-start.1 = (bf16[2,32,256]{2,1,0:T(8,128)(2,1)S(1)}, bf16[2,32,256]{2,1,0:T(8,128)(2,1)S(1)}, u32[]{:S(2)}, u32[]{:S(2)}) collective-permute-start(bf16[2,32,256]{2,1,0:T(8,128)(2,1)S(1)} %get-tuple-element.27), channel_id=1, source_target_pairs={{0,128},{1,129},{2,130},{3,131},{4,132},{5,133},{6,134},{7,135},{8... | collective-permute-start | bytes 98312 | tf_op jit(solution)/shard_map/ppermute | solution.py:31
  6.9 6.5 %collective-permute-start.2 = (bf16[2,32,256]{2,1,0:T(8,128)(2,1)S(1)}, bf16[2,32,256]{2,1,0:T(8,128)(2,1)S(1)}, u32[]{:S(2)}, u32[]{:S(2)}) collective-permute-start(bf16[2,32,256]{2,1,0:T(8,128)(2,1)S(1)} %get-tuple-element.26), channel_id=1, source_target_pairs={{0,64},{1,65},{2,66},{3,67},{4,68},{5,69},{6,70},{7,71},{8,72},{9,... | collective-permute-start | bytes 98312 | tf_op jit(solution)/shard_map/ppermute | solution.py:31
  13.4 76.3 %copy-start = (bf16[4096,1,256]{2,0,1:T(8,128)(2,1)}, bf16[4096,1,256]{2,0,1:T(8,128)(2,1)S(1)}, u32[]{:S(2)}) copy-start(bf16[4096,1,256]{2,0,1:T(8,128)(2,1)S(1)} %get-tuple-element.17) | copy-start | bytes 6291460
  13.5 19.6 %collective-permute-start.3 = (bf16[2,32,256]{2,1,0:T(8,128)(2,1)S(1)}, bf16[2,32,256]{2,1,0:T(8,128)(2,1)S(1)}, u32[]{:S(2)}, u32[]{:S(2)}) collective-permute-start(bf16[2,32,256]{2,1,0:T(8,128)(2,1)S(1)} %fusion.30), channel_id=1, source_target_pairs={{0,768},{1,769},{2,770},{3,771},{4,772},{5,773},{6,774},{7,775},{8... | collective-permute-start | bytes 98312 | tf_op jit(solution)/shard_map/ppermute | solution.py:36
  29.9 5.3 %collective-permute-start.4 = (bf16[2,32,256]{2,1,0:T(8,128)(2,1)S(1)}, bf16[2,32,256]{2,1,0:T(8,128)(2,1)S(1)}, u32[]{:S(2)}, u32[]{:S(2)}) collective-permute-start(bf16[2,32,256]{2,1,0:T(8,128)(2,1)S(1)} %fusion.30), channel_id=1, source_target_pairs={{0,512},{1,513},{2,514},{3,515},{4,516},{5,517},{6,518},{7,519},{8... | collective-permute-start | bytes 98312 | tf_op jit(solution)/shard_map/ppermute | solution.py:36
  31.7 3.8 %collective-permute-start.5 = (bf16[2,32,256]{2,1,0:T(8,128)(2,1)S(1)}, bf16[2,32,256]{2,1,0:T(8,128)(2,1)S(1)}, u32[]{:S(2)}, u32[]{:S(2)}) collective-permute-start(bf16[2,32,256]{2,1,0:T(8,128)(2,1)S(1)} %fusion.30), channel_id=1, source_target_pairs={{0,256},{1,257},{2,258},{3,259},{4,260},{5,261},{6,262},{7,263},{8... | collective-permute-start | bytes 98312 | tf_op jit(solution)/shard_map/ppermute | solution.py:36
  36.6 35.3 %all-to-all-start.1 = ((bf16[32,2,32,256]{3,2,1,0:T(8,128)(2,1)}), bf16[32,2,32,256]{3,2,1,0:T(8,128)(2,1)S(1)}, u32[]{:S(2)}, u32[]{:S(2)}) async-start(bf16[32,2,32,256]{3,2,1,0:T(8,128)(2,1)} %broadcast_in_dim.11), calls=%async_computation.1 | async-start | bytes 2097152 | tf_op jit(solution)/shard_map/all_to_all | solution.py:21
  44.4 3.0 %copy-start.9 = (bf16[1,2,128,256]{3,2,1,0:T(8,128)(2,1)S(1)}, bf16[1,2,128,256]{3,2,1,0:T(8,128)(2,1)}, u32[]{:S(2)}) copy-start(bf16[1,2,128,256]{3,2,1,0:T(8,128)(2,1)} %param.5) | copy-start | bytes 393220
  79.7 29.4 %all-to-all-start = ((bf16[4,2,2,128,256]{3,4,2,1,0:T(8,128)(2,1)}), bf16[4,2,2,128,256]{3,4,2,1,0:T(8,128)(2,1)S(1)}, u32[]{:S(2)}, u32[]{:S(2)}) async-start(bf16[4,2,2,128,256]{3,4,2,1,0:T(8,128)(2,1)} %broadcast_in_dim.10), calls=%async_computation | async-start | bytes 2097152 | tf_op jit(solution)/shard_map/all_to_all | solution.py:21
  109.3 0.8 copy-start.7
  109.3 3.2 %copy-start.5 = (bf16[4,1,2,128,256]{3,4,2,1,0:T(8,128)(2,1)}, bf16[4,1,2,128,256]{3,4,2,1,0:T(8,128)(2,1)S(1)}, u32[]{:S(2)}) copy-start(bf16[4,1,2,128,256]{3,4,2,1,0:T(8,128)(2,1)S(1)} %get-tuple-element.23) | copy-start | bytes 1572868
  113.2 10.9 %all-to-all-start.3 = ((f32[4,3,2,4,4,128]{5,4,3,2,1,0:T(4,128)}), f32[4,3,2,4,4,128]{5,4,3,2,1,0:T(4,128)S(1)}, u32[]{:S(2)}, u32[]{:S(2)}) async-start(f32[4,3,2,4,4,128]{5,4,3,2,1,0:T(4,128)} %broadcast_in_dim.13), calls=%async_computation.3 | async-start | bytes 393216 | tf_op jit(solution)/shard_map/all_to_all | solution.py:21
  124.2 2.5 %copy-start.6 = (bf16[4,1,2,128,256]{3,4,2,1,0:T(8,128)(2,1)S(1)}, bf16[4,1,2,128,256]{3,4,2,1,0:T(8,128)(2,1)}, u32[]{:S(2)}) copy-start(bf16[4,1,2,128,256]{3,4,2,1,0:T(8,128)(2,1)} %copy-done.5) | copy-start | bytes 1572868
  126.7 1.9 copy-start.3
  126.7 1.4 copy-start.8
  126.7 2.1 copy-start.1
  128.8 1.6 copy-start.2
  137.5 6.3 %copy-start.4 = (bf16[2,4,4,128,128]{3,4,2,1,0:T(8,128)(2,1)S(1)}, bf16[2,4,4,128,128]{3,4,2,1,0:T(8,128)(2,1)}, u32[]{:S(2)}) copy-start(bf16[2,4,4,128,128]{3,4,2,1,0:T(8,128)(2,1)} %copy-done.3) | copy-start | bytes 3145732
  138.6 34.0 %all-to-all-start.5 = ((bf16[32,2,32,256]{3,2,1,0:T(8,128)(2,1)}), bf16[32,2,32,256]{3,2,1,0:T(8,128)(2,1)S(1)}, u32[]{:S(2)}, u32[]{:S(2)}) async-start(bf16[32,2,32,256]{3,2,1,0:T(8,128)(2,1)} %bitcast.46), calls=%async_computation.5 | async-start | bytes 2097152 | tf_op jit(solution)/shard_map/all_to_all | solution.py:148
  145.2 66.6 %copy-start.10 = (bf16[1,2,128,256]{3,2,1,0:T(8,128)(2,1)S(1)}, bf16[1,2,128,256]{3,2,1,0:T(8,128)(2,1)}, u32[]{:S(2)}) copy-start(bf16[1,2,128,256]{3,2,1,0:T(8,128)(2,1)} %param.5) | copy-start | bytes 393220
  172.6 47.9 %all-to-all-start.6 = ((f32[4,2,128,256]{2,3,1,0:T(8,128)}), f32[4,2,128,256]{2,3,1,0:T(8,128)S(1)}, u32[]{:S(2)}, u32[]{:S(2)}) async-start(f32[4,2,128,256]{2,3,1,0:T(8,128)} %bitcast.57), calls=%async_computation.6 | async-start | bytes 2097152 | tf_op jit(solution)/shard_map/all_to_all | solution.py:124
  179.3 31.2 %collective-permute-start.6 = (bf16[2,32,256]{2,1,0:T(8,128)(2,1)S(1)}, bf16[2,32,256]{2,1,0:T(8,128)(2,1)S(1)}, u32[]{:S(2)}, u32[]{:S(2)}) collective-permute-start(bf16[2,32,256]{2,1,0:T(8,128)(2,1)S(1)} %convert_element_type.97), channel_id=1, source_target_pairs={{256,0},{257,1},{258,2},{259,3},{260,4},{261,5},{262,6},{263,7},{2... | collective-permute-start | bytes 98312 | tf_op jit(solution)/shard_map/ppermute | solution.py:46
  180.6 29.9 %collective-permute-start.7 = (bf16[2,32,256]{2,1,0:T(8,128)(2,1)S(1)}, bf16[2,32,256]{2,1,0:T(8,128)(2,1)S(1)}, u32[]{:S(2)}, u32[]{:S(2)}) collective-permute-start(bf16[2,32,256]{2,1,0:T(8,128)(2,1)S(1)} %convert_element_type.97), channel_id=1, source_target_pairs={{512,0},{513,1},{514,2},{515,3},{516,4},{517,5},{518,6},{519,7},{5... | collective-permute-start | bytes 98312 | tf_op jit(solution)/shard_map/ppermute | solution.py:46
  181.9 28.6 %collective-permute-start.8 = (bf16[2,32,256]{2,1,0:T(8,128)(2,1)S(1)}, bf16[2,32,256]{2,1,0:T(8,128)(2,1)S(1)}, u32[]{:S(2)}, u32[]{:S(2)}) collective-permute-start(bf16[2,32,256]{2,1,0:T(8,128)(2,1)S(1)} %convert_element_type.97), channel_id=1, source_target_pairs={{768,0},{769,1},{770,2},{771,3},{772,4},{773,5},{774,6},{775,7},{7... | collective-permute-start | bytes 98312 | tf_op jit(solution)/shard_map/ppermute | solution.py:46
  210.5 7.3 %collective-permute-start.10 = (bf16[2,32,256]{2,1,0:T(8,128)(2,1)S(1)}, bf16[2,32,256]{2,1,0:T(8,128)(2,1)S(1)}, u32[]{:S(2)}, u32[]{:S(2)}) collective-permute-start(bf16[2,32,256]{2,1,0:T(8,128)(2,1)S(1)} %get-tuple-element.25), channel_id=1, source_target_pairs={{128,0},{129,1},{130,2},{131,3},{132,4},{133,5},{134,6},{135,7},{1... | collective-permute-start | bytes 98312 | tf_op jit(solution)/shard_map/ppermute | solution.py:52
  212.0 5.9 %collective-permute-start.9 = (bf16[2,32,256]{2,1,0:T(8,128)(2,1)S(1)}, bf16[2,32,256]{2,1,0:T(8,128)(2,1)S(1)}, u32[]{:S(2)}, u32[]{:S(2)}) collective-permute-start(bf16[2,32,256]{2,1,0:T(8,128)(2,1)S(1)} %get-tuple-element.25), channel_id=1, source_target_pairs={{64,0},{65,1},{66,2},{67,3},{68,4},{69,5},{70,6},{71,7},{72,8},{73... | collective-permute-start | bytes 98312 | tf_op jit(solution)/shard_map/ppermute | solution.py:52
  213.3 7.0 %collective-permute-start.11 = (bf16[2,32,256]{2,1,0:T(8,128)(2,1)S(1)}, bf16[2,32,256]{2,1,0:T(8,128)(2,1)S(1)}, u32[]{:S(2)}, u32[]{:S(2)}) collective-permute-start(bf16[2,32,256]{2,1,0:T(8,128)(2,1)S(1)} %get-tuple-element.25), channel_id=1, source_target_pairs={{192,0},{193,1},{194,2},{195,3},{196,4},{197,5},{198,6},{199,7},{2... | collective-permute-start | bytes 98312 | tf_op jit(solution)/shard_map/ppermute | solution.py:52

commit v10 on v8

--- a/solution.py
+++ b/solution.py
@@ -22,14 +22,10 @@
 
 
 def seg_broadcast(value, n_hi, n_x):
-    x = lax.axis_index("x")
     zh = lax.axis_index("zh")
     quarter = value.shape[1] // n_x
     pieces = value.reshape(value.shape[0], n_x, quarter, value.shape[2])
-    mine = pieces[:, 0]
-    for k in range(1, n_x):
-        got = lax.ppermute(pieces[:, k], "x", [(0, k)])
-        mine = jnp.where(x == k, got, mine)
+    mine = lax.all_to_all(jnp.moveaxis(pieces, 1, 0), "x", 0, 0, tiled=False)[0]
     out = mine
     for b in range(1, n_hi):
         got = lax.ppermute(mine, "zh", [(0, b)])
@@ -45,11 +41,9 @@
         got = lax.ppermute(sent, "zh", [(b, 0)])
         acc = acc + got.astype(jnp.float32)
     acc = jnp.where(zh == 0, acc, mine)
-    parts = [acc]
-    sent = acc.astype(jnp.bfloat16)
-    for k in range(1, n_x):
-        parts.append(lax.ppermute(sent, "x", [(k, 0)]).astype(jnp.float32))
-    stacked = jnp.stack(parts, axis=1)
+    parts = gather_axis(acc.astype(jnp.bfloat16), "x", n_x).astype(jnp.float32)
+    parts = jnp.where(jnp.arange(n_x)[:, None, None, None] == 0, acc[None], parts)
+    stacked = jnp.moveaxis(parts, 0, 1)
     return stacked.reshape(stacked.shape[0], -1, stacked.shape[-1])
 
 

time: 216 us -> 220 us (1.019)
  the two profiles are of different devices: /device:TPU:72 before, /device:TPU:56 now
where the time goes in v10:
time: 220 us; the launch traced here: 219 us
  waiting for transfers between devices  79.8 us (36%)
  starting transfers between devices  53 us (24%)
  blocking collectives  46.2 us (21%)
  local copies, waits for them, and re-layouts  19.7 us (9%)
  matrix products  12.1 us (6%)
  other arithmetic  7.4 us (3%)
    all_to_all x4, waiting for transfers between devices, gather_axis(): return lax.all_to_all(spread, axis, 0, 0, tiled=False)  37.6 us
    all_to_all x1, blocking collectives, shards(): lax.all_to_all(pair_sum, ('x', 'ty'), 0, 0, tiled=False).astype(jnp.float32)  34.3 us
    all_to_all x4, starting transfers between devices, gather_axis(): return lax.all_to_all(spread, axis, 0, 0, tiled=False)  22.1 us
    all_to_all x1, waiting for transfers between devices, shards(): lax.all_to_all(context_part, 'dp', 0, 0, tiled=False)  21.6 us
    ppermute x3, starting transfers between devices, seg_broadcast(): got = lax.ppermute(mine, 'zh', [(0, b)])  18.6 us
    ppermute x3, waiting for transfers between devices, seg_reduce(): got = lax.ppermute(sent, 'zh', [(b, 0)])  15.6 us
    all_to_all x1, blocking collectives, shards(): lax.all_to_all(head_terms, 'tc', 0, 0, tiled=False).astype(jnp.float32)  6.3 us
    all_to_all x1, blocking collectives, gather_axis(): return lax.all_to_all(spread, axis, 0, 0, tiled=False)  5.55 us
  transfers between devices with their start and end apart: 12, of which 11 were waited for; matrix products, arithmetic and copies ran while one was open for 6% of the time, Pallas kernels for 0%

profile of v10, /device:TPU:56, one launch (start us, length us, event | category | flops | bytes accessed | tf_op | source)
XLA Modules:
  0.0 218.7 jit_solution(1584923368097636694)
XLA Ops:
  0.0 1.6 copy-done
  1.6 0.7 copy.170
  2.3 4.3 %all-to-all-start.1 = ((bf16[4,2,32,256]{3,2,1,0:T(8,128)(2,1)}), bf16[4,2,32,256]{3,2,1,0:T(8,128)(2,1)S(1)}, u32[]{:S(2)}, u32[]{:S(2)}) async-start(bf16[4,2,32,256]{3,2,1,0:T(8,128)(2,1)} %copy.170), calls=%async_computation.1 | async-start | bytes 262144 | tf_op jit(solution)/shard_map/all_to_all | solution.py:28
  6.6 2.3 %fusion.9 = bf16[256,256]{1,0:T(8,128)(2,1)S(1)} fusion(bf16[256,4096]{1,0:T(8,128)(2,1)S(1)} %bitcast.123, bf16[4096,3,256]{2,0,1:T(8,128)(2,1)} %bitcast.130), kind=kOutput, calls=%fused_computation.18 | convolution fusion | flops 536936448 | bytes 4325376 | tf_op jit(solution)/shard_map/dot_general | solution.py:70
  9.0 0.2 copy.169
  9.1 3.4 %all-to-all-done.1 = bf16[4,2,32,256]{3,2,1,0:T(8,128)(2,1)S(1)} async-done(((bf16[4,2,32,256]{3,2,1,0:T(8,128)(2,1)}), bf16[4,2,32,256]{3,2,1,0:T(8,128)(2,1)S(1)}, u32[]{:S(2)}, u32[]{:S(2)}) %all-to-all-start.1) | async-done | bytes 131104 | tf_op jit(solution)/shard_map/all_to_all | solution.py:28
  12.5 1.2 broadcast_in_dim.23
  13.7 7.3 %all-to-all-start = ((bf16[4,2,2,128,256]{3,4,2,1,0:T(8,128)(2,1)}), bf16[4,2,2,128,256]{3,4,2,1,0:T(8,128)(2,1)S(1)}, u32[]{:S(2)}, u32[]{:S(2)}) async-start(bf16[4,2,2,128,256]{3,4,2,1,0:T(8,128)(2,1)} %broadcast_in_dim.23), calls=%async_computation | async-start | bytes 2097152 | tf_op jit(solution)/shard_map/all_to_all | solution.py:21
  21.0 15.5 %collective-permute-start = (bf16[2,32,256]{2,1,0:T(8,128)(2,1)S(1)}, bf16[2,32,256]{2,1,0:T(8,128)(2,1)S(1)}, u32[]{:S(2)}, u32[]{:S(2)}) collective-permute-start(bf16[2,32,256]{2,1,0:T(8,128)(2,1)S(1)} %slice_bitcast_fusion.6), channel_id=1, source_target_pairs={{0,768},{1,769},{2,770},{3,771},{4,772},{5,773},{6,774},{7,775},{8... | collective-permute-start | bytes 98312 | tf_op jit(solution)/shard_map/ppermute | solution.py:31
  36.5 1.8 collective-permute-start.1
  38.3 1.3 collective-permute-start.2
  39.6 0.3 collective-permute-done.1
  39.9 1.3 collective-permute-done.2
  41.2 5.9 %all-to-all-done = bf16[4,2,2,128,256]{3,4,2,1,0:T(8,128)(2,1)S(1)} async-done(((bf16[4,2,2,128,256]{3,4,2,1,0:T(8,128)(2,1)}), bf16[4,2,2,128,256]{3,4,2,1,0:T(8,128)(2,1)S(1)}, u32[]{:S(2)}, u32[]{:S(2)}) %all-to-all-start) | async-done | bytes 1048608 | tf_op jit(solution)/shard_map/all_to_all | solution.py:21
  47.1 1.2 broadcast_in_dim.24
  48.3 0.1 copy-done.5
  48.4 7.6 %all-to-all-start.2 = ((bf16[32,2,32,256]{3,2,1,0:T(8,128)(2,1)}), bf16[32,2,32,256]{3,2,1,0:T(8,128)(2,1)S(1)}, u32[]{:S(2)}, u32[]{:S(2)}) async-start(bf16[32,2,32,256]{3,2,1,0:T(8,128)(2,1)} %broadcast_in_dim.24), calls=%async_computation.2 | async-start | bytes 2097152 | tf_op jit(solution)/shard_map/all_to_all | solution.py:21
  56.1 4.5 %fusion.31 = (bf16[4096,1,256]{2,0,1:T(8,128)(2,1)}, bf16[4096,1,256]{2,0,1:T(8,128)(2,1)}) fusion(bf16[4096,3,256]{2,0,1:T(8,128)(2,1)} %bitcast.131), kind=kLoop, calls=%fused_computation.58 | loop fusion | bytes 8388608 | tf_op jit(solution)/shard_map/slice | solution.py:128
  60.6 1.1 fusion.32
  61.7 19.1 %all-to-all-done.2 = bf16[32,2,32,256]{3,2,1,0:T(8,128)(2,1)S(1)} async-done(((bf16[32,2,32,256]{3,2,1,0:T(8,128)(2,1)}), bf16[32,2,32,256]{3,2,1,0:T(8,128)(2,1)S(1)}, u32[]{:S(2)}, u32[]{:S(2)}) %all-to-all-start.2) | async-done | bytes 1048608 | tf_op jit(solution)/shard_map/all_to_all | solution.py:21
  80.8 0.3 broadcast_in_dim.25
  81.1 5.5 %all_to_all.45 = bf16[2,32,2,32,256]{4,3,2,1,0:T(8,128)(2,1)S(1)} all-to-all(bf16[2,32,2,32,256]{4,3,2,1,0:T(8,128)(2,1)S(1)} %broadcast_in_dim.25), channel_id=1, replica_groups=mesh['zh'=4,'x'=4,'dp'=4,'ty'=8,'tc'=2] {'tc'}, dimensions={0} | all-to-all | bytes 4194304 | tf_op jit(solution)/shard_map/all_to_all | solution.py:21
  86.7 0.7 fusion.3
  87.4 0.6 copy-done.9
  88.0 0.9 reshape.63
  88.9 3.0 %fusion.1 = bf16[4,2,32,256,1,1]{3,2,5,0,1,4:T(8,128)(2,1)S(1)} fusion(bf16[8,2,256,256,1,1]{3,2,1,0,5,4:T(8,128)(2,1)} %bitcast.126, bf16[2,4,8,2,32,256]{5,4,3,2,1,0:T(8,128)(2,1)} %bitcast.133), kind=kOutput, calls=%fused_computation.3 | convolution fusion | flops 536870912 | bytes 4325376 | tf_op jit(solution)/shard_map/cxymrf,ycfn->mxrn/dot_general | solution.py:86
  91.9 0.2 reshape.64
  92.1 0.2 copy.207
  92.3 1.4 multiply_reduce_fusion.1
  93.7 2.0 fusion.5
  95.6 0.7 broadcast_in_dim.26
  96.4 3.4 %all-to-all-start.4 = ((f32[4,3,2,4,4,128]{5,4,3,2,1,0:T(4,128)}), f32[4,3,2,4,4,128]{5,4,3,2,1,0:T(4,128)S(1)}, u32[]{:S(2)}, u32[]{:S(2)}) async-start(f32[4,3,2,4,4,128]{5,4,3,2,1,0:T(4,128)} %broadcast_in_dim.26), calls=%async_computation.4 | async-start | bytes 393216 | tf_op jit(solution)/shard_map/all_to_all | solution.py:21
  99.7 8.0 %all-to-all-done.4 = f32[4,3,2,4,4,128]{5,4,3,2,1,0:T(4,128)S(1)} async-done(((f32[4,3,2,4,4,128]{5,4,3,2,1,0:T(4,128)}), f32[4,3,2,4,4,128]{5,4,3,2,1,0:T(4,128)S(1)}, u32[]{:S(2)}, u32[]{:S(2)}) %all-to-all-start.4) | async-done | bytes 196640 | tf_op jit(solution)/shard_map/all_to_all | solution.py:21
  107.8 3.1 %fusion.20 = (bf16[2,4,4,128,128]{3,4,2,1,0:T(8,128)(2,1)S(1)}, bf16[2,4,4,128,128]{3,4,2,1,0:T(8,128)(2,1)S(1)}) fusion(f32[2,4,4,128]{3,2,1,0:T(4,128)S(1)} %get-tuple-element.11, f32[2,4,4,128]{3,2,1,0:T(4,128)S(1)} %bitcast_reduce_fusion, f32[2,4,4,128,128]{3,4,2,1,0:T(8,128)} %copy-done.1, f32[2,4,4,128,128]{3,4,2,1,0:T(8,128)} %get-tuple-element.23, ...), kind=kLoop, calls=%fused_computation.30 | loop fusion | flops 4194304 | bytes 6340608 | tf_op jit(solution)/shard_map/convert_element_type | solution.py:112
  110.9 0.5 fusion.12
  111.4 0.5 fusion.10
  112.0 0.9 copy-done.3
  112.9 0.8 fusion.33
  113.7 0.8 copy-done.4
  114.5 0.8 fusion.8
  115.3 0.1 copy.189
  115.4 6.3 %all_to_all.46 = bf16[2,2,128,8,256]{4,2,3,1,0:T(8,128)(2,1)} all-to-all(bf16[2,2,128,8,256]{4,2,3,1,0:T(8,128)(2,1)S(1)} %copy.189), channel_id=1, replica_groups=mesh['zh'=4,'x'=4,'dp'=4,'ty'=8,'tc'=2] {'tc'}, dimensions={0} | all-to-all | bytes 4194304 | tf_op jit(solution)/shard_map/all_to_all | solution.py:134
  121.7 2.1 reduce_sum.70
  123.9 0.1 copy.192
  124.0 34.3 %all_to_all.47 = bf16[32,2,32,256]{3,2,1,0:T(8,128)(2,1)S(1)} all-to-all(bf16[32,2,32,256]{3,2,1,0:T(8,128)(2,1)S(1)} %bitcast.129), channel_id=1, replica_groups=mesh['zh'=4,'x'=4,'dp'=4,'ty'=8,'tc'=2] {'x','ty'}, dimensions={0} | all-to-all | bytes 2097152 | tf_op jit(solution)/shard_map/all_to_all | solution.py:142
  158.3 0.2 convert_reduce_fusion
  158.5 1.3 collective-permute-start.3
  159.8 1.3 collective-permute-start.4
  161.1 1.3 collective-permute-start.5
  162.4 7.2 %collective-permute-done.3 = bf16[2,32,256]{2,1,0:T(8,128)(2,1)S(1)} collective-permute-done((bf16[2,32,256]{2,1,0:T(8,128)(2,1)S(1)}, bf16[2,32,256]{2,1,0:T(8,128)(2,1)S(1)}, u32[]{:S(2)}, u32[]{:S(2)}) %collective-permute-start.3) | collective-permute-done | bytes 32800 | tf_op jit(solution)/shard_map/ppermute | solution.py:41
  169.6 6.9 %collective-permute-done.4 = bf16[2,32,256]{2,1,0:T(8,128)(2,1)S(1)} collective-permute-done((bf16[2,32,256]{2,1,0:T(8,128)(2,1)S(1)}, bf16[2,32,256]{2,1,0:T(8,128)(2,1)S(1)}, u32[]{:S(2)}, u32[]{:S(2)}) %collective-permute-start.4) | collective-permute-done | bytes 32800 | tf_op jit(solution)/shard_map/ppermute | solution.py:41
  176.4 1.5 collective-permute-done.5
  178.0 0.7 broadcast_in_dim.29
  178.6 3.9 %all-to-all-start.7 = ((bf16[4,2,32,256]{3,2,1,0:T(8,128)(2,1)}), bf16[4,2,32,256]{3,2,1,0:T(8,128)(2,1)S(1)}, u32[]{:S(2)}, u32[]{:S(2)}) async-start(bf16[4,2,32,256]{3,2,1,0:T(8,128)(2,1)} %broadcast_in_dim.29), calls=%async_computation.7 | async-start | bytes 262144 | tf_op jit(solution)/shard_map/all_to_all | solution.py:21
  182.5 0.3 convolution_bitcast_fusion
  182.8 1.1 copy.198
  183.9 4.6 %all-to-all-done.7 = bf16[4,2,32,256]{3,2,1,0:T(8,128)(2,1)S(1)} async-done(((bf16[4,2,32,256]{3,2,1,0:T(8,128)(2,1)}), bf16[4,2,32,256]{3,2,1,0:T(8,128)(2,1)S(1)}, u32[]{:S(2)}, u32[]{:S(2)}) %all-to-all-start.7) | async-done | bytes 131104 | tf_op jit(solution)/shard_map/all_to_all | solution.py:21
  188.5 4.1 %all-to-all-start.8 = ((f32[4,2,128,256]{2,3,1,0:T(8,128)}), f32[4,2,128,256]{2,3,1,0:T(8,128)S(1)}, u32[]{:S(2)}, u32[]{:S(2)}) async-start(f32[4,2,128,256]{2,3,1,0:T(8,128)} %bitcast.46), calls=%async_computation.8 | async-start | bytes 2097152 | tf_op jit(solution)/shard_map/all_to_all | solution.py:118
  192.6 0.8 copy.194
  193.4 0.8 convert_select_fusion
  194.2 1.1 copy.195
  195.3 21.6 %all-to-all-done.8 = f32[4,2,128,256]{2,3,1,0:T(8,128)S(1)} async-done(((f32[4,2,128,256]{2,3,1,0:T(8,128)}), f32[4,2,128,256]{2,3,1,0:T(8,128)S(1)}, u32[]{:S(2)}, u32[]{:S(2)}) %all-to-all-start.8) | async-done | bytes 1048608 | tf_op jit(solution)/shard_map/all_to_all | solution.py:118
  216.9 1.0 fusion.22
  217.9 0.8 copy.199
  (43 shorter events, 0.4 us)
Async XLA Ops:
  0.0 1.6 copy-start
  2.3 10.3 %all-to-all-start.1 = ((bf16[4,2,32,256]{3,2,1,0:T(8,128)(2,1)}), bf16[4,2,32,256]{3,2,1,0:T(8,128)(2,1)S(1)}, u32[]{:S(2)}, u32[]{:S(2)}) async-start(bf16[4,2,32,256]{3,2,1,0:T(8,128)(2,1)} %copy.170), calls=%async_computation.1 | async-start | bytes 262144 | tf_op jit(solution)/shard_map/all_to_all | solution.py:28
  6.6 2.3 %copy-start.12 = (bf16[1,2,128,256]{3,2,1,0:T(8,128)(2,1)S(1)}, bf16[1,2,128,256]{3,2,1,0:T(8,128)(2,1)}, u32[]{:S(2)}) copy-start(bf16[1,2,128,256]{3,2,1,0:T(8,128)(2,1)} %param.5) | copy-start | bytes 393220
  13.7 33.4 %all-to-all-start = ((bf16[4,2,2,128,256]{3,4,2,1,0:T(8,128)(2,1)}), bf16[4,2,2,128,256]{3,4,2,1,0:T(8,128)(2,1)S(1)}, u32[]{:S(2)}, u32[]{:S(2)}) async-start(bf16[4,2,2,128,256]{3,4,2,1,0:T(8,128)(2,1)} %broadcast_in_dim.23), calls=%async_computation | async-start | bytes 2097152 | tf_op jit(solution)/shard_map/all_to_all | solution.py:21
  21.0 18.6 %collective-permute-start = (bf16[2,32,256]{2,1,0:T(8,128)(2,1)S(1)}, bf16[2,32,256]{2,1,0:T(8,128)(2,1)S(1)}, u32[]{:S(2)}, u32[]{:S(2)}) collective-permute-start(bf16[2,32,256]{2,1,0:T(8,128)(2,1)S(1)} %slice_bitcast_fusion.6), channel_id=1, source_target_pairs={{0,768},{1,769},{2,770},{3,771},{4,772},{5,773},{6,774},{7,775},{8... | collective-permute-start | bytes 98312 | tf_op jit(solution)/shard_map/ppermute | solution.py:31
  36.5 3.4 %collective-permute-start.1 = (bf16[2,32,256]{2,1,0:T(8,128)(2,1)S(1)}, bf16[2,32,256]{2,1,0:T(8,128)(2,1)S(1)}, u32[]{:S(2)}, u32[]{:S(2)}) collective-permute-start(bf16[2,32,256]{2,1,0:T(8,128)(2,1)S(1)} %slice_bitcast_fusion.6), channel_id=1, source_target_pairs={{0,512},{1,513},{2,514},{3,515},{4,516},{5,517},{6,518},{7,519},{8... | collective-permute-start | bytes 98312 | tf_op jit(solution)/shard_map/ppermute | solution.py:31
  38.3 2.9 %collective-permute-start.2 = (bf16[2,32,256]{2,1,0:T(8,128)(2,1)S(1)}, bf16[2,32,256]{2,1,0:T(8,128)(2,1)S(1)}, u32[]{:S(2)}, u32[]{:S(2)}) collective-permute-start(bf16[2,32,256]{2,1,0:T(8,128)(2,1)S(1)} %slice_bitcast_fusion.6), channel_id=1, source_target_pairs={{0,256},{1,257},{2,258},{3,259},{4,260},{5,261},{6,262},{7,263},{8... | collective-permute-start | bytes 98312 | tf_op jit(solution)/shard_map/ppermute | solution.py:31
  47.1 1.3 copy-start.5
  48.4 32.4 %all-to-all-start.2 = ((bf16[32,2,32,256]{3,2,1,0:T(8,128)(2,1)}), bf16[32,2,32,256]{3,2,1,0:T(8,128)(2,1)S(1)}, u32[]{:S(2)}, u32[]{:S(2)}) async-start(bf16[32,2,32,256]{3,2,1,0:T(8,128)(2,1)} %broadcast_in_dim.24), calls=%async_computation.2 | async-start | bytes 2097152 | tf_op jit(solution)/shard_map/all_to_all | solution.py:21
  56.1 4.5 %copy-start.6 = (bf16[4,2,2,128,256]{3,4,2,1,0:T(8,128)(2,1)S(1)}, bf16[4,2,2,128,256]{3,4,2,1,0:T(8,128)(2,1)}, u32[]{:S(2)}) copy-start(bf16[4,2,2,128,256]{3,4,2,1,0:T(8,128)(2,1)} %copy-done.5) | copy-start | bytes 3145732
  81.1 5.6 %copy-start.2 = (bf16[4096,1,256]{2,0,1:T(8,128)(2,1)S(1)}, bf16[4096,1,256]{2,0,1:T(8,128)(2,1)}, u32[]{:S(2)}) copy-start(bf16[4096,1,256]{2,0,1:T(8,128)(2,1)} %get-tuple-element.15) | copy-start | bytes 6291460
  86.7 1.3 copy-start.9
  88.9 3.4 %copy-start.11 = (bf16[4,1,2,128,256]{3,4,2,0,1:T(8,128)(2,1)S(1)}, bf16[4,1,2,128,256]{3,4,2,0,1:T(8,128)(2,1)}, u32[]{:S(2)}) copy-start(bf16[4,1,2,128,256]{3,4,2,0,1:T(8,128)(2,1)} %get-tuple-element.19) | copy-start | bytes 1572868
  91.9 1.8 copy-start.10
  93.6 2.0 copy-start.1
  96.4 11.4 %all-to-all-start.4 = ((f32[4,3,2,4,4,128]{5,4,3,2,1,0:T(4,128)}), f32[4,3,2,4,4,128]{5,4,3,2,1,0:T(4,128)S(1)}, u32[]{:S(2)}, u32[]{:S(2)}) async-start(f32[4,3,2,4,4,128]{5,4,3,2,1,0:T(4,128)} %broadcast_in_dim.26), calls=%async_computation.4 | async-start | bytes 393216 | tf_op jit(solution)/shard_map/all_to_all | solution.py:21
  110.9 1.0 copy-start.7
  110.9 2.0 copy-start.3
  112.9 1.6 copy-start.4
  124.0 58.5 %copy-start.8 = (bf16[2,4,4,128,128]{3,4,2,1,0:T(8,128)(2,1)S(1)}, bf16[2,4,4,128,128]{3,4,2,1,0:T(8,128)(2,1)}, u32[]{:S(2)}) copy-start(bf16[2,4,4,128,128]{3,4,2,1,0:T(8,128)(2,1)} %copy-done.7) | copy-start | bytes 3145732
  158.5 11.1 %collective-permute-start.3 = (bf16[2,32,256]{2,1,0:T(8,128)(2,1)S(1)}, bf16[2,32,256]{2,1,0:T(8,128)(2,1)S(1)}, u32[]{:S(2)}, u32[]{:S(2)}) collective-permute-start(bf16[2,32,256]{2,1,0:T(8,128)(2,1)S(1)} %convert_element_type.97), channel_id=1, source_target_pairs={{256,0},{257,1},{258,2},{259,3},{260,4},{261,5},{262,6},{263,7},{2... | collective-permute-start | bytes 98312 | tf_op jit(solution)/shard_map/ppermute | solution.py:41
  159.8 16.7 %collective-permute-start.4 = (bf16[2,32,256]{2,1,0:T(8,128)(2,1)S(1)}, bf16[2,32,256]{2,1,0:T(8,128)(2,1)S(1)}, u32[]{:S(2)}, u32[]{:S(2)}) collective-permute-start(bf16[2,32,256]{2,1,0:T(8,128)(2,1)S(1)} %convert_element_type.97), channel_id=1, source_target_pairs={{512,0},{513,1},{514,2},{515,3},{516,4},{517,5},{518,6},{519,7},{5... | collective-permute-start | bytes 98312 | tf_op jit(solution)/shard_map/ppermute | solution.py:41
  161.1 16.9 %collective-permute-start.5 = (bf16[2,32,256]{2,1,0:T(8,128)(2,1)S(1)}, bf16[2,32,256]{2,1,0:T(8,128)(2,1)S(1)}, u32[]{:S(2)}, u32[]{:S(2)}) collective-permute-start(bf16[2,32,256]{2,1,0:T(8,128)(2,1)S(1)} %convert_element_type.97), channel_id=1, source_target_pairs={{768,0},{769,1},{770,2},{771,3},{772,4},{773,5},{774,6},{775,7},{7... | collective-permute-start | bytes 98312 | tf_op jit(solution)/shard_map/ppermute | solution.py:41
  178.6 9.8 %all-to-all-start.7 = ((bf16[4,2,32,256]{3,2,1,0:T(8,128)(2,1)}), bf16[4,2,32,256]{3,2,1,0:T(8,128)(2,1)S(1)}, u32[]{:S(2)}, u32[]{:S(2)}) async-start(bf16[4,2,32,256]{3,2,1,0:T(8,128)(2,1)} %broadcast_in_dim.29), calls=%async_computation.7 | async-start | bytes 262144 | tf_op jit(solution)/shard_map/all_to_all | solution.py:21
  182.8 9.8 %copy-start.13 = (bf16[1,2,128,256]{3,2,1,0:T(8,128)(2,1)S(1)}, bf16[1,2,128,256]{3,2,1,0:T(8,128)(2,1)}, u32[]{:S(2)}) copy-start(bf16[1,2,128,256]{3,2,1,0:T(8,128)(2,1)} %param.5) | copy-start | bytes 393220
  188.5 28.4 %all-to-all-start.8 = ((f32[4,2,128,256]{2,3,1,0:T(8,128)}), f32[4,2,128,256]{2,3,1,0:T(8,128)S(1)}, u32[]{:S(2)}, u32[]{:S(2)}) async-start(f32[4,2,128,256]{2,3,1,0:T(8,128)} %bitcast.46), calls=%async_computation.8 | async-start | bytes 2097152 | tf_op jit(solution)/shard_map/all_to_all | solution.py:118

commit v11 on v10

--- a/solution.py
+++ b/solution.py
@@ -22,10 +22,14 @@
 
 
 def seg_broadcast(value, n_hi, n_x):
+    x = lax.axis_index("x")
     zh = lax.axis_index("zh")
     quarter = value.shape[1] // n_x
     pieces = value.reshape(value.shape[0], n_x, quarter, value.shape[2])
-    mine = lax.all_to_all(jnp.moveaxis(pieces, 1, 0), "x", 0, 0, tiled=False)[0]
+    mine = pieces[:, 0]
+    for k in range(1, n_x):
+        got = lax.ppermute(pieces[:, k], "x", [(0, k)])
+        mine = jnp.where(x == k, got, mine)
     out = mine
     for b in range(1, n_hi):
         got = lax.ppermute(mine, "zh", [(0, b)])

time: 220 us -> 215 us (0.977)
  waiting for transfers between devices: 79.8 us -> 67.1 us
  starting transfers between devices: 53 us -> 60.7 us
    ppermute x0 -> x3, starting transfers between devices: none -> 7.25 us  [seg_broadcast(): got = lax.ppermute(pieces[:, k], 'x', [(0, k)])]
    all_to_all x4, waiting for transfers between devices: 37.6 us -> 31 us  [gather_axis(): return lax.all_to_all(spread, axis, 0, 0, tiled=False)]
    all_to_all x1 -> x0, starting transfers between devices: 4.29 us -> none  [seg_broadcast(): mine = lax.all_to_all(jnp.moveaxis(pieces, 1, 0), 'x', 0, 0, tiled=False)[0]]
    all_to_all x4, starting transfers between devices: 22.1 us -> 26.3 us  [gather_axis(): return lax.all_to_all(spread, axis, 0, 0, tiled=False)]
    all_to_all x1 -> x0, waiting for transfers between devices: 3.42 us -> none  [seg_broadcast(): mine = lax.all_to_all(jnp.moveaxis(pieces, 1, 0), 'x', 0, 0, tiled=False)[0]]
    ppermute x3, waiting for transfers between devices: 15.6 us -> 12.8 us  [seg_reduce(): got = lax.ppermute(sent, 'zh', [(b, 0)])]
  transfers between devices with their start and end apart: 12 -> 14, of which waited for: 11 -> 11; matrix products, arithmetic and copies ran while one was open for 6% -> 5% of each run, Pallas kernels for 0% -> 0%
where the time goes in v11:
time: 215 us; the launch traced here: 213 us
  waiting for transfers between devices  67.1 us (31%)
  starting transfers between devices  60.7 us (28%)
  blocking collectives  45.8 us (21%)
  local copies, waits for them, and re-layouts  19.2 us (9%)
  matrix products  12.2 us (6%)
  other arithmetic  7.41 us (3%)
    all_to_all x1, blocking collectives, shards(): lax.all_to_all(pair_sum, ('x', 'ty'), 0, 0, tiled=False).astype(jnp.float32)  33.9 us
    all_to_all x4, waiting for transfers between devices, gather_axis(): return lax.all_to_all(spread, axis, 0, 0, tiled=False)  31 us
    all_to_all x4, starting transfers between devices, gather_axis(): return lax.all_to_all(spread, axis, 0, 0, tiled=False)  26.3 us
    all_to_all x1, waiting for transfers between devices, shards(): lax.all_to_all(context_part, 'dp', 0, 0, tiled=False)  20.2 us
    ppermute x3, starting transfers between devices, seg_broadcast(): got = lax.ppermute(mine, 'zh', [(0, b)])  18.6 us
    ppermute x3, waiting for transfers between devices, seg_reduce(): got = lax.ppermute(sent, 'zh', [(b, 0)])  12.8 us
    ppermute x3, starting transfers between devices, seg_broadcast(): got = lax.ppermute(pieces[:, k], 'x', [(0, k)])  7.25 us
    all_to_all x1, blocking collectives, shards(): lax.all_to_all(head_terms, 'tc', 0, 0, tiled=False).astype(jnp.float32)  6.31 us
  transfers between devices with their start and end apart: 14, of which 11 were waited for; matrix products, arithmetic and copies ran while one was open for 5% of the time, Pallas kernels for 0%

profile of v11, /device:TPU:56, one launch (start us, length us, event | category | flops | bytes accessed | tf_op | source)
XLA Modules:
  0.0 212.7 jit_solution(1586152930633950661)
XLA Ops:
  0.0 1.6 copy-done
  1.6 2.3 %fusion.9 = bf16[256,256]{1,0:T(8,128)(2,1)S(1)} fusion(bf16[256,4096]{1,0:T(8,128)(2,1)S(1)} %bitcast.137, bf16[4096,3,256]{2,0,1:T(8,128)(2,1)} %bitcast.144), kind=kOutput, calls=%fused_computation.18 | convolution fusion | flops 536936448 | bytes 4325376 | tf_op jit(solution)/shard_map/dot_general | solution.py:74
  4.0 0.2 copy.185
  4.2 1.2 broadcast_in_dim.23
  5.3 7.3 %all-to-all-start = ((bf16[4,2,2,128,256]{3,4,2,1,0:T(8,128)(2,1)}), bf16[4,2,2,128,256]{3,4,2,1,0:T(8,128)(2,1)S(1)}, u32[]{:S(2)}, u32[]{:S(2)}) async-start(bf16[4,2,2,128,256]{3,4,2,1,0:T(8,128)(2,1)} %broadcast_in_dim.23), calls=%async_computation | async-start | bytes 2097152 | tf_op jit(solution)/shard_map/all_to_all | solution.py:21
  12.6 4.7 %collective-permute-start = (bf16[2,32,256]{2,1,0:T(8,128)(2,1)S(1)}, bf16[2,32,256]{2,1,0:T(8,128)(2,1)S(1)}, u32[]{:S(2)}, u32[]{:S(2)}) collective-permute-start(bf16[2,32,256]{2,1,0:T(8,128)(2,1)S(1)} %get-tuple-element.23), channel_id=1, source_target_pairs={{0,192},{1,193},{2,194},{3,195},{4,196},{5,197},{6,198},{7,199},{8... | collective-permute-start | bytes 98312 | tf_op jit(solution)/shard_map/ppermute | solution.py:31
  17.3 1.3 collective-permute-start.1
  18.6 1.3 collective-permute-start.2
  19.9 0.3 collective-permute-done.1
  20.3 1.2 collective-permute-done.2
  21.5 15.5 %collective-permute-start.3 = (bf16[2,32,256]{2,1,0:T(8,128)(2,1)S(1)}, bf16[2,32,256]{2,1,0:T(8,128)(2,1)S(1)}, u32[]{:S(2)}, u32[]{:S(2)}) collective-permute-start(bf16[2,32,256]{2,1,0:T(8,128)(2,1)S(1)} %fusion.32), channel_id=1, source_target_pairs={{0,768},{1,769},{2,770},{3,771},{4,772},{5,773},{6,774},{7,775},{8... | collective-permute-start | bytes 98312 | tf_op jit(solution)/shard_map/ppermute | solution.py:35
  37.0 1.8 collective-permute-start.4
  38.8 1.3 collective-permute-start.5
  40.2 0.3 collective-permute-done.4
  40.4 1.3 collective-permute-done.5
  41.8 1.2 broadcast_in_dim.24
  43.1 9.2 %all-to-all-start.1 = ((bf16[32,2,32,256]{3,2,1,0:T(8,128)(2,1)}), bf16[32,2,32,256]{3,2,1,0:T(8,128)(2,1)S(1)}, u32[]{:S(2)}, u32[]{:S(2)}) async-start(bf16[32,2,32,256]{3,2,1,0:T(8,128)(2,1)} %broadcast_in_dim.24), calls=%async_computation.1 | async-start | bytes 2097152 | tf_op jit(solution)/shard_map/all_to_all | solution.py:21
  52.3 4.5 %fusion.34 = (bf16[4096,1,256]{2,0,1:T(8,128)(2,1)}, bf16[4096,1,256]{2,0,1:T(8,128)(2,1)}) fusion(bf16[4096,3,256]{2,0,1:T(8,128)(2,1)} %bitcast.145), kind=kLoop, calls=%fused_computation.64 | loop fusion | bytes 8388608 | tf_op jit(solution)/shard_map/slice | solution.py:132
  56.8 1.1 fusion.35
  57.9 18.6 %all-to-all-done.1 = bf16[32,2,32,256]{3,2,1,0:T(8,128)(2,1)S(1)} async-done(((bf16[32,2,32,256]{3,2,1,0:T(8,128)(2,1)}), bf16[32,2,32,256]{3,2,1,0:T(8,128)(2,1)S(1)}, u32[]{:S(2)}, u32[]{:S(2)}) %all-to-all-start.1) | async-done | bytes 1048608 | tf_op jit(solution)/shard_map/all_to_all | solution.py:21
  76.6 0.3 broadcast_in_dim.25
  76.8 5.5 %all_to_all.40 = bf16[2,32,2,32,256]{4,3,2,1,0:T(8,128)(2,1)S(1)} all-to-all(bf16[2,32,2,32,256]{4,3,2,1,0:T(8,128)(2,1)S(1)} %broadcast_in_dim.25), channel_id=1, replica_groups=mesh['zh'=4,'x'=4,'dp'=4,'ty'=8,'tc'=2] {'tc'}, dimensions={0} | all-to-all | bytes 4194304 | tf_op jit(solution)/shard_map/all_to_all | solution.py:21
  82.4 0.7 fusion.3
  83.1 0.6 copy-done.9
  83.7 0.9 reshape.63
  84.6 3.0 %fusion.1 = bf16[4,2,32,256,1,1]{3,2,5,0,1,4:T(8,128)(2,1)S(1)} fusion(bf16[8,2,256,256,1,1]{3,2,1,0,5,4:T(8,128)(2,1)} %bitcast.140, bf16[2,4,8,2,32,256]{5,4,3,2,1,0:T(8,128)(2,1)} %bitcast.147), kind=kOutput, calls=%fused_computation.3 | convolution fusion | flops 536870912 | bytes 4325376 | tf_op jit(solution)/shard_map/cxymrf,ycfn->mxrn/dot_general | solution.py:90
  87.7 0.2 reshape.64
  87.8 0.2 copy.225
  88.0 1.4 multiply_reduce_fusion.1
  89.4 2.0 fusion.5
  91.4 0.7 broadcast_in_dim.26
  92.1 5.9 %all-to-all-start.3 = ((f32[4,3,2,4,4,128]{5,4,3,2,1,0:T(4,128)}), f32[4,3,2,4,4,128]{5,4,3,2,1,0:T(4,128)S(1)}, u32[]{:S(2)}, u32[]{:S(2)}) async-start(f32[4,3,2,4,4,128]{5,4,3,2,1,0:T(4,128)} %broadcast_in_dim.26), calls=%async_computation.3 | async-start | bytes 393216 | tf_op jit(solution)/shard_map/all_to_all | solution.py:21
  98.1 7.8 %all-to-all-done.3 = f32[4,3,2,4,4,128]{5,4,3,2,1,0:T(4,128)S(1)} async-done(((f32[4,3,2,4,4,128]{5,4,3,2,1,0:T(4,128)}), f32[4,3,2,4,4,128]{5,4,3,2,1,0:T(4,128)S(1)}, u32[]{:S(2)}, u32[]{:S(2)}) %all-to-all-start.3) | async-done | bytes 196640 | tf_op jit(solution)/shard_map/all_to_all | solution.py:21
  106.0 3.1 %fusion.20 = (bf16[2,4,4,128,128]{3,4,2,1,0:T(8,128)(2,1)S(1)}, bf16[2,4,4,128,128]{3,4,2,1,0:T(8,128)(2,1)S(1)}) fusion(f32[2,4,4,128]{3,2,1,0:T(4,128)S(1)} %get-tuple-element.11, f32[2,4,4,128]{3,2,1,0:T(4,128)S(1)} %bitcast_reduce_fusion, f32[2,4,4,128,128]{3,4,2,1,0:T(8,128)} %copy-done.1, f32[2,4,4,128,128]{3,4,2,1,0:T(8,128)} %get-tuple-element.26, ...), kind=kLoop, calls=%fused_computation.30 | loop fusion | flops 4194304 | bytes 6340608 | tf_op jit(solution)/shard_map/convert_element_type | solution.py:116
  109.1 0.5 fusion.12
  109.6 0.5 fusion.10
  110.1 0.9 copy-done.3
  111.0 0.8 fusion.36
  111.8 0.8 copy-done.4
  112.6 0.8 fusion.8
  113.4 0.1 copy.207
  113.5 6.3 %all_to_all.41 = bf16[2,2,128,8,256]{4,2,3,1,0:T(8,128)(2,1)} all-to-all(bf16[2,2,128,8,256]{4,2,3,1,0:T(8,128)(2,1)S(1)} %copy.207), channel_id=1, replica_groups=mesh['zh'=4,'x'=4,'dp'=4,'ty'=8,'tc'=2] {'tc'}, dimensions={0} | all-to-all | bytes 4194304 | tf_op jit(solution)/shard_map/all_to_all | solution.py:138
  119.8 2.1 reduce_sum.70
  122.0 0.1 copy.210
  122.1 33.9 %all_to_all.42 = bf16[32,2,32,256]{3,2,1,0:T(8,128)(2,1)S(1)} all-to-all(bf16[32,2,32,256]{3,2,1,0:T(8,128)(2,1)S(1)} %bitcast.143), channel_id=1, replica_groups=mesh['zh'=4,'x'=4,'dp'=4,'ty'=8,'tc'=2] {'x','ty'}, dimensions={0} | all-to-all | bytes 2097152 | tf_op jit(solution)/shard_map/all_to_all | solution.py:146
  156.1 0.2 convert_reduce_fusion
  156.2 1.3 collective-permute-start.6
  157.5 1.3 collective-permute-start.7
  158.8 1.3 collective-permute-start.8
  160.2 6.1 %collective-permute-done.6 = bf16[2,32,256]{2,1,0:T(8,128)(2,1)S(1)} collective-permute-done((bf16[2,32,256]{2,1,0:T(8,128)(2,1)S(1)}, bf16[2,32,256]{2,1,0:T(8,128)(2,1)S(1)}, u32[]{:S(2)}, u32[]{:S(2)}) %collective-permute-start.6) | collective-permute-done | bytes 32800 | tf_op jit(solution)/shard_map/ppermute | solution.py:45
  166.2 6.0 %collective-permute-done.7 = bf16[2,32,256]{2,1,0:T(8,128)(2,1)S(1)} collective-permute-done((bf16[2,32,256]{2,1,0:T(8,128)(2,1)S(1)}, bf16[2,32,256]{2,1,0:T(8,128)(2,1)S(1)}, u32[]{:S(2)}, u32[]{:S(2)}) %collective-permute-start.7) | collective-permute-done | bytes 32800 | tf_op jit(solution)/shard_map/ppermute | solution.py:45
  172.2 0.8 collective-permute-done.8
  173.0 0.7 broadcast_in_dim.29
  173.6 3.9 %all-to-all-start.6 = ((bf16[4,2,32,256]{3,2,1,0:T(8,128)(2,1)}), bf16[4,2,32,256]{3,2,1,0:T(8,128)(2,1)S(1)}, u32[]{:S(2)}, u32[]{:S(2)}) async-start(bf16[4,2,32,256]{3,2,1,0:T(8,128)(2,1)} %broadcast_in_dim.29), calls=%async_computation.6 | async-start | bytes 262144 | tf_op jit(solution)/shard_map/all_to_all | solution.py:21
  177.5 0.3 convolution_bitcast_fusion
  177.8 1.1 copy.216
  178.9 4.6 %all-to-all-done.6 = bf16[4,2,32,256]{3,2,1,0:T(8,128)(2,1)S(1)} async-done(((bf16[4,2,32,256]{3,2,1,0:T(8,128)(2,1)}), bf16[4,2,32,256]{3,2,1,0:T(8,128)(2,1)S(1)}, u32[]{:S(2)}, u32[]{:S(2)}) %all-to-all-start.6) | async-done | bytes 131104 | tf_op jit(solution)/shard_map/all_to_all | solution.py:21
  183.5 4.7 %all-to-all-start.7 = ((f32[4,2,128,256]{2,3,1,0:T(8,128)}), f32[4,2,128,256]{2,3,1,0:T(8,128)S(1)}, u32[]{:S(2)}, u32[]{:S(2)}) async-start(f32[4,2,128,256]{2,3,1,0:T(8,128)} %bitcast.48), calls=%async_computation.7 | async-start | bytes 2097152 | tf_op jit(solution)/shard_map/all_to_all | solution.py:122
  188.1 0.8 copy.212
  188.9 0.8 convert_select_fusion
  189.7 1.1 copy.213
  190.8 20.2 %all-to-all-done.7 = f32[4,2,128,256]{2,3,1,0:T(8,128)S(1)} async-done(((f32[4,2,128,256]{2,3,1,0:T(8,128)}), f32[4,2,128,256]{2,3,1,0:T(8,128)S(1)}, u32[]{:S(2)}, u32[]{:S(2)}) %all-to-all-start.7) | async-done | bytes 1048608 | tf_op jit(solution)/shard_map/all_to_all | solution.py:122
  211.0 1.0 fusion.22
  212.0 0.8 copy.217
  (47 shorter events, 0.5 us)
Async XLA Ops:
  0.0 1.6 copy-start
  1.6 2.3 %copy-start.12 = (bf16[1,2,128,256]{3,2,1,0:T(8,128)(2,1)S(1)}, bf16[1,2,128,256]{3,2,1,0:T(8,128)(2,1)}, u32[]{:S(2)}) copy-start(bf16[1,2,128,256]{3,2,1,0:T(8,128)(2,1)} %param.5) | copy-start | bytes 393220
  5.3 36.4 %all-to-all-start = ((bf16[4,2,2,128,256]{3,4,2,1,0:T(8,128)(2,1)}), bf16[4,2,2,128,256]{3,4,2,1,0:T(8,128)(2,1)S(1)}, u32[]{:S(2)}, u32[]{:S(2)}) async-start(bf16[4,2,2,128,256]{3,4,2,1,0:T(8,128)(2,1)} %broadcast_in_dim.23), calls=%async_computation | async-start | bytes 2097152 | tf_op jit(solution)/shard_map/all_to_all | solution.py:21
  12.6 7.3 %collective-permute-start = (bf16[2,32,256]{2,1,0:T(8,128)(2,1)S(1)}, bf16[2,32,256]{2,1,0:T(8,128)(2,1)S(1)}, u32[]{:S(2)}, u32[]{:S(2)}) collective-permute-start(bf16[2,32,256]{2,1,0:T(8,128)(2,1)S(1)} %get-tuple-element.23), channel_id=1, source_target_pairs={{0,192},{1,193},{2,194},{3,195},{4,196},{5,197},{6,198},{7,199},{8... | collective-permute-start | bytes 98312 | tf_op jit(solution)/shard_map/ppermute | solution.py:31
  17.3 2.9 %collective-permute-start.1 = (bf16[2,32,256]{2,1,0:T(8,128)(2,1)S(1)}, bf16[2,32,256]{2,1,0:T(8,128)(2,1)S(1)}, u32[]{:S(2)}, u32[]{:S(2)}) collective-permute-start(bf16[2,32,256]{2,1,0:T(8,128)(2,1)S(1)} %get-tuple-element.22), channel_id=1, source_target_pairs={{0,128},{1,129},{2,130},{3,131},{4,132},{5,133},{6,134},{7,135},{8... | collective-permute-start | bytes 98312 | tf_op jit(solution)/shard_map/ppermute | solution.py:31
  18.6 2.9 %collective-permute-start.2 = (bf16[2,32,256]{2,1,0:T(8,128)(2,1)S(1)}, bf16[2,32,256]{2,1,0:T(8,128)(2,1)S(1)}, u32[]{:S(2)}, u32[]{:S(2)}) collective-permute-start(bf16[2,32,256]{2,1,0:T(8,128)(2,1)S(1)} %get-tuple-element.21), channel_id=1, source_target_pairs={{0,64},{1,65},{2,66},{3,67},{4,68},{5,69},{6,70},{7,71},{8,72},{9,... | collective-permute-start | bytes 98312 | tf_op jit(solution)/shard_map/ppermute | solution.py:31
  21.5 18.7 %collective-permute-start.3 = (bf16[2,32,256]{2,1,0:T(8,128)(2,1)S(1)}, bf16[2,32,256]{2,1,0:T(8,128)(2,1)S(1)}, u32[]{:S(2)}, u32[]{:S(2)}) collective-permute-start(bf16[2,32,256]{2,1,0:T(8,128)(2,1)S(1)} %fusion.32), channel_id=1, source_target_pairs={{0,768},{1,769},{2,770},{3,771},{4,772},{5,773},{6,774},{7,775},{8... | collective-permute-start | bytes 98312 | tf_op jit(solution)/shard_map/ppermute | solution.py:35
  37.0 3.4 %collective-permute-start.4 = (bf16[2,32,256]{2,1,0:T(8,128)(2,1)S(1)}, bf16[2,32,256]{2,1,0:T(8,128)(2,1)S(1)}, u32[]{:S(2)}, u32[]{:S(2)}) collective-permute-start(bf16[2,32,256]{2,1,0:T(8,128)(2,1)S(1)} %fusion.32), channel_id=1, source_target_pairs={{0,512},{1,513},{2,514},{3,515},{4,516},{5,517},{6,518},{7,519},{8... | collective-permute-start | bytes 98312 | tf_op jit(solution)/shard_map/ppermute | solution.py:35
  38.8 2.9 %collective-permute-start.5 = (bf16[2,32,256]{2,1,0:T(8,128)(2,1)S(1)}, bf16[2,32,256]{2,1,0:T(8,128)(2,1)S(1)}, u32[]{:S(2)}, u32[]{:S(2)}) collective-permute-start(bf16[2,32,256]{2,1,0:T(8,128)(2,1)S(1)} %fusion.32), channel_id=1, source_target_pairs={{0,256},{1,257},{2,258},{3,259},{4,260},{5,261},{6,262},{7,263},{8... | collective-permute-start | bytes 98312 | tf_op jit(solution)/shard_map/ppermute | solution.py:35
  41.7 1.3 copy-start.5
  43.1 33.5 %all-to-all-start.1 = ((bf16[32,2,32,256]{3,2,1,0:T(8,128)(2,1)}), bf16[32,2,32,256]{3,2,1,0:T(8,128)(2,1)S(1)}, u32[]{:S(2)}, u32[]{:S(2)}) async-start(bf16[32,2,32,256]{3,2,1,0:T(8,128)(2,1)} %broadcast_in_dim.24), calls=%async_computation.1 | async-start | bytes 2097152 | tf_op jit(solution)/shard_map/all_to_all | solution.py:21
  52.3 4.5 %copy-start.6 = (bf16[4,2,2,128,256]{3,4,2,1,0:T(8,128)(2,1)S(1)}, bf16[4,2,2,128,256]{3,4,2,1,0:T(8,128)(2,1)}, u32[]{:S(2)}) copy-start(bf16[4,2,2,128,256]{3,4,2,1,0:T(8,128)(2,1)} %copy-done.5) | copy-start | bytes 3145732
  76.8 5.6 %copy-start.2 = (bf16[4096,1,256]{2,0,1:T(8,128)(2,1)S(1)}, bf16[4096,1,256]{2,0,1:T(8,128)(2,1)}, u32[]{:S(2)}) copy-start(bf16[4096,1,256]{2,0,1:T(8,128)(2,1)} %get-tuple-element.15) | copy-start | bytes 6291460
  82.4 1.3 copy-start.9
  84.6 3.4 %copy-start.11 = (bf16[4,1,2,128,256]{3,4,2,0,1:T(8,128)(2,1)S(1)}, bf16[4,1,2,128,256]{3,4,2,0,1:T(8,128)(2,1)}, u32[]{:S(2)}) copy-start(bf16[4,1,2,128,256]{3,4,2,0,1:T(8,128)(2,1)} %get-tuple-element.19) | copy-start | bytes 1572868
  87.6 1.8 copy-start.10
  89.4 2.0 copy-start.1
  92.1 13.7 %all-to-all-start.3 = ((f32[4,3,2,4,4,128]{5,4,3,2,1,0:T(4,128)}), f32[4,3,2,4,4,128]{5,4,3,2,1,0:T(4,128)S(1)}, u32[]{:S(2)}, u32[]{:S(2)}) async-start(f32[4,3,2,4,4,128]{5,4,3,2,1,0:T(4,128)} %broadcast_in_dim.26), calls=%async_computation.3 | async-start | bytes 393216 | tf_op jit(solution)/shard_map/all_to_all | solution.py:21
  109.1 1.0 copy-start.7
  109.1 2.0 copy-start.3
  111.0 1.6 copy-start.4
  122.1 55.4 %copy-start.8 = (bf16[2,4,4,128,128]{3,4,2,1,0:T(8,128)(2,1)S(1)}, bf16[2,4,4,128,128]{3,4,2,1,0:T(8,128)(2,1)}, u32[]{:S(2)}) copy-start(bf16[2,4,4,128,128]{3,4,2,1,0:T(8,128)(2,1)} %copy-done.7) | copy-start | bytes 3145732
  156.2 10.0 %collective-permute-start.6 = (bf16[2,32,256]{2,1,0:T(8,128)(2,1)S(1)}, bf16[2,32,256]{2,1,0:T(8,128)(2,1)S(1)}, u32[]{:S(2)}, u32[]{:S(2)}) collective-permute-start(bf16[2,32,256]{2,1,0:T(8,128)(2,1)S(1)} %convert_element_type.97), channel_id=1, source_target_pairs={{256,0},{257,1},{258,2},{259,3},{260,4},{261,5},{262,6},{263,7},{2... | collective-permute-start | bytes 98312 | tf_op jit(solution)/shard_map/ppermute | solution.py:45
  157.5 14.6 %collective-permute-start.7 = (bf16[2,32,256]{2,1,0:T(8,128)(2,1)S(1)}, bf16[2,32,256]{2,1,0:T(8,128)(2,1)S(1)}, u32[]{:S(2)}, u32[]{:S(2)}) collective-permute-start(bf16[2,32,256]{2,1,0:T(8,128)(2,1)S(1)} %convert_element_type.97), channel_id=1, source_target_pairs={{512,0},{513,1},{514,2},{515,3},{516,4},{517,5},{518,6},{519,7},{5... | collective-permute-start | bytes 98312 | tf_op jit(solution)/shard_map/ppermute | solution.py:45
  158.8 14.1 %collective-permute-start.8 = (bf16[2,32,256]{2,1,0:T(8,128)(2,1)S(1)}, bf16[2,32,256]{2,1,0:T(8,128)(2,1)S(1)}, u32[]{:S(2)}, u32[]{:S(2)}) collective-permute-start(bf16[2,32,256]{2,1,0:T(8,128)(2,1)S(1)} %convert_element_type.97), channel_id=1, source_target_pairs={{768,0},{769,1},{770,2},{771,3},{772,4},{773,5},{774,6},{775,7},{7... | collective-permute-start | bytes 98312 | tf_op jit(solution)/shard_map/ppermute | solution.py:45
  173.6 9.8 %all-to-all-start.6 = ((bf16[4,2,32,256]{3,2,1,0:T(8,128)(2,1)}), bf16[4,2,32,256]{3,2,1,0:T(8,128)(2,1)S(1)}, u32[]{:S(2)}, u32[]{:S(2)}) async-start(bf16[4,2,32,256]{3,2,1,0:T(8,128)(2,1)} %broadcast_in_dim.29), calls=%async_computation.6 | async-start | bytes 262144 | tf_op jit(solution)/shard_map/all_to_all | solution.py:21
  177.8 10.3 %copy-start.13 = (bf16[1,2,128,256]{3,2,1,0:T(8,128)(2,1)S(1)}, bf16[1,2,128,256]{3,2,1,0:T(8,128)(2,1)}, u32[]{:S(2)}) copy-start(bf16[1,2,128,256]{3,2,1,0:T(8,128)(2,1)} %param.5) | copy-start | bytes 393220
  183.5 27.5 %all-to-all-start.7 = ((f32[4,2,128,256]{2,3,1,0:T(8,128)}), f32[4,2,128,256]{2,3,1,0:T(8,128)S(1)}, u32[]{:S(2)}, u32[]{:S(2)}) async-start(f32[4,2,128,256]{2,3,1,0:T(8,128)} %bitcast.48), calls=%async_computation.7 | async-start | bytes 2097152 | tf_op jit(solution)/shard_map/all_to_all | solution.py:122
